TPU v7x, 512 devices: a whole 4x8x8 slice. The times are simulated.
512 devices in a mesh: bl: 128 (over y, z_hi, x, core), ta: 4 (over z_lo).
Axes of the slice: x: 4, y: 8, z: 8 (z_hi: 2, z_lo: 4; z = z_hi * 4 + z_lo), core: 2. Of those that a mesh axis runs over, the one named last changes fastest.
Arguments:
- visibility: bfloat16 [2, 8, 16384, 1024], P(None, 'ta', 'bl'), may hold values from -6 to 6
- delay_kbin: int32 [1024], replicated, may hold values from 0 to 511
- block_bin: int32 [128], replicated, may hold values from 0 to 127
- bin_slot: int32 [128], replicated, may hold values from 0 to 127, each once
- pair_flags: int32 [8, 128], replicated, may hold values 0 or 1
Outputs:
- bandpower: float32 [128, 512], P('bl')
Inputs may be any that keep to these rules, and one draw needn't show every extreme that they name: `bin_slot`: each row number once.
All inputs are finite; a program needn't handle non-finite values.
Results may differ from a plain program's by a relative error of at most 0.0055.
Values may be sent and summed in bfloat16 or wider, within the bound.
No kernel may reach another device: no remote copies, remote signals or barrier semaphores. Data moves between devices by JAX's collectives and lax.ppermute only.
A program may use at most 64 MiB of HBM per device.

v0:
```python
import math

import ml_dtypes
import numpy as np

import jax
import jax.numpy as jnp
from jax import lax
from jax.sharding import PartitionSpec as P


def shifted(block, axis, distance):
    devices = range(lax.axis_size(axis))
    route = [((i - distance) % len(devices), i) for i in devices]
    return lax.ppermute(block, axis, route)


def delay_tables(num_chans):
    chan_idx = np.arange(num_chans, dtype=np.int32)
    phase_idx = chan_idx[:, None] * chan_idx[None, :] % num_chans
    step_angle = np.float32(2.0 * math.pi / num_chans)
    phase_angle = step_angle * phase_idx.astype(np.float32)
    base_angle = step_angle * chan_idx.astype(np.float32)

    def cos32(angle):
        return np.cos(angle.astype(np.float64)).astype(np.float32)

    taper_win = (
        np.float32(0.35875)
        - np.float32(0.48829) * cos32(base_angle)
        + np.float32(0.14128) * cos32(np.float32(2.0) * base_angle)
        - np.float32(0.01168) * cos32(np.float32(3.0) * base_angle)
    )
    scale_norm = np.float32(1.0) / np.sqrt(np.sum(taper_win * taper_win, dtype=np.float32))
    weight_col = (taper_win * scale_norm)[:, None]
    cos_tab = (weight_col * cos32(phase_angle)).astype(ml_dtypes.bfloat16)
    sin_tab = (weight_col * np.sin(phase_angle.astype(np.float64)).astype(np.float32)).astype(
        ml_dtypes.bfloat16
    )
    return (jnp.asarray(cos_tab), jnp.asarray(sin_tab))


def delay_transform(block_data, cos_tab, sin_tab):
    num_rows = block_data.shape[1]
    flat_rows = block_data.reshape(2 * num_rows, block_data.shape[2])
    cos_part = jnp.dot(flat_rows, cos_tab, preferred_element_type=jnp.float32).reshape(
        2, num_rows, -1
    )
    sin_part = jnp.dot(flat_rows, sin_tab, preferred_element_type=jnp.float32).reshape(
        2, num_rows, -1
    )
    real_part = cos_part[0] + sin_part[1]
    imag_part = cos_part[1] - sin_part[0]
    return jnp.stack([real_part, imag_part]).astype(jnp.bfloat16)


def cross_power(own_block, other_block):
    own_f = own_block.astype(jnp.float32)
    other_f = other_block.astype(jnp.float32)
    return jnp.sum(own_f[0] * other_f[0] + own_f[1] * other_f[1], axis=0)


def accumulate(power_sum, flag_value, own_block, partner):
    return power_sum + flag_value.astype(jnp.float32) * cross_power(own_block, partner)


def per_device(visibility, delay_kbin, block_bin, bin_slot, pair_flags):
    num_times = visibility.shape[1]
    num_rows = visibility.shape[2]
    num_chans = visibility.shape[3]
    num_kbins = num_chans // 2
    num_bins = bin_slot.shape[0]
    cycle_len = pair_flags.shape[0]
    cos_tab, sin_tab = delay_tables(num_chans)
    spectra = delay_transform(
        visibility.reshape(2, num_times * num_rows, num_chans), cos_tab, sin_tab
    )
    my_block = lax.axis_index("bl")
    num_blocks = lax.axis_size("bl")
    half = cycle_len // 2
    flags_window = lax.dynamic_slice_in_dim(
        jnp.concatenate([pair_flags, pair_flags], axis=1), my_block, half + 1, axis=1
    )
    bins_window = lax.dynamic_slice_in_dim(
        jnp.concatenate([block_bin, block_bin]), my_block, half + 1
    )
    power_rows = [jnp.zeros((num_chans,), jnp.float32) for _ in range(half + 1)]
    below = spectra
    above = spectra
    for step in range(1, half + 1):
        below = shifted(below, "bl", 1)
        previous_above = above
        above = shifted(above, "bl", -1)
        odd = 2 * step - 1
        power_rows[step - 1] = accumulate(
            power_rows[step - 1], flags_window[odd - 1, step - 1], previous_above, below
        )
        power_rows[step] = accumulate(
            power_rows[step], flags_window[odd, step], above, below
        )
    power_table = jnp.stack(power_rows)
    k_onehot = (delay_kbin[:, None] == jnp.arange(num_kbins, dtype=jnp.int32)[None, :]).astype(
        jnp.float32
    )
    scale_value = 1.0 / math.sqrt(num_rows * num_times * lax.axis_size("ta"))
    binned = jnp.dot(power_table, k_onehot, precision=lax.Precision.HIGHEST) * scale_value
    binned = lax.psum(binned, "ta")
    target_rows = bin_slot[bins_window]
    slot_onehot = (
        jnp.arange(num_bins, dtype=jnp.int32)[:, None] == target_rows[None, :]
    ).astype(jnp.float32)
    partial_table = jnp.sum(slot_onehot[:, :, None] * binned[None, :, :], axis=1)
    received = lax.all_to_all(partial_table, "bl", 0, 0, tiled=True)
    return jnp.sum(received, axis=0, keepdims=True)


def solution(mesh):
    placed = (P(None, "ta", "bl", None), P(), P(), P(), P())
    return jax.shard_map(
        per_device, mesh=mesh, in_specs=placed, out_specs=P("bl", None), check_vma=False
    )
```

profile of v0, /device:TPU:1, one launch (start us, length us, event | category | flops | bytes accessed | tf_op | source)
XLA Modules:
  0.0 216.9 jit_solution(11376522704825544241)
XLA Ops:
  0.0 1.2 copy-done
  1.2 3.0 %convolution_bitcast_fusion = f32[512,1024]{1,0:T(8,128)S(1)} fusion(bf16[512,1024]{1,0:T(8,128)(2,1)S(1)} %bitcast.29, bf16[1024,1024]{1,0:T(8,128)(2,1)} %constant.22.clone), kind=kOutput, calls=%fused_computation.3 | convolution fusion | flops 1073741824 | bytes 5242880 | tf_op jit(solution)/shard_map/dot_general | solution.py:49
  4.2 1.3 convolution_bitcast_fusion.1
  5.5 0.5 fusion.9
  6.3 8.8 %collective-permute-start.1 = (bf16[2,256,1024]{2,1,0:T(8,128)(2,1)S(1)}, bf16[2,256,1024]{2,1,0:T(8,128)(2,1)S(1)}, u32[]{:S(2)}, u32[]{:S(2)}) collective-permute-start(bf16[2,256,1024]{2,1,0:T(8,128)(2,1)S(1)} %get-tuple-element.16), channel_id=1, source_target_pairs={{4,0},{8,4},{12,8},{16,12},{20,16},{24,20},{28,24},{32,28},{36,32}... | collective-permute-start | bytes 3145736 | tf_op jit(solution)/shard_map/ppermute | solution.py:15
  15.1 1.9 collective-permute-start
  17.0 6.3 %collective-permute-done.1 = bf16[2,256,1024]{2,1,0:T(8,128)(2,1)S(1)} collective-permute-done((bf16[2,256,1024]{2,1,0:T(8,128)(2,1)S(1)}, bf16[2,256,1024]{2,1,0:T(8,128)(2,1)S(1)}, u32[]{:S(2)}, u32[]{:S(2)}) %collective-permute-start.1) | collective-permute-done | bytes 1048608 | tf_op jit(solution)/shard_map/ppermute | solution.py:15
  23.3 1.0 copy-done.2
  24.2 22.7 %collective-permute-start.3 = (bf16[2,256,1024]{2,1,0:T(8,128)(2,1)S(1)}, bf16[2,256,1024]{2,1,0:T(8,128)(2,1)}, u32[]{:S(2)}, u32[]{:S(2)}) collective-permute-start(bf16[2,256,1024]{2,1,0:T(8,128)(2,1)S(1)} %collective-permute-done.1), channel_id=1, source_target_pairs={{4,0},{8,4},{12,8},{16,12},{20,16},{24,20},{28,24},{32,28},{36,32}... | collective-permute-start | bytes 3145736 | tf_op jit(solution)/shard_map/ppermute | solution.py:15
  47.0 1.9 collective-permute-start.2
  48.9 0.4 collective-permute-done.3
  49.4 32.4 %collective-permute-start.5 = (bf16[2,256,1024]{2,1,0:T(8,128)(2,1)}, bf16[2,256,1024]{2,1,0:T(8,128)(2,1)}, u32[]{:S(2)}, u32[]{:S(2)}) collective-permute-start(bf16[2,256,1024]{2,1,0:T(8,128)(2,1)} %collective-permute-done.3), channel_id=1, source_target_pairs={{4,0},{8,4},{12,8},{16,12},{20,16},{24,20},{28,24},{32,28},{36,32}... | collective-permute-start | bytes 3145736 | tf_op jit(solution)/shard_map/ppermute | solution.py:15
  81.7 1.9 collective-permute-start.4
  83.8 0.7 fusion.14
  89.4 27.5 %collective-permute-start.7 = (bf16[2,256,1024]{2,1,0:T(8,128)(2,1)}, bf16[2,256,1024]{2,1,0:T(8,128)(2,1)}, u32[]{:S(2)}, u32[]{:S(2)}) collective-permute-start(bf16[2,256,1024]{2,1,0:T(8,128)(2,1)} %collective-permute-done.5), channel_id=1, source_target_pairs={{4,0},{8,4},{12,8},{16,12},{20,16},{24,20},{28,24},{32,28},{36,32}... | collective-permute-start | bytes 3145736 | tf_op jit(solution)/shard_map/ppermute | solution.py:15
  117.0 1.9 collective-permute-start.6
  119.0 0.6 gather_fusion
  119.7 1.5 convert_element_type.98
  121.5 1.5 convert_element_type.104
  123.0 1.5 convert_element_type.101
  124.5 1.3 add_reduce_fusion.3
  125.8 1.5 convert_element_type.110
  127.3 1.5 convert_element_type.107
  128.8 1.5 convert_element_type.116
  130.3 4.3 %collective-permute-done.6 = bf16[2,256,1024]{2,1,0:T(8,128)(2,1)} collective-permute-done((bf16[2,256,1024]{2,1,0:T(8,128)(2,1)}, bf16[2,256,1024]{2,1,0:T(8,128)(2,1)}, u32[]{:S(2)}, u32[]{:S(2)}) %collective-permute-start.6) | collective-permute-done | bytes 1048608 | tf_op jit(solution)/shard_map/ppermute | solution.py:15
  134.6 1.5 convert_element_type.113
  136.0 1.3 fusion.3
  137.5 0.8 fusion.1
  138.3 14.8 %psum.7 = f32[5,512]{1,0:T(8,128)S(1)} all-reduce(f32[5,512]{1,0:T(8,128)S(1)} %fusion.1), channel_id=1, replica_groups=mesh['bl'=128,'ta'=4] {'ta'}, use_global_device_ids=true, to_apply=%region_8.0 | all-reduce | flops 2560 | bytes 20480 | tf_op jit(solution)/shard_map/psum | solution.py:107
  153.2 0.3 copy.8
  153.5 62.7 %all_to_all.9 = f32[128,1,512]{2,1,0:T(1,128)S(1)} all-to-all(f32[128,1,512]{2,1,0:T(1,128)S(1)} %copy.8), channel_id=1, replica_groups=mesh['bl'=128,'ta'=4] {'bl'}, dimensions={0} | all-to-all | bytes 524288 | tf_op jit(solution)/shard_map/all_to_all | solution.py:113
  216.1 0.8 reduce_sum.99
  (33 shorter events, 1.0 us)
Async XLA Ops:
  0.0 1.2 copy-start
  1.2 3.0 %copy-start.8 = (bf16[1024,1024]{1,0:T(8,128)(2,1)S(1)}, bf16[1024,1024]{1,0:T(8,128)(2,1)}, u32[]{:S(2)}) copy-start(bf16[1024,1024]{1,0:T(8,128)(2,1)} %constant.21.clone) | copy-start | bytes 6291460
  6.0 77.7 %copy-start.5 = (s32[8,128]{1,0:T(8,128)S(1)}, s32[8,128]{1,0:T(8,128)}, u32[]{:S(2)}) copy-start(s32[8,128]{1,0:T(8,128)} %param.11) | copy-start | bytes 12292
  6.0 83.4 %copy-start.7 = (s32[128]{0:T(128)S(1)}, s32[128]{0:T(128)}, u32[]{:S(2)}) copy-start(s32[128]{0:T(128)} %param.9) | copy-start | bytes 1540
  6.1 112.9 %copy-start.1 = (s32[128]{0:T(128)S(1)}, s32[128]{0:T(128)}, u32[]{:S(2)}) copy-start(s32[128]{0:T(128)} %param.10) | copy-start | bytes 1540
  6.3 17.0 %collective-permute-start.1 = (bf16[2,256,1024]{2,1,0:T(8,128)(2,1)S(1)}, bf16[2,256,1024]{2,1,0:T(8,128)(2,1)S(1)}, u32[]{:S(2)}, u32[]{:S(2)}) collective-permute-start(bf16[2,256,1024]{2,1,0:T(8,128)(2,1)S(1)} %get-tuple-element.16), channel_id=1, source_target_pairs={{4,0},{8,4},{12,8},{16,12},{20,16},{24,20},{28,24},{32,28},{36,32}... | collective-permute-start | bytes 3145736 | tf_op jit(solution)/shard_map/ppermute | solution.py:15
  15.1 31.9 %collective-permute-start = (bf16[2,256,1024]{2,1,0:T(8,128)(2,1)S(1)}, bf16[2,256,1024]{2,1,0:T(8,128)(2,1)S(1)}, u32[]{:S(2)}, u32[]{:S(2)}) collective-permute-start(bf16[2,256,1024]{2,1,0:T(8,128)(2,1)S(1)} %get-tuple-element.16), channel_id=1, source_target_pairs={{508,0},{0,4},{4,8},{8,12},{12,16},{16,20},{20,24},{24,28},{28,32}... | collective-permute-start | bytes 3145736 | tf_op jit(solution)/shard_map/ppermute | solution.py:15
  23.3 1.0 copy-start.2
  24.2 25.1 %collective-permute-start.3 = (bf16[2,256,1024]{2,1,0:T(8,128)(2,1)S(1)}, bf16[2,256,1024]{2,1,0:T(8,128)(2,1)}, u32[]{:S(2)}, u32[]{:S(2)}) collective-permute-start(bf16[2,256,1024]{2,1,0:T(8,128)(2,1)S(1)} %collective-permute-done.1), channel_id=1, source_target_pairs={{4,0},{8,4},{12,8},{16,12},{20,16},{24,20},{28,24},{32,28},{36,32}... | collective-permute-start | bytes 3145736 | tf_op jit(solution)/shard_map/ppermute | solution.py:15
  47.0 2.4 %copy-start.3 = (bf16[2,256,1024]{2,1,0:T(8,128)(2,1)}, bf16[2,256,1024]{2,1,0:T(8,128)(2,1)S(1)}, u32[]{:S(2)}) copy-start(bf16[2,256,1024]{2,1,0:T(8,128)(2,1)S(1)} %collective-permute-done) | copy-start | bytes 3145732
  47.0 34.8 %collective-permute-start.2 = (bf16[2,256,1024]{2,1,0:T(8,128)(2,1)S(1)}, bf16[2,256,1024]{2,1,0:T(8,128)(2,1)}, u32[]{:S(2)}, u32[]{:S(2)}) collective-permute-start(bf16[2,256,1024]{2,1,0:T(8,128)(2,1)S(1)} %collective-permute-done), channel_id=1, source_target_pairs={{508,0},{0,4},{4,8},{8,12},{12,16},{16,20},{20,24},{24,28},{28,32}... | collective-permute-start | bytes 3145736 | tf_op jit(solution)/shard_map/ppermute | solution.py:15
  49.4 40.1 %collective-permute-start.5 = (bf16[2,256,1024]{2,1,0:T(8,128)(2,1)}, bf16[2,256,1024]{2,1,0:T(8,128)(2,1)}, u32[]{:S(2)}, u32[]{:S(2)}) collective-permute-start(bf16[2,256,1024]{2,1,0:T(8,128)(2,1)} %collective-permute-done.3), channel_id=1, source_target_pairs={{4,0},{8,4},{12,8},{16,12},{20,16},{24,20},{28,24},{32,28},{36,32}... | collective-permute-start | bytes 3145736 | tf_op jit(solution)/shard_map/ppermute | solution.py:15
  81.7 35.2 %collective-permute-start.4 = (bf16[2,256,1024]{2,1,0:T(8,128)(2,1)}, bf16[2,256,1024]{2,1,0:T(8,128)(2,1)}, u32[]{:S(2)}, u32[]{:S(2)}) collective-permute-start(bf16[2,256,1024]{2,1,0:T(8,128)(2,1)} %collective-permute-done.2), channel_id=1, source_target_pairs={{508,0},{0,4},{4,8},{8,12},{12,16},{16,20},{20,24},{24,28},{28,32}... | collective-permute-start | bytes 3145736 | tf_op jit(solution)/shard_map/ppermute | solution.py:15
  89.4 39.4 %collective-permute-start.7 = (bf16[2,256,1024]{2,1,0:T(8,128)(2,1)}, bf16[2,256,1024]{2,1,0:T(8,128)(2,1)}, u32[]{:S(2)}, u32[]{:S(2)}) collective-permute-start(bf16[2,256,1024]{2,1,0:T(8,128)(2,1)} %collective-permute-done.5), channel_id=1, source_target_pairs={{4,0},{8,4},{12,8},{16,12},{20,16},{24,20},{28,24},{32,28},{36,32}... | collective-permute-start | bytes 3145736 | tf_op jit(solution)/shard_map/ppermute | solution.py:15
  117.0 17.6 %collective-permute-start.6 = (bf16[2,256,1024]{2,1,0:T(8,128)(2,1)}, bf16[2,256,1024]{2,1,0:T(8,128)(2,1)}, u32[]{:S(2)}, u32[]{:S(2)}) collective-permute-start(bf16[2,256,1024]{2,1,0:T(8,128)(2,1)} %collective-permute-done.4), channel_id=1, source_target_pairs={{508,0},{0,4},{4,8},{8,12},{12,16},{16,20},{20,24},{24,28},{28,32}... | collective-permute-start | bytes 3145736 | tf_op jit(solution)/shard_map/ppermute | solution.py:15
  119.6 1.6 copy-start.4
  136.0 1.4 copy-start.6
where the time goes:
time: 218 us; the launch traced here: 217 us
  starting transfers between devices  99.1 us (45%)
  blocking collectives  77.5 us (36%)
  other arithmetic  15.2 us (7%)
  waiting for transfers between devices  11 us (5%)
  between operations  5.29 us (2%)
  matrix products  5.04 us (2%)
  local copies, waits for them, and re-layouts  3.87 us (2%)
    ppermute x8, starting transfers between devices, shifted(): return lax.ppermute(block, axis, route)  99.1 us
    all_to_all x1, blocking collectives, per_device(): received = lax.all_to_all(partial_table, 'bl', 0, 0, tiled=True)  62.7 us
    psum x1, blocking collectives, per_device(): binned = lax.psum(binned, 'ta')  14.8 us
    ppermute x8, waiting for transfers between devices, shifted(): return lax.ppermute(block, axis, route)  11 us
    convert_element_type x5, other arithmetic, cross_power(): own_f = own_block.astype(jnp.float32)  6.16 us
    convert_element_type x4, other arithmetic, cross_power(): other_f = other_block.astype(jnp.float32)  4.66 us
  transfers between devices with their start and end apart: 8, of which 3 were waited for; matrix products, arithmetic and copies ran while one was open for 6% of the time, Pallas kernels for 0%

commit v1 on v0

--- a/solution.py
+++ b/solution.py
@@ -104,14 +104,13 @@
     )
     scale_value = 1.0 / math.sqrt(num_rows * num_times * lax.axis_size("ta"))
     binned = jnp.dot(power_table, k_onehot, precision=lax.Precision.HIGHEST) * scale_value
-    binned = lax.psum(binned, "ta")
     target_rows = bin_slot[bins_window]
     slot_onehot = (
         jnp.arange(num_bins, dtype=jnp.int32)[:, None] == target_rows[None, :]
     ).astype(jnp.float32)
     partial_table = jnp.sum(slot_onehot[:, :, None] * binned[None, :, :], axis=1)
     received = lax.all_to_all(partial_table, "bl", 0, 0, tiled=True)
-    return jnp.sum(received, axis=0, keepdims=True)
+    return lax.psum(jnp.sum(received, axis=0, keepdims=True), "ta")
 
 
 def solution(mesh):

time: 218 us -> 209 us (0.959)
  blocking collectives: 77.5 us -> 68.8 us
    all_to_all x1, blocking collectives: 62.7 us -> 54.8 us  [per_device(): received = lax.all_to_all(partial_table, 'bl', 0, 0, tiled=True)]
where the time goes in v1:
time: 209 us; the launch traced here: 208 us
  starting transfers between devices  99.1 us (47%)
  blocking collectives  68.8 us (33%)
  other arithmetic  14.6 us (7%)
  waiting for transfers between devices  11 us (5%)
  between operations  5.29 us (3%)
  matrix products  5.04 us (2%)
  local copies, waits for them, and re-layouts  3.87 us (2%)
    ppermute x8, starting transfers between devices, shifted(): return lax.ppermute(block, axis, route)  99.1 us
    all_to_all x1, blocking collectives, per_device(): received = lax.all_to_all(partial_table, 'bl', 0, 0, tiled=True)  54.8 us
    psum x1, blocking collectives, per_device(): return lax.psum(jnp.sum(received, axis=0, keepdims=True), 'ta')  14 us
    ppermute x8, waiting for transfers between devices, shifted(): return lax.ppermute(block, axis, route)  11 us
    convert_element_type x5, other arithmetic, cross_power(): own_f = own_block.astype(jnp.float32)  6.16 us
    convert_element_type x4, other arithmetic, cross_power(): other_f = other_block.astype(jnp.float32)  4.66 us
  transfers between devices with their start and end apart: 8, of which 3 were waited for; matrix products, arithmetic and copies ran while one was open for 6% of the time, Pallas kernels for 0%

profile of v1, /device:TPU:1, one launch (start us, length us, event | category | flops | bytes accessed | tf_op | source)
XLA Modules:
  0.0 207.7 jit_solution(2035640749204718951)
XLA Ops:
  0.0 1.2 copy-done
  1.2 3.0 %convolution_bitcast_fusion = f32[512,1024]{1,0:T(8,128)S(1)} fusion(bf16[512,1024]{1,0:T(8,128)(2,1)S(1)} %bitcast.29, bf16[1024,1024]{1,0:T(8,128)(2,1)} %constant.22.clone), kind=kOutput, calls=%fused_computation.3 | convolution fusion | flops 1073741824 | bytes 5242880 | tf_op jit(solution)/shard_map/dot_general | solution.py:49
  4.2 1.3 convolution_bitcast_fusion.1
  5.5 0.5 fusion.9
  6.3 8.8 %collective-permute-start.1 = (bf16[2,256,1024]{2,1,0:T(8,128)(2,1)S(1)}, bf16[2,256,1024]{2,1,0:T(8,128)(2,1)S(1)}, u32[]{:S(2)}, u32[]{:S(2)}) collective-permute-start(bf16[2,256,1024]{2,1,0:T(8,128)(2,1)S(1)} %get-tuple-element.16), channel_id=1, source_target_pairs={{4,0},{8,4},{12,8},{16,12},{20,16},{24,20},{28,24},{32,28},{36,32}... | collective-permute-start | bytes 3145736 | tf_op jit(solution)/shard_map/ppermute | solution.py:15
  15.1 1.9 collective-permute-start
  17.0 6.3 %collective-permute-done.1 = bf16[2,256,1024]{2,1,0:T(8,128)(2,1)S(1)} collective-permute-done((bf16[2,256,1024]{2,1,0:T(8,128)(2,1)S(1)}, bf16[2,256,1024]{2,1,0:T(8,128)(2,1)S(1)}, u32[]{:S(2)}, u32[]{:S(2)}) %collective-permute-start.1) | collective-permute-done | bytes 1048608 | tf_op jit(solution)/shard_map/ppermute | solution.py:15
  23.3 1.0 copy-done.2
  24.2 22.7 %collective-permute-start.3 = (bf16[2,256,1024]{2,1,0:T(8,128)(2,1)S(1)}, bf16[2,256,1024]{2,1,0:T(8,128)(2,1)}, u32[]{:S(2)}, u32[]{:S(2)}) collective-permute-start(bf16[2,256,1024]{2,1,0:T(8,128)(2,1)S(1)} %collective-permute-done.1), channel_id=1, source_target_pairs={{4,0},{8,4},{12,8},{16,12},{20,16},{24,20},{28,24},{32,28},{36,32}... | collective-permute-start | bytes 3145736 | tf_op jit(solution)/shard_map/ppermute | solution.py:15
  47.0 1.9 collective-permute-start.2
  48.9 0.4 collective-permute-done.3
  49.4 32.4 %collective-permute-start.5 = (bf16[2,256,1024]{2,1,0:T(8,128)(2,1)}, bf16[2,256,1024]{2,1,0:T(8,128)(2,1)}, u32[]{:S(2)}, u32[]{:S(2)}) collective-permute-start(bf16[2,256,1024]{2,1,0:T(8,128)(2,1)} %collective-permute-done.3), channel_id=1, source_target_pairs={{4,0},{8,4},{12,8},{16,12},{20,16},{24,20},{28,24},{32,28},{36,32}... | collective-permute-start | bytes 3145736 | tf_op jit(solution)/shard_map/ppermute | solution.py:15
  81.7 1.9 collective-permute-start.4
  83.8 0.7 fusion.14
  89.4 27.5 %collective-permute-start.7 = (bf16[2,256,1024]{2,1,0:T(8,128)(2,1)}, bf16[2,256,1024]{2,1,0:T(8,128)(2,1)}, u32[]{:S(2)}, u32[]{:S(2)}) collective-permute-start(bf16[2,256,1024]{2,1,0:T(8,128)(2,1)} %collective-permute-done.5), channel_id=1, source_target_pairs={{4,0},{8,4},{12,8},{16,12},{20,16},{24,20},{28,24},{32,28},{36,32}... | collective-permute-start | bytes 3145736 | tf_op jit(solution)/shard_map/ppermute | solution.py:15
  117.0 1.9 collective-permute-start.6
  119.0 0.6 gather_fusion
  119.7 1.5 convert_element_type.98
  121.3 0.2 convert_element_type.95
  121.5 1.5 convert_element_type.104
  123.0 1.5 convert_element_type.101
  124.5 1.3 add_reduce_fusion.3
  125.8 1.5 convert_element_type.110
  127.3 1.5 convert_element_type.107
  128.8 1.5 convert_element_type.116
  130.3 4.3 %collective-permute-done.6 = bf16[2,256,1024]{2,1,0:T(8,128)(2,1)} collective-permute-done((bf16[2,256,1024]{2,1,0:T(8,128)(2,1)}, bf16[2,256,1024]{2,1,0:T(8,128)(2,1)}, u32[]{:S(2)}, u32[]{:S(2)}) %collective-permute-start.6) | collective-permute-done | bytes 1048608 | tf_op jit(solution)/shard_map/ppermute | solution.py:15
  134.6 1.5 convert_element_type.113
  136.0 1.3 fusion.3
  137.5 0.8 fusion.1
  138.4 0.3 copy.8
  138.7 54.8 %all_to_all.9 = f32[128,1,512]{2,1,0:T(1,128)S(1)} all-to-all(f32[128,1,512]{2,1,0:T(1,128)S(1)} %copy.8), channel_id=1, replica_groups=mesh['bl'=128,'ta'=4] {'bl'}, dimensions={0} | all-to-all | bytes 524288 | tf_op jit(solution)/shard_map/all_to_all | solution.py:112
  193.7 14.0 %psum.7 = f32[1,512]{1,0:T(1,128)} all-reduce(f32[1,512]{1,0:T(1,128)S(1)} %bitcast.37), channel_id=1, replica_groups=mesh['bl'=128,'ta'=4] {'ta'}, use_global_device_ids=true, to_apply=%region_10.0 | all-reduce | flops 512 | bytes 4096 | tf_op jit(solution)/shard_map/psum | solution.py:113
  (33 shorter events, 1.0 us)
Async XLA Ops:
  0.0 1.2 copy-start
  1.2 3.0 %copy-start.8 = (bf16[1024,1024]{1,0:T(8,128)(2,1)S(1)}, bf16[1024,1024]{1,0:T(8,128)(2,1)}, u32[]{:S(2)}) copy-start(bf16[1024,1024]{1,0:T(8,128)(2,1)} %constant.21.clone) | copy-start | bytes 6291460
  6.0 77.7 %copy-start.5 = (s32[8,128]{1,0:T(8,128)S(1)}, s32[8,128]{1,0:T(8,128)}, u32[]{:S(2)}) copy-start(s32[8,128]{1,0:T(8,128)} %param.11) | copy-start | bytes 12292
  6.0 83.4 %copy-start.7 = (s32[128]{0:T(128)S(1)}, s32[128]{0:T(128)}, u32[]{:S(2)}) copy-start(s32[128]{0:T(128)} %param.9) | copy-start | bytes 1540
  6.1 112.9 %copy-start.1 = (s32[128]{0:T(128)S(1)}, s32[128]{0:T(128)}, u32[]{:S(2)}) copy-start(s32[128]{0:T(128)} %param.10) | copy-start | bytes 1540
  6.3 17.0 %collective-permute-start.1 = (bf16[2,256,1024]{2,1,0:T(8,128)(2,1)S(1)}, bf16[2,256,1024]{2,1,0:T(8,128)(2,1)S(1)}, u32[]{:S(2)}, u32[]{:S(2)}) collective-permute-start(bf16[2,256,1024]{2,1,0:T(8,128)(2,1)S(1)} %get-tuple-element.16), channel_id=1, source_target_pairs={{4,0},{8,4},{12,8},{16,12},{20,16},{24,20},{28,24},{32,28},{36,32}... | collective-permute-start | bytes 3145736 | tf_op jit(solution)/shard_map/ppermute | solution.py:15
  15.1 31.9 %collective-permute-start = (bf16[2,256,1024]{2,1,0:T(8,128)(2,1)S(1)}, bf16[2,256,1024]{2,1,0:T(8,128)(2,1)S(1)}, u32[]{:S(2)}, u32[]{:S(2)}) collective-permute-start(bf16[2,256,1024]{2,1,0:T(8,128)(2,1)S(1)} %get-tuple-element.16), channel_id=1, source_target_pairs={{508,0},{0,4},{4,8},{8,12},{12,16},{16,20},{20,24},{24,28},{28,32}... | collective-permute-start | bytes 3145736 | tf_op jit(solution)/shard_map/ppermute | solution.py:15
  23.3 1.0 copy-start.2
  24.2 25.1 %collective-permute-start.3 = (bf16[2,256,1024]{2,1,0:T(8,128)(2,1)S(1)}, bf16[2,256,1024]{2,1,0:T(8,128)(2,1)}, u32[]{:S(2)}, u32[]{:S(2)}) collective-permute-start(bf16[2,256,1024]{2,1,0:T(8,128)(2,1)S(1)} %collective-permute-done.1), channel_id=1, source_target_pairs={{4,0},{8,4},{12,8},{16,12},{20,16},{24,20},{28,24},{32,28},{36,32}... | collective-permute-start | bytes 3145736 | tf_op jit(solution)/shard_map/ppermute | solution.py:15
  47.0 2.4 %copy-start.3 = (bf16[2,256,1024]{2,1,0:T(8,128)(2,1)}, bf16[2,256,1024]{2,1,0:T(8,128)(2,1)S(1)}, u32[]{:S(2)}) copy-start(bf16[2,256,1024]{2,1,0:T(8,128)(2,1)S(1)} %collective-permute-done) | copy-start | bytes 3145732
  47.0 34.8 %collective-permute-start.2 = (bf16[2,256,1024]{2,1,0:T(8,128)(2,1)S(1)}, bf16[2,256,1024]{2,1,0:T(8,128)(2,1)}, u32[]{:S(2)}, u32[]{:S(2)}) collective-permute-start(bf16[2,256,1024]{2,1,0:T(8,128)(2,1)S(1)} %collective-permute-done), channel_id=1, source_target_pairs={{508,0},{0,4},{4,8},{8,12},{12,16},{16,20},{20,24},{24,28},{28,32}... | collective-permute-start | bytes 3145736 | tf_op jit(solution)/shard_map/ppermute | solution.py:15
  49.4 40.1 %collective-permute-start.5 = (bf16[2,256,1024]{2,1,0:T(8,128)(2,1)}, bf16[2,256,1024]{2,1,0:T(8,128)(2,1)}, u32[]{:S(2)}, u32[]{:S(2)}) collective-permute-start(bf16[2,256,1024]{2,1,0:T(8,128)(2,1)} %collective-permute-done.3), channel_id=1, source_target_pairs={{4,0},{8,4},{12,8},{16,12},{20,16},{24,20},{28,24},{32,28},{36,32}... | collective-permute-start | bytes 3145736 | tf_op jit(solution)/shard_map/ppermute | solution.py:15
  81.7 35.2 %collective-permute-start.4 = (bf16[2,256,1024]{2,1,0:T(8,128)(2,1)}, bf16[2,256,1024]{2,1,0:T(8,128)(2,1)}, u32[]{:S(2)}, u32[]{:S(2)}) collective-permute-start(bf16[2,256,1024]{2,1,0:T(8,128)(2,1)} %collective-permute-done.2), channel_id=1, source_target_pairs={{508,0},{0,4},{4,8},{8,12},{12,16},{16,20},{20,24},{24,28},{28,32}... | collective-permute-start | bytes 3145736 | tf_op jit(solution)/shard_map/ppermute | solution.py:15
  89.4 39.4 %collective-permute-start.7 = (bf16[2,256,1024]{2,1,0:T(8,128)(2,1)}, bf16[2,256,1024]{2,1,0:T(8,128)(2,1)}, u32[]{:S(2)}, u32[]{:S(2)}) collective-permute-start(bf16[2,256,1024]{2,1,0:T(8,128)(2,1)} %collective-permute-done.5), channel_id=1, source_target_pairs={{4,0},{8,4},{12,8},{16,12},{20,16},{24,20},{28,24},{32,28},{36,32}... | collective-permute-start | bytes 3145736 | tf_op jit(solution)/shard_map/ppermute | solution.py:15
  117.0 17.6 %collective-permute-start.6 = (bf16[2,256,1024]{2,1,0:T(8,128)(2,1)}, bf16[2,256,1024]{2,1,0:T(8,128)(2,1)}, u32[]{:S(2)}, u32[]{:S(2)}) collective-permute-start(bf16[2,256,1024]{2,1,0:T(8,128)(2,1)} %collective-permute-done.4), channel_id=1, source_target_pairs={{508,0},{0,4},{4,8},{8,12},{12,16},{16,20},{20,24},{24,28},{28,32}... | collective-permute-start | bytes 3145736 | tf_op jit(solution)/shard_map/ppermute | solution.py:15
  119.6 1.6 copy-start.4
  136.0 1.4 copy-start.6

commit v2 on v1

--- a/solution.py
+++ b/solution.py
@@ -12,6 +12,12 @@
 def shifted(block, axis, distance):
     devices = range(lax.axis_size(axis))
     route = [((i - distance) % len(devices), i) for i in devices]
+    return lax.ppermute(block, axis, route)
+
+
+def group_shifted(block, axis, group, distance):
+    devices = range(lax.axis_size(axis))
+    route = [(i, i - i % group + (i + distance) % group) for i in devices]
     return lax.ppermute(block, axis, route)
 
 
@@ -60,10 +66,6 @@
     return jnp.sum(own_f[0] * other_f[0] + own_f[1] * other_f[1], axis=0)
 
 
-def accumulate(power_sum, flag_value, own_block, partner):
-    return power_sum + flag_value.astype(jnp.float32) * cross_power(own_block, partner)
-
-
 def per_device(visibility, delay_kbin, block_bin, bin_slot, pair_flags):
     num_times = visibility.shape[1]
     num_rows = visibility.shape[2]
@@ -77,34 +79,40 @@
     )
     my_block = lax.axis_index("bl")
     num_blocks = lax.axis_size("bl")
-    half = cycle_len // 2
-    flags_window = lax.dynamic_slice_in_dim(
-        jnp.concatenate([pair_flags, pair_flags], axis=1), my_block, half + 1, axis=1
-    )
-    bins_window = lax.dynamic_slice_in_dim(
-        jnp.concatenate([block_bin, block_bin]), my_block, half + 1
-    )
-    power_rows = [jnp.zeros((num_chans,), jnp.float32) for _ in range(half + 1)]
-    below = spectra
-    above = spectra
-    for step in range(1, half + 1):
-        below = shifted(below, "bl", 1)
-        previous_above = above
-        above = shifted(above, "bl", -1)
-        odd = 2 * step - 1
-        power_rows[step - 1] = accumulate(
-            power_rows[step - 1], flags_window[odd - 1, step - 1], previous_above, below
-        )
-        power_rows[step] = accumulate(
-            power_rows[step], flags_window[odd, step], above, below
-        )
+    group = cycle_len
+    position = my_block % group
+    below_group = shifted(spectra, "bl", group)
+    ahead = [spectra]
+    behind = [spectra]
+    for _ in range(group // 2):
+        ahead.append(group_shifted(ahead[-1], "bl", group, -1))
+    for _ in range(group - 1 - group // 2):
+        behind.append(group_shifted(behind[-1], "bl", group, 1))
+    offsets = jnp.arange(1, cycle_len + 1, dtype=jnp.int32)
+    partner_pos = (position + offsets) % group
+    owners = my_block - position + partner_pos
+    flags = pair_flags[offsets - 1, owners]
+    power_rows = []
+    for offset in range(1, cycle_len + 1):
+        if offset == group:
+            held = spectra
+        elif offset <= group // 2:
+            held = ahead[offset]
+        else:
+            held = behind[group - offset]
+        pair_power = cross_power(held, below_group)
+        if offset < group:
+            pair_power = jnp.where(
+                position + offset < group, cross_power(held, spectra), pair_power
+            )
+        power_rows.append(flags[offset - 1].astype(jnp.float32) * pair_power)
     power_table = jnp.stack(power_rows)
     k_onehot = (delay_kbin[:, None] == jnp.arange(num_kbins, dtype=jnp.int32)[None, :]).astype(
         jnp.float32
     )
     scale_value = 1.0 / math.sqrt(num_rows * num_times * lax.axis_size("ta"))
     binned = jnp.dot(power_table, k_onehot, precision=lax.Precision.HIGHEST) * scale_value
-    target_rows = bin_slot[bins_window]
+    target_rows = bin_slot[block_bin[owners]]
     slot_onehot = (
         jnp.arange(num_bins, dtype=jnp.int32)[:, None] == target_rows[None, :]
     ).astype(jnp.float32)

time: 209 us -> 153 us (0.73)
  starting transfers between devices: 99.1 us -> 31.7 us
  waiting for transfers between devices: 11 us -> 45.7 us
  blocking collectives: 68.8 us -> 44.7 us
    ppermute x8 -> x1, starting transfers between devices: 99.1 us -> 7.45 us  [shifted(): return lax.ppermute(block, axis, route)]
    ppermute x0 -> x7, starting transfers between devices: none -> 24.3 us  [group_shifted(): return lax.ppermute(block, axis, route)]
    ppermute x0 -> x7, waiting for transfers between devices: none -> 21.8 us  [group_shifted(): return lax.ppermute(block, axis, route)]
    all_to_all x1, blocking collectives: 54.8 us -> 33.1 us  [per_device(): received = lax.all_to_all(partial_table, 'bl', 0, 0, tiled=True)]
    ppermute x8 -> x1, waiting for transfers between devices: 11 us -> 23.9 us  [shifted(): return lax.ppermute(block, axis, route)]
    psum x1, blocking collectives: 14 us -> 11.6 us  [per_device(): return lax.psum(jnp.sum(received, axis=0, keepdims=True), 'ta')]
    convert_element_type x4 -> x2, other arithmetic: 4.66 us -> 2.64 us  [cross_power(): other_f = other_block.astype(jnp.float32)]
    convert_element_type x5 -> x7, other arithmetic: 6.16 us -> 6.63 us  [cross_power(): own_f = own_block.astype(jnp.float32)]
  transfers between devices with their start and end apart: 8 -> 8, of which waited for: 3 -> 5; matrix products, arithmetic and copies ran while one was open for 6% -> 8% of each run, Pallas kernels for 0% -> 0%
where the time goes in v2:
time: 153 us; the launch traced here: 152 us
  waiting for transfers between devices  45.7 us (30%)
  blocking collectives  44.7 us (29%)
  starting transfers between devices  31.7 us (21%)
  other arithmetic  14.1 us (9%)
  between operations  5.42 us (4%)
  local copies, waits for them, and re-layouts  5.21 us (3%)
  matrix products  5.04 us (3%)
    all_to_all x1, blocking collectives, per_device(): received = lax.all_to_all(partial_table, 'bl', 0, 0, tiled=True)  33.1 us
    ppermute x7, starting transfers between devices, group_shifted(): return lax.ppermute(block, axis, route)  24.3 us
    ppermute x1, waiting for transfers between devices, shifted(): return lax.ppermute(block, axis, route)  23.9 us
    ppermute x7, waiting for transfers between devices, group_shifted(): return lax.ppermute(block, axis, route)  21.8 us
    psum x1, blocking collectives, per_device(): return lax.psum(jnp.sum(received, axis=0, keepdims=True), 'ta')  11.6 us
    ppermute x1, starting transfers between devices, shifted(): return lax.ppermute(block, axis, route)  7.45 us
    convert_element_type x7, other arithmetic, cross_power(): own_f = own_block.astype(jnp.float32)  6.63 us
    reduce_sum x2, other arithmetic, cross_power(): return jnp.sum(own_f[0] * other_f[0] + own_f[1] * other_f[1], axis=0)  3.29 us
  transfers between devices with their start and end apart: 8, of which 5 were waited for; matrix products, arithmetic and copies ran while one was open for 8% of the time, Pallas kernels for 0%

profile of v2, /device:TPU:1, one launch (start us, length us, event | category | flops | bytes accessed | tf_op | source)
XLA Modules:
  0.0 151.9 jit_solution(3445832781112115832)
XLA Ops:
  0.0 1.2 copy-done
  1.2 3.0 %convolution_bitcast_fusion = f32[512,1024]{1,0:T(8,128)S(1)} fusion(bf16[512,1024]{1,0:T(8,128)(2,1)S(1)} %bitcast.40, bf16[1024,1024]{1,0:T(8,128)(2,1)} %constant.57.clone), kind=kOutput, calls=%fused_computation.6 | convolution fusion | flops 1073741824 | bytes 5242880 | tf_op jit(solution)/shard_map/dot_general | solution.py:55
  4.2 1.3 convolution_bitcast_fusion.1
  5.5 0.5 fusion.5
  6.1 1.2 fusion.12
  7.3 6.9 %collective-permute-start = (bf16[2,256,1024]{2,1,0:T(8,128)(2,1)}, bf16[2,256,1024]{2,1,0:T(8,128)(2,1)S(1)}, u32[]{:S(2)}, u32[]{:S(2)}) collective-permute-start(bf16[2,256,1024]{2,1,0:T(8,128)(2,1)} %get-tuple-element.30), channel_id=1, source_target_pairs={{0,28},{4,0},{8,4},{12,8},{16,12},{20,16},{24,20},{28,24},{32,60},... | collective-permute-start | bytes 3145736 | tf_op jit(solution)/shard_map/ppermute | solution.py:21
  14.1 8.8 %collective-permute-done = bf16[2,256,1024]{2,1,0:T(8,128)(2,1)S(1)} collective-permute-done((bf16[2,256,1024]{2,1,0:T(8,128)(2,1)}, bf16[2,256,1024]{2,1,0:T(8,128)(2,1)S(1)}, u32[]{:S(2)}, u32[]{:S(2)}) %collective-permute-start) | collective-permute-done | bytes 1048608 | tf_op jit(solution)/shard_map/ppermute | solution.py:21
  22.9 1.0 copy-done.4
  23.9 3.8 %collective-permute-start.2 = (bf16[2,256,1024]{2,1,0:T(8,128)(2,1)S(1)}, bf16[2,256,1024]{2,1,0:T(8,128)(2,1)}, u32[]{:S(2)}, u32[]{:S(2)}) collective-permute-start(bf16[2,256,1024]{2,1,0:T(8,128)(2,1)S(1)} %collective-permute-done), channel_id=1, source_target_pairs={{0,28},{4,0},{8,4},{12,8},{16,12},{20,16},{24,20},{28,24},{32,60},... | collective-permute-start | bytes 3145736 | tf_op jit(solution)/shard_map/ppermute | solution.py:21
  27.8 7.4 %collective-permute-start.1 = (bf16[2,256,1024]{2,1,0:T(8,128)(2,1)}, bf16[2,256,1024]{2,1,0:T(8,128)(2,1)}, u32[]{:S(2)}, u32[]{:S(2)}) collective-permute-start(bf16[2,256,1024]{2,1,0:T(8,128)(2,1)} %get-tuple-element.30), channel_id=1, source_target_pairs={{480,0},{484,4},{488,8},{492,12},{496,16},{500,20},{504,24},{508,2... | collective-permute-start | bytes 3145736 | tf_op jit(solution)/shard_map/ppermute | solution.py:15
  35.2 1.4 collective-permute-start.6
  36.6 1.6 %collective-permute-done.2 = bf16[2,256,1024]{2,1,0:T(8,128)(2,1)} collective-permute-done((bf16[2,256,1024]{2,1,0:T(8,128)(2,1)S(1)}, bf16[2,256,1024]{2,1,0:T(8,128)(2,1)}, u32[]{:S(2)}, u32[]{:S(2)}) %collective-permute-start.2) | collective-permute-done | bytes 1048608 | tf_op jit(solution)/shard_map/ppermute | solution.py:21
  38.3 4.8 %collective-permute-start.3 = (bf16[2,256,1024]{2,1,0:T(8,128)(2,1)}, bf16[2,256,1024]{2,1,0:T(8,128)(2,1)}, u32[]{:S(2)}, u32[]{:S(2)}) collective-permute-start(bf16[2,256,1024]{2,1,0:T(8,128)(2,1)} %collective-permute-done.2), channel_id=1, source_target_pairs={{0,28},{4,0},{8,4},{12,8},{16,12},{20,16},{24,20},{28,24},{32,60},... | collective-permute-start | bytes 3145736 | tf_op jit(solution)/shard_map/ppermute | solution.py:21
  43.1 0.6 gather_fusion.2
  43.8 0.7 fusion.13
  49.6 0.6 gather_fusion
  50.3 0.6 gather_fusion.1
  50.9 1.5 %convert_element_type.128 = f32[2,256,1024]{2,1,0:T(8,128)S(1)} convert(bf16[2,256,1024]{2,1,0:T(8,128)(2,1)} %collective-permute-done.5) | non-fusion elementwise | flops 524288 | bytes 3145728 | tf_op jit(solution)/shard_map/convert_element_type | solution.py:64
  52.7 23.9 %collective-permute-done.1 = bf16[2,256,1024]{2,1,0:T(8,128)(2,1)} collective-permute-done((bf16[2,256,1024]{2,1,0:T(8,128)(2,1)}, bf16[2,256,1024]{2,1,0:T(8,128)(2,1)}, u32[]{:S(2)}, u32[]{:S(2)}) %collective-permute-start.1) | collective-permute-done | bytes 1048608 | tf_op jit(solution)/shard_map/ppermute | solution.py:15
  76.6 1.5 convert_element_type.110
  78.1 1.5 convert_element_type.113
  79.6 1.5 convert_element_type.125
  81.0 7.4 %collective-permute-start.7 = (bf16[2,256,1024]{2,1,0:T(8,128)(2,1)}, bf16[2,256,1024]{2,1,0:T(8,128)(2,1)S(1)}, u32[]{:S(2)}, u32[]{:S(2)}) collective-permute-start(bf16[2,256,1024]{2,1,0:T(8,128)(2,1)} %collective-permute-done.6), channel_id=1, source_target_pairs={{0,4},{4,8},{8,12},{12,16},{16,20},{20,24},{24,28},{28,0},{32,36},... | collective-permute-start | bytes 3145736 | tf_op jit(solution)/shard_map/ppermute | solution.py:21
  88.4 1.6 %add_reduce_fusion.2 = (f32[1024]{0:T(1024)S(1)}, f32[1024]{0:T(1024)S(1)}, f32[1024]{0:T(1024)S(1)}, f32[1024]{0:T(1024)S(1)}, f32[1024]{0:T(1024)S(1)}, /*index=5*/f32[1024]{0:T(1024)S(1)}, f32[1024]{0:T(1024)S(1)}) fusion(f32[2,256,1024]{2,1,0:T(8,128)S(1)} %convert_element_type.128, f32[2,256,1024]{2,1,0:T(8,128)S(1)} %get-tuple-element.29, ...), kind=kLoop, calls=%fused_computation.17 | loop fusion | flops 7332864 | bytes 12611584 | tf_op jit(solution)/shard_map/reduce_sum | solution.py:66
  90.1 1.5 convert_element_type.116
  91.6 8.9 %collective-permute-done.7 = bf16[2,256,1024]{2,1,0:T(8,128)(2,1)S(1)} collective-permute-done((bf16[2,256,1024]{2,1,0:T(8,128)(2,1)}, bf16[2,256,1024]{2,1,0:T(8,128)(2,1)S(1)}, u32[]{:S(2)}, u32[]{:S(2)}) %collective-permute-start.7) | collective-permute-done | bytes 1048608 | tf_op jit(solution)/shard_map/ppermute | solution.py:21
  100.7 2.4 %collective-permute-done.4 = bf16[2,256,1024]{2,1,0:T(8,128)(2,1)S(1)} collective-permute-done((bf16[2,256,1024]{2,1,0:T(8,128)(2,1)}, bf16[2,256,1024]{2,1,0:T(8,128)(2,1)S(1)}, u32[]{:S(2)}, u32[]{:S(2)}) %collective-permute-start.4) | collective-permute-done | bytes 1048608 | tf_op jit(solution)/shard_map/ppermute | solution.py:21
  103.4 1.7 %add_reduce_fusion.1 = (f32[1024]{0:T(1024)S(1)}, f32[1024]{0:T(1024)S(1)}, f32[1024]{0:T(1024)S(1)}, f32[1024]{0:T(1024)S(1)}, f32[1024]{0:T(1024)S(1)}, /*inde...) fusion(f32[2,256,1024]{2,1,0:T(8,128)S(1)} %convert_element_type.128, ...), kind=kLoop, calls=%fused_computation.16 | loop fusion | flops 8380416 | bytes 12615680 | tf_op jit(solution)/shard_map/reduce_sum | solution.py:66
  105.2 0.8 fusion.1
  106.0 0.6 multiply_reduce_fusion
  107.0 33.1 %all_to_all.9 = f32[128,1,512]{2,1,0:T(1,128)S(1)} all-to-all(f32[128,1,512]{2,1,0:T(1,128)S(1)} %copy.8), channel_id=1, replica_groups=mesh['bl'=128,'ta'=4] {'bl'}, dimensions={0} | all-to-all | bytes 524288 | tf_op jit(solution)/shard_map/all_to_all | solution.py:120
  140.3 11.6 %psum.7 = f32[1,512]{1,0:T(1,128)} all-reduce(f32[1,512]{1,0:T(1,128)S(1)} %bitcast.51), channel_id=1, replica_groups=mesh['bl'=128,'ta'=4] {'ta'}, use_global_device_ids=true, to_apply=%region_17.18 | all-reduce | flops 512 | bytes 4096 | tf_op jit(solution)/shard_map/psum | solution.py:121
  (38 shorter events, 1.4 us)
Async XLA Ops:
  0.0 1.2 copy-start
  1.2 3.0 %copy-start.7 = (bf16[1024,1024]{1,0:T(8,128)(2,1)S(1)}, bf16[1024,1024]{1,0:T(8,128)(2,1)}, u32[]{:S(2)}) copy-start(bf16[1024,1024]{1,0:T(8,128)(2,1)} %constant.56.clone) | copy-start | bytes 6291460
  6.0 37.1 %copy-start.3 = (s32[8,128]{1,0:T(8,128)S(1)}, s32[8,128]{1,0:T(8,128)}, u32[]{:S(2)}) copy-start(s32[8,128]{1,0:T(8,128)} %param.11) | copy-start | bytes 12292
  6.0 43.6 %copy-start.1 = (s32[128]{0:T(128)S(1)}, s32[128]{0:T(128)}, u32[]{:S(2)}) copy-start(s32[128]{0:T(128)} %param.9) | copy-start | bytes 1540
  6.1 44.2 %copy-start.2 = (s32[128]{0:T(128)S(1)}, s32[128]{0:T(128)}, u32[]{:S(2)}) copy-start(s32[128]{0:T(128)} %param.10) | copy-start | bytes 1540
  7.3 15.7 %collective-permute-start = (bf16[2,256,1024]{2,1,0:T(8,128)(2,1)}, bf16[2,256,1024]{2,1,0:T(8,128)(2,1)S(1)}, u32[]{:S(2)}, u32[]{:S(2)}) collective-permute-start(bf16[2,256,1024]{2,1,0:T(8,128)(2,1)} %get-tuple-element.30), channel_id=1, source_target_pairs={{0,28},{4,0},{8,4},{12,8},{16,12},{20,16},{24,20},{28,24},{32,60},... | collective-permute-start | bytes 3145736 | tf_op jit(solution)/shard_map/ppermute | solution.py:21
  14.1 21.1 %collective-permute-start.5 = (bf16[2,256,1024]{2,1,0:T(8,128)(2,1)}, bf16[2,256,1024]{2,1,0:T(8,128)(2,1)}, u32[]{:S(2)}, u32[]{:S(2)}) collective-permute-start(bf16[2,256,1024]{2,1,0:T(8,128)(2,1)} %get-tuple-element.30), channel_id=1, source_target_pairs={{0,4},{4,8},{8,12},{12,16},{16,20},{20,24},{24,28},{28,0},{32,36},... | collective-permute-start | bytes 3145736 | tf_op jit(solution)/shard_map/ppermute | solution.py:21
  22.9 1.0 copy-start.4
  23.9 14.3 %collective-permute-start.2 = (bf16[2,256,1024]{2,1,0:T(8,128)(2,1)S(1)}, bf16[2,256,1024]{2,1,0:T(8,128)(2,1)}, u32[]{:S(2)}, u32[]{:S(2)}) collective-permute-start(bf16[2,256,1024]{2,1,0:T(8,128)(2,1)S(1)} %collective-permute-done), channel_id=1, source_target_pairs={{0,28},{4,0},{8,4},{12,8},{16,12},{20,16},{24,20},{28,24},{32,60},... | collective-permute-start | bytes 3145736 | tf_op jit(solution)/shard_map/ppermute | solution.py:21
  27.8 48.8 %collective-permute-start.1 = (bf16[2,256,1024]{2,1,0:T(8,128)(2,1)}, bf16[2,256,1024]{2,1,0:T(8,128)(2,1)}, u32[]{:S(2)}, u32[]{:S(2)}) collective-permute-start(bf16[2,256,1024]{2,1,0:T(8,128)(2,1)} %get-tuple-element.30), channel_id=1, source_target_pairs={{480,0},{484,4},{488,8},{492,12},{496,16},{500,20},{504,24},{508,2... | collective-permute-start | bytes 3145736 | tf_op jit(solution)/shard_map/ppermute | solution.py:15
  35.2 44.3 %collective-permute-start.6 = (bf16[2,256,1024]{2,1,0:T(8,128)(2,1)}, bf16[2,256,1024]{2,1,0:T(8,128)(2,1)}, u32[]{:S(2)}, u32[]{:S(2)}) collective-permute-start(bf16[2,256,1024]{2,1,0:T(8,128)(2,1)} %collective-permute-done.5), channel_id=1, source_target_pairs={{0,4},{4,8},{8,12},{12,16},{16,20},{20,24},{24,28},{28,0},{32,36},... | collective-permute-start | bytes 3145736 | tf_op jit(solution)/shard_map/ppermute | solution.py:21
  38.3 50.1 %collective-permute-start.3 = (bf16[2,256,1024]{2,1,0:T(8,128)(2,1)}, bf16[2,256,1024]{2,1,0:T(8,128)(2,1)}, u32[]{:S(2)}, u32[]{:S(2)}) collective-permute-start(bf16[2,256,1024]{2,1,0:T(8,128)(2,1)} %collective-permute-done.2), channel_id=1, source_target_pairs={{0,28},{4,0},{8,4},{12,8},{16,12},{20,16},{24,20},{28,24},{32,60},... | collective-permute-start | bytes 3145736 | tf_op jit(solution)/shard_map/ppermute | solution.py:21
  50.9 1.6 %copy-start.5 = (bf16[2,256,1024]{2,1,0:T(8,128)(2,1)S(1)}, bf16[2,256,1024]{2,1,0:T(8,128)(2,1)}, u32[]{:S(2)}) copy-start(bf16[2,256,1024]{2,1,0:T(8,128)(2,1)} %copy-done.4) | copy-start | bytes 3145732
  81.0 19.4 %collective-permute-start.7 = (bf16[2,256,1024]{2,1,0:T(8,128)(2,1)}, bf16[2,256,1024]{2,1,0:T(8,128)(2,1)S(1)}, u32[]{:S(2)}, u32[]{:S(2)}) collective-permute-start(bf16[2,256,1024]{2,1,0:T(8,128)(2,1)} %collective-permute-done.6), channel_id=1, source_target_pairs={{0,4},{4,8},{8,12},{12,16},{16,20},{20,24},{24,28},{28,0},{32,36},... | collective-permute-start | bytes 3145736 | tf_op jit(solution)/shard_map/ppermute | solution.py:21
  88.4 14.7 %collective-permute-start.4 = (bf16[2,256,1024]{2,1,0:T(8,128)(2,1)}, bf16[2,256,1024]{2,1,0:T(8,128)(2,1)S(1)}, u32[]{:S(2)}, u32[]{:S(2)}) collective-permute-start(bf16[2,256,1024]{2,1,0:T(8,128)(2,1)} %collective-permute-done.3), channel_id=1, source_target_pairs={{0,28},{4,0},{8,4},{12,8},{16,12},{20,16},{24,20},{28,24},{32,60},... | collective-permute-start | bytes 3145736 | tf_op jit(solution)/shard_map/ppermute | solution.py:21
  103.4 1.8 %copy-start.6 = (s32[1024]{0:T(1024)S(1)}, s32[1024]{0:T(1024)}, u32[]{:S(2)}) copy-start(s32[1024]{0:T(1024)} %param.8) | copy-start | bytes 12292

commit v3 on v2

--- a/solution.py
+++ b/solution.py
@@ -81,7 +81,9 @@
     num_blocks = lax.axis_size("bl")
     group = cycle_len
     position = my_block % group
-    below_group = shifted(spectra, "bl", group)
+    split = num_chans // 2
+    below_low = shifted(spectra[:, :, :split], "bl", group)
+    above_high = shifted(spectra[:, :, split:], "bl", -group)
     ahead = [spectra]
     behind = [spectra]
     for _ in range(group // 2):
@@ -91,7 +93,10 @@
     offsets = jnp.arange(1, cycle_len + 1, dtype=jnp.int32)
     partner_pos = (position + offsets) % group
     owners = my_block - position + partner_pos
-    flags = pair_flags[offsets - 1, owners]
+    flags = pair_flags[offsets - 1, owners].astype(jnp.float32)
+    up_owner = (my_block + group) % num_blocks
+    up_flags = pair_flags[:, up_owner].astype(jnp.float32)
+    upper_half = jnp.zeros((split,), jnp.float32)
     power_rows = []
     for offset in range(1, cycle_len + 1):
         if offset == group:
@@ -100,12 +105,21 @@
             held = ahead[offset]
         else:
             held = behind[group - offset]
-        pair_power = cross_power(held, below_group)
+        low_half = cross_power(held[:, :, :split], below_low)
+        pair_power = jnp.concatenate([low_half, jnp.zeros((num_chans - split,), jnp.float32)])
         if offset < group:
             pair_power = jnp.where(
                 position + offset < group, cross_power(held, spectra), pair_power
             )
-        power_rows.append(flags[offset - 1].astype(jnp.float32) * pair_power)
+        power_rows.append(flags[offset - 1] * pair_power)
+        reach = offset % group
+        upper_half = upper_half + jnp.where(
+            position + reach < group,
+            up_flags[group - reach - 1] * cross_power(above_high, held[:, :, split:]),
+            0.0,
+        )
+    power_rows.append(jnp.concatenate([jnp.zeros((split,), jnp.float32), upper_half]))
+    owners = jnp.concatenate([owners, up_owner[None]])
     power_table = jnp.stack(power_rows)
     k_onehot = (delay_kbin[:, None] == jnp.arange(num_kbins, dtype=jnp.int32)[None, :]).astype(
         jnp.float32

time: 153 us -> 165 us (1.078)
  other arithmetic: 14.1 us -> 34.3 us
  starting transfers between devices: 31.7 us -> 23.2 us
  waiting for transfers between devices: 45.7 us -> 52 us
  between operations: 5.42 us -> 0.39 us
    ppermute x1 -> x2, waiting for transfers between devices: 23.9 us -> 36.9 us  [shifted(): return lax.ppermute(block, axis, route)]
    ppermute x7, starting transfers between devices: 24.3 us -> 12 us  [group_shifted(): return lax.ppermute(block, axis, route)]
    convert_element_type x2 -> x10, other arithmetic: 2.64 us -> 10.5 us  [cross_power(): other_f = other_block.astype(jnp.float32)]
    ppermute x7, waiting for transfers between devices: 21.8 us -> 15.1 us  [group_shifted(): return lax.ppermute(block, axis, route)]
    add x0 -> x1, other arithmetic: none -> 5.12 us  [per_device(): upper_half + jnp.where(position + reach < group, up_flags[group - reach -...]
    mul x8 -> x5, other arithmetic: 0.09 us -> 4.9 us  [per_device(): power_rows.append(flags[offset - 1] * pair_power)]
    psum x1, blocking collectives: 11.6 us -> 7.2 us  [per_device(): return lax.psum(jnp.sum(received, axis=0, keepdims=True), 'ta')]
    all_to_all x1, blocking collectives: 33.1 us -> 37.3 us  [per_device(): received = lax.all_to_all(partial_table, 'bl', 0, 0, tiled=True)]
  transfers between devices with their start and end apart: 8 -> 9, of which waited for: 5 -> 5; matrix products, arithmetic and copies ran while one was open for 8% -> 13% of each run, Pallas kernels for 0% -> 0%
where the time goes in v3:
time: 165 us; the launch traced here: 164 us
  waiting for transfers between devices  52 us (32%)
  blocking collectives  44.5 us (27%)
  other arithmetic  34.3 us (21%)
  starting transfers between devices  23.2 us (14%)
  matrix products  5.04 us (3%)
  local copies, waits for them, and re-layouts  4.86 us (3%)
    all_to_all x1, blocking collectives, per_device(): received = lax.all_to_all(partial_table, 'bl', 0, 0, tiled=True)  37.3 us
    ppermute x2, waiting for transfers between devices, shifted(): return lax.ppermute(block, axis, route)  36.9 us
    ppermute x7, waiting for transfers between devices, group_shifted(): return lax.ppermute(block, axis, route)  15.1 us
    ppermute x7, starting transfers between devices, group_shifted(): return lax.ppermute(block, axis, route)  12 us
    ppermute x2, starting transfers between devices, shifted(): return lax.ppermute(block, axis, route)  11.2 us
    convert_element_type x10, other arithmetic, cross_power(): other_f = other_block.astype(jnp.float32)  10.5 us
    convert_element_type x8, other arithmetic, cross_power(): own_f = own_block.astype(jnp.float32)  7.73 us
    psum x1, blocking collectives, per_device(): return lax.psum(jnp.sum(received, axis=0, keepdims=True), 'ta')  7.2 us
  transfers between devices with their start and end apart: 9, of which 5 were waited for; matrix products, arithmetic and copies ran while one was open for 13% of the time, Pallas kernels for 0%

profile of v3, /device:TPU:1, one launch (start us, length us, event | category | flops | bytes accessed | tf_op | source)
XLA Modules:
  0.0 164.3 jit_solution(11401123798974798455)
XLA Ops:
  0.0 1.2 copy-done
  1.2 3.0 %convolution_bitcast_fusion = f32[512,1024]{1,0:T(8,128)S(1)} fusion(bf16[512,1024]{1,0:T(8,128)(2,1)S(1)} %bitcast.52, bf16[1024,1024]{1,0:T(8,128)(2,1)} %constant.72.clone), kind=kOutput, calls=%fused_computation.6 | convolution fusion | flops 1073741824 | bytes 5242880 | tf_op jit(solution)/shard_map/dot_general | solution.py:55
  4.2 1.3 convolution_bitcast_fusion.1
  6.0 1.2 fusion.67
  7.3 6.9 %collective-permute-start = (bf16[2,256,1024]{2,1,0:T(8,128)(2,1)}, bf16[2,256,1024]{2,1,0:T(8,128)(2,1)}, u32[]{:S(2)}, u32[]{:S(2)}) collective-permute-start(bf16[2,256,1024]{2,1,0:T(8,128)(2,1)} %get-tuple-element.54), channel_id=1, source_target_pairs={{0,28},{4,0},{8,4},{12,8},{16,12},{20,16},{24,20},{28,24},{32,60},... | collective-permute-start | bytes 3145736 | tf_op jit(solution)/shard_map/ppermute | solution.py:21
  14.1 1.8 %fusion.68 = (f32[2,256,512]{2,1,0:T(8,128)}, bf16[2,256,512]{2,1,0:T(8,128)(2,1)}, f32[2,256,512]{2,1,0:T(8,128)}, bf16[2,256,512]{2,1,0:T(8,128)(2,1)}) fusion(bf16[1,256,1024]{2,1,0:T(8,128)(2,1)S(1)} %get-tuple-element.33, bf16[1,256,1024]{2,1,0:T(8,128)(2,1)S(1)} %get-tuple-element.32), kind=kLoop, calls=%fused_computation.164 | loop fusion | flops 1048576 | bytes 4194304 | tf_op jit(solution)/shard_map/convert_element_type | solution.py:65
  15.9 9.3 %collective-permute-start.8 = (bf16[2,256,512]{2,1,0:T(8,128)(2,1)}, bf16[2,256,512]{2,1,0:T(8,128)(2,1)}, u32[]{:S(2)}, u32[]{:S(2)}) collective-permute-start(bf16[2,256,512]{2,1,0:T(8,128)(2,1)} %get-tuple-element.29), channel_id=1, source_target_pairs={{32,0},{36,4},{40,8},{44,12},{48,16},{52,20},{56,24},{60,28},{64,3... | collective-permute-start | bytes 1572872 | tf_op jit(solution)/shard_map/ppermute | solution.py:15
  25.2 1.9 %collective-permute-start.1 = (bf16[2,256,512]{2,1,0:T(8,128)(2,1)}, bf16[2,256,512]{2,1,0:T(8,128)(2,1)}, u32[]{:S(2)}, u32[]{:S(2)}) collective-permute-start(bf16[2,256,512]{2,1,0:T(8,128)(2,1)} %get-tuple-element.50), channel_id=1, source_target_pairs={{480,0},{484,4},{488,8},{492,12},{496,16},{500,20},{504,24},{508,2... | collective-permute-start | bytes 1572872 | tf_op jit(solution)/shard_map/ppermute | solution.py:15
  27.3 1.4 collective-permute-start.2
  32.5 30.0 %collective-permute-done.8 = bf16[2,256,512]{2,1,0:T(8,128)(2,1)} collective-permute-done((bf16[2,256,512]{2,1,0:T(8,128)(2,1)}, bf16[2,256,512]{2,1,0:T(8,128)(2,1)}, u32[]{:S(2)}, u32[]{:S(2)}) %collective-permute-start.8) | collective-permute-done | bytes 524320 | tf_op jit(solution)/shard_map/ppermute | solution.py:15
  62.5 1.2 convert_element_type.134
  63.7 6.9 %collective-permute-done.1 = bf16[2,256,512]{2,1,0:T(8,128)(2,1)} collective-permute-done((bf16[2,256,512]{2,1,0:T(8,128)(2,1)}, bf16[2,256,512]{2,1,0:T(8,128)(2,1)}, u32[]{:S(2)}, u32[]{:S(2)}) %collective-permute-start.1) | collective-permute-done | bytes 524320 | tf_op jit(solution)/shard_map/ppermute | solution.py:15
  70.6 1.2 convert_element_type.119
  71.7 1.5 convert_element_type.116
  73.2 1.5 convert_element_type.130
  75.2 1.5 slice_convert_fusion.6
  76.6 1.4 slice_convert_fusion
  78.0 1.5 convert_element_type.120
  79.5 1.8 %collective-permute-start.7 = (bf16[2,256,1024]{2,1,0:T(8,128)(2,1)}, bf16[2,256,1024]{2,1,0:T(8,128)(2,1)S(1)}, u32[]{:S(2)}, u32[]{:S(2)}) collective-permute-start(bf16[2,256,1024]{2,1,0:T(8,128)(2,1)} %collective-permute-done.6), channel_id=1, source_target_pairs={{0,4},{4,8},{8,12},{12,16},{16,20},{20,24},{24,28},{28,0},{32,36},... | collective-permute-start | bytes 3145736 | tf_op jit(solution)/shard_map/ppermute | solution.py:21
  81.3 1.5 convert_element_type.128
  82.8 1.5 slice_convert_fusion.1
  84.3 1.6 slice_convert_fusion.5
  85.9 4.1 %collective-permute-done.3 = bf16[2,256,1024]{2,1,0:T(8,128)(2,1)S(1)} collective-permute-done((bf16[2,256,1024]{2,1,0:T(8,128)(2,1)}, bf16[2,256,1024]{2,1,0:T(8,128)(2,1)S(1)}, u32[]{:S(2)}, u32[]{:S(2)}) %collective-permute-start.3) | collective-permute-done | bytes 1048608 | tf_op jit(solution)/shard_map/ppermute | solution.py:21
  90.0 1.1 collective-permute-start.4
  93.9 10.3 %collective-permute-done.4 = bf16[2,256,1024]{2,1,0:T(8,128)(2,1)S(1)} collective-permute-done((bf16[2,256,1024]{2,1,0:T(8,128)(2,1)S(1)}, bf16[2,256,1024]{2,1,0:T(8,128)(2,1)S(1)}, u32[]{:S(2)}, u32[]{:S(2)}) %collective-permute-start.4) | collective-permute-done | bytes 1048608 | tf_op jit(solution)/shard_map/ppermute | solution.py:21
  105.0 5.1 %select_add_fusion = f32[512]{0:T(512)S(1)} fusion(f32[512]{0:T(512)S(1)} %get-tuple-element.19, f32[512]{0:T(512)S(1)} %get-tuple-element.18, f32[512]{0:T(512)S(1)} %get-tuple-element.17, f32[512]{0:T(512)S(1)} %get-tuple-element.15, f32[512]{0:T(512)S(1)} %get-tuple-element.14, f32[512]{0:T(512)S(1)} %get-tuple-element.13, f32[512]{0:T(512)S(1)} %get-tuple-element.16, ...), kind=kLoop, calls=%fused_computation.149 | loop fusion | flops 11776 | bytes 18472 | tf_op jit(solution)/shard_map/add | solution.py:116
  111.7 2.2 %fusion.3 = (f32[1024]{0:T(1024)S(1)}, f32[1024]{0:T(1024)S(1)}, f32[1024]{0:T(1024)S(1)}, f32[1024]{0:T(1024)S(1)}, f32[1024]{0:T(1024)S(1)}, /*index=5*/f32[1024]{0:T(1024)S(1)}, f32[1024]{0:T(1024)S(1)}) fusion(f32[2,256,1024]{2,1,0:T(8,128)S(1)} %convert_element_type.130, f32[2,256,1024]{2,1,0:T(8,128)S(1)} %get-tuple-element.53, ...), kind=kLoop, calls=%fused_computation.16 | loop fusion | flops 7332864 | bytes 16805888 | tf_op jit(solution)/shard_map/reduce_sum | solution.py:66
  114.6 1.2 select_multiply_fusion
  115.8 1.2 select_multiply_fusion.2
  117.0 1.2 select_multiply_fusion.4
  119.6 37.3 %all_to_all.9 = f32[128,1,512]{2,1,0:T(1,128)S(1)} all-to-all(f32[128,1,512]{2,1,0:T(1,128)S(1)} %copy.8), channel_id=1, replica_groups=mesh['bl'=128,'ta'=4] {'bl'}, dimensions={0} | all-to-all | bytes 524288 | tf_op jit(solution)/shard_map/all_to_all | solution.py:134
  157.1 7.2 %psum.7 = f32[1,512]{1,0:T(1,128)} all-reduce(f32[1,512]{1,0:T(1,128)S(1)} %bitcast.64), channel_id=1, replica_groups=mesh['bl'=128,'ta'=4] {'ta'}, use_global_device_ids=true, to_apply=%region_25.26 | all-reduce | flops 512 | bytes 4096 | tf_op jit(solution)/shard_map/psum | solution.py:135
  (56 shorter events, 12.4 us)
Async XLA Ops:
  0.0 1.2 copy-start
  1.2 3.0 %copy-start.7 = (bf16[1024,1024]{1,0:T(8,128)(2,1)S(1)}, bf16[1024,1024]{1,0:T(8,128)(2,1)}, u32[]{:S(2)}) copy-start(bf16[1024,1024]{1,0:T(8,128)(2,1)} %constant.71.clone) | copy-start | bytes 6291460
  7.2 21.4 %copy-start.1 = (s32[128]{0:T(128)S(1)}, s32[128]{0:T(128)}, u32[]{:S(2)}) copy-start(s32[128]{0:T(128)} %param.9) | copy-start | bytes 1540
  7.3 22.1 %copy-start.3 = (s32[8,128]{1,0:T(8,128)S(1)}, s32[8,128]{1,0:T(8,128)}, u32[]{:S(2)}) copy-start(s32[8,128]{1,0:T(8,128)} %param.11) | copy-start | bytes 12292
  7.3 23.2 %copy-start.2 = (s32[128]{0:T(128)S(1)}, s32[128]{0:T(128)}, u32[]{:S(2)}) copy-start(s32[128]{0:T(128)} %param.10) | copy-start | bytes 1540
  7.3 20.0 %collective-permute-start = (bf16[2,256,1024]{2,1,0:T(8,128)(2,1)}, bf16[2,256,1024]{2,1,0:T(8,128)(2,1)}, u32[]{:S(2)}, u32[]{:S(2)}) collective-permute-start(bf16[2,256,1024]{2,1,0:T(8,128)(2,1)} %get-tuple-element.54), channel_id=1, source_target_pairs={{0,28},{4,0},{8,4},{12,8},{16,12},{20,16},{24,20},{28,24},{32,60},... | collective-permute-start | bytes 3145736 | tf_op jit(solution)/shard_map/ppermute | solution.py:21
  14.1 15.3 %collective-permute-start.5 = (bf16[2,256,1024]{2,1,0:T(8,128)(2,1)}, bf16[2,256,1024]{2,1,0:T(8,128)(2,1)}, u32[]{:S(2)}, u32[]{:S(2)}) collective-permute-start(bf16[2,256,1024]{2,1,0:T(8,128)(2,1)} %get-tuple-element.54), channel_id=1, source_target_pairs={{0,4},{4,8},{8,12},{12,16},{16,20},{20,24},{24,28},{28,0},{32,36},... | collective-permute-start | bytes 3145736 | tf_op jit(solution)/shard_map/ppermute | solution.py:21
  15.9 46.6 %collective-permute-start.8 = (bf16[2,256,512]{2,1,0:T(8,128)(2,1)}, bf16[2,256,512]{2,1,0:T(8,128)(2,1)}, u32[]{:S(2)}, u32[]{:S(2)}) collective-permute-start(bf16[2,256,512]{2,1,0:T(8,128)(2,1)} %get-tuple-element.29), channel_id=1, source_target_pairs={{32,0},{36,4},{40,8},{44,12},{48,16},{52,20},{56,24},{60,28},{64,3... | collective-permute-start | bytes 1572872 | tf_op jit(solution)/shard_map/ppermute | solution.py:15
  25.2 45.3 %collective-permute-start.1 = (bf16[2,256,512]{2,1,0:T(8,128)(2,1)}, bf16[2,256,512]{2,1,0:T(8,128)(2,1)}, u32[]{:S(2)}, u32[]{:S(2)}) collective-permute-start(bf16[2,256,512]{2,1,0:T(8,128)(2,1)} %get-tuple-element.50), channel_id=1, source_target_pairs={{480,0},{484,4},{488,8},{492,12},{496,16},{500,20},{504,24},{508,2... | collective-permute-start | bytes 1572872 | tf_op jit(solution)/shard_map/ppermute | solution.py:15
  27.3 47.4 %collective-permute-start.2 = (bf16[2,256,1024]{2,1,0:T(8,128)(2,1)}, bf16[2,256,1024]{2,1,0:T(8,128)(2,1)}, u32[]{:S(2)}, u32[]{:S(2)}) collective-permute-start(bf16[2,256,1024]{2,1,0:T(8,128)(2,1)} %collective-permute-done), channel_id=1, source_target_pairs={{0,28},{4,0},{8,4},{12,8},{16,12},{20,16},{24,20},{28,24},{32,60},... | collective-permute-start | bytes 3145736 | tf_op jit(solution)/shard_map/ppermute | solution.py:21
  29.4 50.1 %collective-permute-start.6 = (bf16[2,256,1024]{2,1,0:T(8,128)(2,1)}, bf16[2,256,1024]{2,1,0:T(8,128)(2,1)}, u32[]{:S(2)}, u32[]{:S(2)}) collective-permute-start(bf16[2,256,1024]{2,1,0:T(8,128)(2,1)} %collective-permute-done.5), channel_id=1, source_target_pairs={{0,4},{4,8},{8,12},{12,16},{16,20},{20,24},{24,28},{28,0},{32,36},... | collective-permute-start | bytes 3145736 | tf_op jit(solution)/shard_map/ppermute | solution.py:21
  74.7 15.3 %collective-permute-start.3 = (bf16[2,256,1024]{2,1,0:T(8,128)(2,1)}, bf16[2,256,1024]{2,1,0:T(8,128)(2,1)S(1)}, u32[]{:S(2)}, u32[]{:S(2)}) collective-permute-start(bf16[2,256,1024]{2,1,0:T(8,128)(2,1)} %collective-permute-done.2), channel_id=1, source_target_pairs={{0,28},{4,0},{8,4},{12,8},{16,12},{20,16},{24,20},{28,24},{32,60},... | collective-permute-start | bytes 3145736 | tf_op jit(solution)/shard_map/ppermute | solution.py:21
  79.5 13.9 %collective-permute-start.7 = (bf16[2,256,1024]{2,1,0:T(8,128)(2,1)}, bf16[2,256,1024]{2,1,0:T(8,128)(2,1)S(1)}, u32[]{:S(2)}, u32[]{:S(2)}) collective-permute-start(bf16[2,256,1024]{2,1,0:T(8,128)(2,1)} %collective-permute-done.6), channel_id=1, source_target_pairs={{0,4},{4,8},{8,12},{12,16},{16,20},{20,24},{24,28},{28,0},{32,36},... | collective-permute-start | bytes 3145736 | tf_op jit(solution)/shard_map/ppermute | solution.py:21
  84.3 6.7 %copy-start.5 = (f32[2,256,512]{2,1,0:T(8,128)S(1)}, f32[2,256,512]{2,1,0:T(8,128)}, u32[]{:S(2)}) copy-start(f32[2,256,512]{2,1,0:T(8,128)} %get-tuple-element.28) | copy-start | bytes 3145732
  90.0 14.2 %collective-permute-start.4 = (bf16[2,256,1024]{2,1,0:T(8,128)(2,1)S(1)}, bf16[2,256,1024]{2,1,0:T(8,128)(2,1)S(1)}, u32[]{:S(2)}, u32[]{:S(2)}) collective-permute-start(bf16[2,256,1024]{2,1,0:T(8,128)(2,1)S(1)} %collective-permute-done.3), channel_id=1, source_target_pairs={{0,28},{4,0},{8,4},{12,8},{16,12},{20,16},{24,20},{28,24},{32,60},... | collective-permute-start | bytes 3145736 | tf_op jit(solution)/shard_map/ppermute | solution.py:21
  104.3 5.8 %copy-start.4 = (f32[2,256,512]{2,1,0:T(8,128)S(1)}, f32[2,256,512]{2,1,0:T(8,128)}, u32[]{:S(2)}) copy-start(f32[2,256,512]{2,1,0:T(8,128)} %get-tuple-element.49) | copy-start | bytes 3145732
  111.7 6.6 %copy-start.6 = (s32[1024]{0:T(1024)S(1)}, s32[1024]{0:T(1024)}, u32[]{:S(2)}) copy-start(s32[1024]{0:T(1024)} %param.8) | copy-start | bytes 12292

commit v4 on v2

--- a/solution.py
+++ b/solution.py
@@ -92,19 +92,23 @@
     partner_pos = (position + offsets) % group
     owners = my_block - position + partner_pos
     flags = pair_flags[offsets - 1, owners]
+    held_blocks = []
+    for offset in range(1, cycle_len + 1):
+        if offset == group:
+            held_blocks.append(spectra)
+        elif offset <= group // 2:
+            held_blocks.append(ahead[offset])
+        else:
+            held_blocks.append(behind[group - offset])
+    inner_power = lax.optimization_barrier(
+        [cross_power(held, spectra) for held in held_blocks[:-1]]
+    )
+    below_group, held_blocks = lax.optimization_barrier((below_group, held_blocks))
     power_rows = []
     for offset in range(1, cycle_len + 1):
-        if offset == group:
-            held = spectra
-        elif offset <= group // 2:
-            held = ahead[offset]
-        else:
-            held = behind[group - offset]
-        pair_power = cross_power(held, below_group)
+        pair_power = cross_power(held_blocks[offset - 1], below_group)
         if offset < group:
-            pair_power = jnp.where(
-                position + offset < group, cross_power(held, spectra), pair_power
-            )
+            pair_power = jnp.where(position + offset < group, inner_power[offset - 1], pair_power)
         power_rows.append(flags[offset - 1].astype(jnp.float32) * pair_power)
     power_table = jnp.stack(power_rows)
     k_onehot = (delay_kbin[:, None] == jnp.arange(num_kbins, dtype=jnp.int32)[None, :]).astype(

time: 153 us -> 162 us (1.059)
  other arithmetic: 14.1 us -> 25.1 us
  waiting for transfers between devices: 45.7 us -> 36.8 us
  blocking collectives: 44.7 us -> 51.3 us
    convert_element_type x7 -> x15, other arithmetic: 6.63 us -> 16.1 us  [cross_power(): own_f = own_block.astype(jnp.float32)]
    all_to_all x1, blocking collectives: 33.1 us -> 39.7 us  [per_device(): received = lax.all_to_all(partial_table, 'bl', 0, 0, tiled=True)]
    ppermute x1, waiting for transfers between devices: 23.9 us -> 18.6 us  [shifted(): return lax.ppermute(block, axis, route)]
    ppermute x7, waiting for transfers between devices: 21.8 us -> 18.2 us  [group_shifted(): return lax.ppermute(block, axis, route)]
    reduce_sum x2 -> x3, other arithmetic: 3.29 us -> 4.81 us  [cross_power(): return jnp.sum(own_f[0] * other_f[0] + own_f[1] * other_f[1], axis=0)]
  transfers between devices with their start and end apart: 8 -> 8, of which waited for: 5 -> 4; matrix products, arithmetic and copies ran while one was open for 8% -> 6% of each run, Pallas kernels for 0% -> 0%
where the time goes in v4:
time: 162 us; the launch traced here: 161 us
  blocking collectives  51.3 us (32%)
  waiting for transfers between devices  36.8 us (23%)
  starting transfers between devices  31.1 us (19%)
  other arithmetic  25.1 us (15%)
  local copies, waits for them, and re-layouts  6.15 us (4%)
  between operations  5.55 us (3%)
  matrix products  5.04 us (3%)
    all_to_all x1, blocking collectives, per_device(): received = lax.all_to_all(partial_table, 'bl', 0, 0, tiled=True)  39.7 us
    ppermute x7, starting transfers between devices, group_shifted(): return lax.ppermute(block, axis, route)  24.5 us
    ppermute x1, waiting for transfers between devices, shifted(): return lax.ppermute(block, axis, route)  18.6 us
    ppermute x7, waiting for transfers between devices, group_shifted(): return lax.ppermute(block, axis, route)  18.2 us
    convert_element_type x15, other arithmetic, cross_power(): own_f = own_block.astype(jnp.float32)  16.1 us
    psum x1, blocking collectives, per_device(): return lax.psum(jnp.sum(received, axis=0, keepdims=True), 'ta')  11.6 us
    ppermute x1, starting transfers between devices, shifted(): return lax.ppermute(block, axis, route)  6.65 us
    reduce_sum x3, other arithmetic, cross_power(): return jnp.sum(own_f[0] * other_f[0] + own_f[1] * other_f[1], axis=0)  4.81 us
  transfers between devices with their start and end apart: 8, of which 4 were waited for; matrix products, arithmetic and copies ran while one was open for 6% of the time, Pallas kernels for 0%

profile of v4, /device:TPU:1, one launch (start us, length us, event | category | flops | bytes accessed | tf_op | source)
XLA Modules:
  0.0 161.0 jit_solution(3153974028689572973)
XLA Ops:
  0.0 1.2 copy-done
  1.2 3.0 %convolution_bitcast_fusion = f32[512,1024]{1,0:T(8,128)S(1)} fusion(bf16[512,1024]{1,0:T(8,128)(2,1)S(1)} %bitcast.40, bf16[1024,1024]{1,0:T(8,128)(2,1)} %constant.57.clone), kind=kOutput, calls=%fused_computation.6 | convolution fusion | flops 1073741824 | bytes 5242880 | tf_op jit(solution)/shard_map/dot_general | solution.py:55
  4.2 1.3 convolution_bitcast_fusion.1
  6.0 1.2 fusion.42
  7.2 6.9 %collective-permute-start = (bf16[2,256,1024]{2,1,0:T(8,128)(2,1)}, bf16[2,256,1024]{2,1,0:T(8,128)(2,1)S(1)}, u32[]{:S(2)}, u32[]{:S(2)}) collective-permute-start(bf16[2,256,1024]{2,1,0:T(8,128)(2,1)} %get-tuple-element.36), channel_id=1, source_target_pairs={{0,28},{4,0},{8,4},{12,8},{16,12},{20,16},{24,20},{28,24},{32,60},... | collective-permute-start | bytes 3145736 | tf_op jit(solution)/shard_map/ppermute | solution.py:21
  14.1 8.7 %collective-permute-done = bf16[2,256,1024]{2,1,0:T(8,128)(2,1)S(1)} collective-permute-done((bf16[2,256,1024]{2,1,0:T(8,128)(2,1)}, bf16[2,256,1024]{2,1,0:T(8,128)(2,1)S(1)}, u32[]{:S(2)}, u32[]{:S(2)}) %collective-permute-start) | collective-permute-done | bytes 1048608 | tf_op jit(solution)/shard_map/ppermute | solution.py:21
  22.8 3.9 %collective-permute-start.1 = (bf16[2,256,1024]{2,1,0:T(8,128)(2,1)S(1)}, bf16[2,256,1024]{2,1,0:T(8,128)(2,1)S(1)}, u32[]{:S(2)}, u32[]{:S(2)}) collective-permute-start(bf16[2,256,1024]{2,1,0:T(8,128)(2,1)S(1)} %collective-permute-done), channel_id=1, source_target_pairs={{0,28},{4,0},{8,4},{12,8},{16,12},{20,16},{24,20},{28,24},{32,60},... | collective-permute-start | bytes 3145736 | tf_op jit(solution)/shard_map/ppermute | solution.py:21
  26.8 1.0 copy-done.4
  27.7 1.8 %collective-permute-start.5 = (bf16[2,256,1024]{2,1,0:T(8,128)(2,1)S(1)}, bf16[2,256,1024]{2,1,0:T(8,128)(2,1)}, u32[]{:S(2)}, u32[]{:S(2)}) collective-permute-start(bf16[2,256,1024]{2,1,0:T(8,128)(2,1)S(1)} %collective-permute-done.4), channel_id=1, source_target_pairs={{0,4},{4,8},{8,12},{12,16},{16,20},{20,24},{24,28},{28,0},{32,36},... | collective-permute-start | bytes 3145736 | tf_op jit(solution)/shard_map/ppermute | solution.py:21
  29.5 7.9 %collective-permute-done.1 = bf16[2,256,1024]{2,1,0:T(8,128)(2,1)S(1)} collective-permute-done((bf16[2,256,1024]{2,1,0:T(8,128)(2,1)S(1)}, bf16[2,256,1024]{2,1,0:T(8,128)(2,1)S(1)}, u32[]{:S(2)}, u32[]{:S(2)}) %collective-permute-start.1) | collective-permute-done | bytes 1048608 | tf_op jit(solution)/shard_map/ppermute | solution.py:21
  37.5 4.6 %collective-permute-start.2 = (bf16[2,256,1024]{2,1,0:T(8,128)(2,1)S(1)}, bf16[2,256,1024]{2,1,0:T(8,128)(2,1)}, u32[]{:S(2)}, u32[]{:S(2)}) collective-permute-start(bf16[2,256,1024]{2,1,0:T(8,128)(2,1)S(1)} %collective-permute-done.1), channel_id=1, source_target_pairs={{0,28},{4,0},{8,4},{12,8},{16,12},{20,16},{24,20},{28,24},{32,60},... | collective-permute-start | bytes 3145736 | tf_op jit(solution)/shard_map/ppermute | solution.py:21
  42.1 1.8 %collective-permute-start.6 = (bf16[2,256,1024]{2,1,0:T(8,128)(2,1)}, bf16[2,256,1024]{2,1,0:T(8,128)(2,1)}, u32[]{:S(2)}, u32[]{:S(2)}) collective-permute-start(bf16[2,256,1024]{2,1,0:T(8,128)(2,1)} %collective-permute-done.5), channel_id=1, source_target_pairs={{0,4},{4,8},{8,12},{12,16},{16,20},{20,24},{24,28},{28,0},{32,36},... | collective-permute-start | bytes 3145736 | tf_op jit(solution)/shard_map/ppermute | solution.py:21
  43.9 6.6 %collective-permute-start.7 = (bf16[2,256,1024]{2,1,0:T(8,128)(2,1)}, bf16[2,256,1024]{2,1,0:T(8,128)(2,1)}, u32[]{:S(2)}, u32[]{:S(2)}) collective-permute-start(bf16[2,256,1024]{2,1,0:T(8,128)(2,1)} %get-tuple-element.36), channel_id=1, source_target_pairs={{480,0},{484,4},{488,8},{492,12},{496,16},{500,20},{504,24},{508,2... | collective-permute-start | bytes 3145736 | tf_op jit(solution)/shard_map/ppermute | solution.py:15
  50.5 1.6 collective-permute-done.2
  52.1 5.4 %collective-permute-start.3 = (bf16[2,256,1024]{2,1,0:T(8,128)(2,1)}, bf16[2,256,1024]{2,1,0:T(8,128)(2,1)}, u32[]{:S(2)}, u32[]{:S(2)}) collective-permute-start(bf16[2,256,1024]{2,1,0:T(8,128)(2,1)} %collective-permute-done.2), channel_id=1, source_target_pairs={{0,28},{4,0},{8,4},{12,8},{16,12},{20,16},{24,20},{28,24},{32,60},... | collective-permute-start | bytes 3145736 | tf_op jit(solution)/shard_map/ppermute | solution.py:21
  65.4 1.5 convert_element_type.124
  68.4 1.5 convert_element_type.130
  69.9 1.5 convert_element_type.127
  71.4 1.5 convert_element_type.129
  72.9 18.6 %collective-permute-done.7 = bf16[2,256,1024]{2,1,0:T(8,128)(2,1)} collective-permute-done((bf16[2,256,1024]{2,1,0:T(8,128)(2,1)}, bf16[2,256,1024]{2,1,0:T(8,128)(2,1)}, u32[]{:S(2)}, u32[]{:S(2)}) %collective-permute-start.7) | collective-permute-done | bytes 1048608 | tf_op jit(solution)/shard_map/ppermute | solution.py:15
  91.5 1.5 convert_element_type.133
  93.0 1.5 convert_element_type.139
  94.4 1.5 convert_element_type.142
  95.9 1.5 convert_element_type.145
  97.4 1.6 convert_element_type.154
  99.5 1.5 convert_element_type.148
  101.2 1.5 convert_element_type.128
  102.7 2.2 %fusion.19 = (f32[1024]{0:T(1024)S(1)}, f32[1024]{0:T(1024)S(1)}, f32[1024]{0:T(1024)S(1)}, f32[1024]{0:T(1024)S(1)}, f32[1024]{0:T(1024)S(1)}, /*index=5*/f32[1024]{0:T(1024)S(1)}, f32[1024]{0:T(1024)S(1)}) fusion(f32[2,256,1024]{2,1,0:T(8,128)S(1)} %convert_element_type.131, f32[2,256,1024]{2,1,0:T(8,128)S(1)} %get-tuple-element.57, ...), kind=kLoop, calls=%fused_computation.43 | loop fusion | flops 7332864 | bytes 16805888 | tf_op jit(solution)/shard_map/reduce_sum | solution.py:66
  104.9 1.3 fusion.3
  106.2 1.3 fusion.5
  109.5 39.7 %all_to_all.9 = f32[128,1,512]{2,1,0:T(1,128)S(1)} all-to-all(f32[128,1,512]{2,1,0:T(1,128)S(1)} %copy.8), channel_id=1, replica_groups=mesh['bl'=128,'ta'=4] {'bl'}, dimensions={0} | all-to-all | bytes 524288 | tf_op jit(solution)/shard_map/all_to_all | solution.py:124
  149.4 11.6 %psum.7 = f32[1,512]{1,0:T(1,128)} all-reduce(f32[1,512]{1,0:T(1,128)S(1)} %bitcast.51), channel_id=1, replica_groups=mesh['bl'=128,'ta'=4] {'ta'}, use_global_device_ids=true, to_apply=%region_17.18 | all-reduce | flops 512 | bytes 4096 | tf_op jit(solution)/shard_map/psum | solution.py:125
  (55 shorter events, 7.5 us)
Async XLA Ops:
  0.0 1.2 copy-start
  1.2 3.0 %copy-start.11 = (bf16[1024,1024]{1,0:T(8,128)(2,1)S(1)}, bf16[1024,1024]{1,0:T(8,128)(2,1)}, u32[]{:S(2)}) copy-start(bf16[1024,1024]{1,0:T(8,128)(2,1)} %constant.56.clone) | copy-start | bytes 6291460
  6.0 51.5 %copy-start.3 = (s32[8,128]{1,0:T(8,128)S(1)}, s32[8,128]{1,0:T(8,128)}, u32[]{:S(2)}) copy-start(s32[8,128]{1,0:T(8,128)} %param.11) | copy-start | bytes 12292
  6.0 58.0 %copy-start.1 = (s32[128]{0:T(128)S(1)}, s32[128]{0:T(128)}, u32[]{:S(2)}) copy-start(s32[128]{0:T(128)} %param.9) | copy-start | bytes 1540
  6.0 58.7 %copy-start.2 = (s32[128]{0:T(128)S(1)}, s32[128]{0:T(128)}, u32[]{:S(2)}) copy-start(s32[128]{0:T(128)} %param.10) | copy-start | bytes 1540
  7.2 15.6 %collective-permute-start = (bf16[2,256,1024]{2,1,0:T(8,128)(2,1)}, bf16[2,256,1024]{2,1,0:T(8,128)(2,1)S(1)}, u32[]{:S(2)}, u32[]{:S(2)}) collective-permute-start(bf16[2,256,1024]{2,1,0:T(8,128)(2,1)} %get-tuple-element.36), channel_id=1, source_target_pairs={{0,28},{4,0},{8,4},{12,8},{16,12},{20,16},{24,20},{28,24},{32,60},... | collective-permute-start | bytes 3145736 | tf_op jit(solution)/shard_map/ppermute | solution.py:21
  14.1 12.6 %collective-permute-start.4 = (bf16[2,256,1024]{2,1,0:T(8,128)(2,1)}, bf16[2,256,1024]{2,1,0:T(8,128)(2,1)S(1)}, u32[]{:S(2)}, u32[]{:S(2)}) collective-permute-start(bf16[2,256,1024]{2,1,0:T(8,128)(2,1)} %get-tuple-element.36), channel_id=1, source_target_pairs={{0,4},{4,8},{8,12},{12,16},{16,20},{20,24},{24,28},{28,0},{32,36},... | collective-permute-start | bytes 3145736 | tf_op jit(solution)/shard_map/ppermute | solution.py:21
  22.8 19.3 %copy-start.6 = (bf16[2,256,1024]{2,1,0:T(8,128)(2,1)}, bf16[2,256,1024]{2,1,0:T(8,128)(2,1)S(1)}, u32[]{:S(2)}) copy-start(bf16[2,256,1024]{2,1,0:T(8,128)(2,1)S(1)} %collective-permute-done) | copy-start | bytes 3145732
  22.8 14.6 %collective-permute-start.1 = (bf16[2,256,1024]{2,1,0:T(8,128)(2,1)S(1)}, bf16[2,256,1024]{2,1,0:T(8,128)(2,1)S(1)}, u32[]{:S(2)}, u32[]{:S(2)}) collective-permute-start(bf16[2,256,1024]{2,1,0:T(8,128)(2,1)S(1)} %collective-permute-done), channel_id=1, source_target_pairs={{0,28},{4,0},{8,4},{12,8},{16,12},{20,16},{24,20},{28,24},{32,60},... | collective-permute-start | bytes 3145736 | tf_op jit(solution)/shard_map/ppermute | solution.py:21
  26.8 1.0 copy-start.4
  27.7 14.4 %collective-permute-start.5 = (bf16[2,256,1024]{2,1,0:T(8,128)(2,1)S(1)}, bf16[2,256,1024]{2,1,0:T(8,128)(2,1)}, u32[]{:S(2)}, u32[]{:S(2)}) collective-permute-start(bf16[2,256,1024]{2,1,0:T(8,128)(2,1)S(1)} %collective-permute-done.4), channel_id=1, source_target_pairs={{0,4},{4,8},{8,12},{12,16},{16,20},{20,24},{24,28},{28,0},{32,36},... | collective-permute-start | bytes 3145736 | tf_op jit(solution)/shard_map/ppermute | solution.py:21
  37.5 6.4 %copy-start.8 = (bf16[2,256,1024]{2,1,0:T(8,128)(2,1)}, bf16[2,256,1024]{2,1,0:T(8,128)(2,1)S(1)}, u32[]{:S(2)}) copy-start(bf16[2,256,1024]{2,1,0:T(8,128)(2,1)S(1)} %collective-permute-done.1) | copy-start | bytes 3145732
  37.5 14.6 %collective-permute-start.2 = (bf16[2,256,1024]{2,1,0:T(8,128)(2,1)S(1)}, bf16[2,256,1024]{2,1,0:T(8,128)(2,1)}, u32[]{:S(2)}, u32[]{:S(2)}) collective-permute-start(bf16[2,256,1024]{2,1,0:T(8,128)(2,1)S(1)} %collective-permute-done.1), channel_id=1, source_target_pairs={{0,28},{4,0},{8,4},{12,8},{16,12},{20,16},{24,20},{28,24},{32,60},... | collective-permute-start | bytes 3145736 | tf_op jit(solution)/shard_map/ppermute | solution.py:21
  42.1 29.3 %collective-permute-start.6 = (bf16[2,256,1024]{2,1,0:T(8,128)(2,1)}, bf16[2,256,1024]{2,1,0:T(8,128)(2,1)}, u32[]{:S(2)}, u32[]{:S(2)}) collective-permute-start(bf16[2,256,1024]{2,1,0:T(8,128)(2,1)} %collective-permute-done.5), channel_id=1, source_target_pairs={{0,4},{4,8},{8,12},{12,16},{16,20},{20,24},{24,28},{28,0},{32,36},... | collective-permute-start | bytes 3145736 | tf_op jit(solution)/shard_map/ppermute | solution.py:21
  43.9 47.6 %collective-permute-start.7 = (bf16[2,256,1024]{2,1,0:T(8,128)(2,1)}, bf16[2,256,1024]{2,1,0:T(8,128)(2,1)}, u32[]{:S(2)}, u32[]{:S(2)}) collective-permute-start(bf16[2,256,1024]{2,1,0:T(8,128)(2,1)} %get-tuple-element.36), channel_id=1, source_target_pairs={{480,0},{484,4},{488,8},{492,12},{496,16},{500,20},{504,24},{508,2... | collective-permute-start | bytes 3145736 | tf_op jit(solution)/shard_map/ppermute | solution.py:15
  52.1 39.4 %collective-permute-start.3 = (bf16[2,256,1024]{2,1,0:T(8,128)(2,1)}, bf16[2,256,1024]{2,1,0:T(8,128)(2,1)}, u32[]{:S(2)}, u32[]{:S(2)}) collective-permute-start(bf16[2,256,1024]{2,1,0:T(8,128)(2,1)} %collective-permute-done.2), channel_id=1, source_target_pairs={{0,28},{4,0},{8,4},{12,8},{16,12},{20,16},{24,20},{28,24},{32,60},... | collective-permute-start | bytes 3145736 | tf_op jit(solution)/shard_map/ppermute | solution.py:21
  65.4 1.6 copy-start.5
  67.0 1.2 copy-start.9
  97.4 1.6 copy-start.7
  106.2 1.5 copy-start.10

commit v5 on v4

--- a/solution.py
+++ b/solution.py
@@ -103,7 +103,7 @@
     inner_power = lax.optimization_barrier(
         [cross_power(held, spectra) for held in held_blocks[:-1]]
     )
-    below_group, held_blocks = lax.optimization_barrier((below_group, held_blocks))
+    below_group, ahead[3], behind[3] = lax.optimization_barrier((below_group, ahead[3], behind[3]))
     power_rows = []
     for offset in range(1, cycle_len + 1):
         pair_power = cross_power(held_blocks[offset - 1], below_group)

time: 162 us -> 155 us (0.957)
  other arithmetic: 25.1 us -> 16.6 us
  waiting for transfers between devices: 36.8 us -> 43.7 us
  starting transfers between devices: 31.1 us -> 27.3 us
    convert_element_type x15 -> x7, other arithmetic: 16.1 us -> 9.09 us  [cross_power(): own_f = own_block.astype(jnp.float32)]
    ppermute x1, waiting for transfers between devices: 18.6 us -> 25.1 us  [shifted(): return lax.ppermute(block, axis, route)]
    ppermute x7, starting transfers between devices: 24.5 us -> 19.8 us  [group_shifted(): return lax.ppermute(block, axis, route)]
    reduce_sum x3 -> x2, other arithmetic: 4.81 us -> 3.3 us  [cross_power(): return jnp.sum(own_f[0] * other_f[0] + own_f[1] * other_f[1], axis=0)]
  transfers between devices with their start and end apart: 8 -> 8, of which waited for: 4 -> 3; matrix products, arithmetic and copies ran while one was open for 6% -> 9% of each run, Pallas kernels for 0% -> 0%
where the time goes in v5:
time: 155 us; the launch traced here: 154 us
  blocking collectives  50.9 us (33%)
  waiting for transfers between devices  43.7 us (28%)
  starting transfers between devices  27.3 us (18%)
  other arithmetic  16.6 us (11%)
  between operations  5.21 us (3%)
  local copies, waits for them, and re-layouts  5.18 us (3%)
  matrix products  5.04 us (3%)
    all_to_all x1, blocking collectives, per_device(): received = lax.all_to_all(partial_table, 'bl', 0, 0, tiled=True)  39.3 us
    ppermute x1, waiting for transfers between devices, shifted(): return lax.ppermute(block, axis, route)  25.1 us
    ppermute x7, starting transfers between devices, group_shifted(): return lax.ppermute(block, axis, route)  19.8 us
    ppermute x7, waiting for transfers between devices, group_shifted(): return lax.ppermute(block, axis, route)  18.6 us
    psum x1, blocking collectives, per_device(): return lax.psum(jnp.sum(received, axis=0, keepdims=True), 'ta')  11.5 us
    convert_element_type x7, other arithmetic, cross_power(): own_f = own_block.astype(jnp.float32)  9.09 us
    ppermute x1, starting transfers between devices, shifted(): return lax.ppermute(block, axis, route)  7.45 us
    reduce_sum x2, other arithmetic, cross_power(): return jnp.sum(own_f[0] * other_f[0] + own_f[1] * other_f[1], axis=0)  3.3 us
  transfers between devices with their start and end apart: 8, of which 3 were waited for; matrix products, arithmetic and copies ran while one was open for 9% of the time, Pallas kernels for 0%

profile of v5, /device:TPU:1, one launch (start us, length us, event | category | flops | bytes accessed | tf_op | source)
XLA Modules:
  0.0 153.8 jit_solution(7918455055706856760)
XLA Ops:
  0.0 1.2 copy-done
  1.2 3.0 %convolution_bitcast_fusion = f32[512,1024]{1,0:T(8,128)S(1)} fusion(bf16[512,1024]{1,0:T(8,128)(2,1)S(1)} %bitcast.40, bf16[1024,1024]{1,0:T(8,128)(2,1)} %constant.57.clone), kind=kOutput, calls=%fused_computation.6 | convolution fusion | flops 1073741824 | bytes 5242880 | tf_op jit(solution)/shard_map/dot_general | solution.py:55
  4.2 1.3 convolution_bitcast_fusion.1
  6.1 1.2 fusion.12
  7.3 6.9 %collective-permute-start = (bf16[2,256,1024]{2,1,0:T(8,128)(2,1)}, bf16[2,256,1024]{2,1,0:T(8,128)(2,1)S(1)}, u32[]{:S(2)}, u32[]{:S(2)}) collective-permute-start(bf16[2,256,1024]{2,1,0:T(8,128)(2,1)} %get-tuple-element.47), channel_id=1, source_target_pairs={{0,28},{4,0},{8,4},{12,8},{16,12},{20,16},{24,20},{28,24},{32,60},... | collective-permute-start | bytes 3145736 | tf_op jit(solution)/shard_map/ppermute | solution.py:21
  14.1 8.7 %collective-permute-done = bf16[2,256,1024]{2,1,0:T(8,128)(2,1)S(1)} collective-permute-done((bf16[2,256,1024]{2,1,0:T(8,128)(2,1)}, bf16[2,256,1024]{2,1,0:T(8,128)(2,1)S(1)}, u32[]{:S(2)}, u32[]{:S(2)}) %collective-permute-start) | collective-permute-done | bytes 1048608 | tf_op jit(solution)/shard_map/ppermute | solution.py:21
  22.8 1.0 copy-done.4
  23.8 3.9 %collective-permute-start.1 = (bf16[2,256,1024]{2,1,0:T(8,128)(2,1)S(1)}, bf16[2,256,1024]{2,1,0:T(8,128)(2,1)}, u32[]{:S(2)}, u32[]{:S(2)}) collective-permute-start(bf16[2,256,1024]{2,1,0:T(8,128)(2,1)S(1)} %collective-permute-done), channel_id=1, source_target_pairs={{0,28},{4,0},{8,4},{12,8},{16,12},{20,16},{24,20},{28,24},{32,60},... | collective-permute-start | bytes 3145736 | tf_op jit(solution)/shard_map/ppermute | solution.py:21
  27.8 0.8 collective-permute-start.5
  28.6 9.9 %collective-permute-done.1 = bf16[2,256,1024]{2,1,0:T(8,128)(2,1)} collective-permute-done((bf16[2,256,1024]{2,1,0:T(8,128)(2,1)S(1)}, bf16[2,256,1024]{2,1,0:T(8,128)(2,1)}, u32[]{:S(2)}, u32[]{:S(2)}) %collective-permute-start.1) | collective-permute-done | bytes 1048608 | tf_op jit(solution)/shard_map/ppermute | solution.py:21
  38.5 4.6 %collective-permute-start.2 = (bf16[2,256,1024]{2,1,0:T(8,128)(2,1)}, bf16[2,256,1024]{2,1,0:T(8,128)(2,1)}, u32[]{:S(2)}, u32[]{:S(2)}) collective-permute-start(bf16[2,256,1024]{2,1,0:T(8,128)(2,1)} %collective-permute-done.1), channel_id=1, source_target_pairs={{0,28},{4,0},{8,4},{12,8},{16,12},{20,16},{24,20},{28,24},{32,60},... | collective-permute-start | bytes 3145736 | tf_op jit(solution)/shard_map/ppermute | solution.py:21
  43.1 7.4 %collective-permute-start.7 = (bf16[2,256,1024]{2,1,0:T(8,128)(2,1)}, bf16[2,256,1024]{2,1,0:T(8,128)(2,1)}, u32[]{:S(2)}, u32[]{:S(2)}) collective-permute-start(bf16[2,256,1024]{2,1,0:T(8,128)(2,1)} %get-tuple-element.47), channel_id=1, source_target_pairs={{480,0},{484,4},{488,8},{492,12},{496,16},{500,20},{504,24},{508,2... | collective-permute-start | bytes 3145736 | tf_op jit(solution)/shard_map/ppermute | solution.py:15
  50.6 0.6 collective-permute-start.6
  51.2 0.6 gather_fusion.2
  51.8 0.7 fusion.13
  57.4 0.6 gather_fusion
  58.1 3.0 %collective-permute-start.3 = (bf16[2,256,1024]{2,1,0:T(8,128)(2,1)}, bf16[2,256,1024]{2,1,0:T(8,128)(2,1)}, u32[]{:S(2)}, u32[]{:S(2)}) collective-permute-start(bf16[2,256,1024]{2,1,0:T(8,128)(2,1)} %collective-permute-done.2), channel_id=1, source_target_pairs={{0,28},{4,0},{8,4},{12,8},{16,12},{20,16},{24,20},{28,24},{32,60},... | collective-permute-start | bytes 3145736 | tf_op jit(solution)/shard_map/ppermute | solution.py:21
  61.0 0.6 gather_fusion.1
  61.7 1.5 %convert_element_type.115 = f32[2,256,1024]{2,1,0:T(8,128)S(1)} convert(bf16[2,256,1024]{2,1,0:T(8,128)(2,1)} %copy-done.6) | non-fusion elementwise | flops 524288 | bytes 3145728 | tf_op jit(solution)/shard_map/convert_element_type | solution.py:64
  63.5 1.5 convert_element_type.110
  65.0 1.5 convert_element_type.114
  66.5 25.1 %collective-permute-done.7 = bf16[2,256,1024]{2,1,0:T(8,128)(2,1)} collective-permute-done((bf16[2,256,1024]{2,1,0:T(8,128)(2,1)}, bf16[2,256,1024]{2,1,0:T(8,128)(2,1)}, u32[]{:S(2)}, u32[]{:S(2)}) %collective-permute-start.7) | collective-permute-done | bytes 1048608 | tf_op jit(solution)/shard_map/ppermute | solution.py:15
  91.5 1.5 convert_element_type.116
  93.0 1.5 convert_element_type.113
  94.5 1.5 convert_element_type.111
  95.9 1.6 %add_reduce_fusion.6 = (f32[1024]{0:T(1024)S(1)}, f32[1024]{0:T(1024)S(1)}, f32[1024]{0:T(1024)S(1)}, f32[1024]{0:T(1024)S(1)}, f32[1024]{0:T(1024)S(1)}, /*index=5*/f32[1024]{0:T(1024)S(1)}, f32[1024]{0:T(1024)S(1)}) fusion(f32[2,256,1024]{2,1,0:T(8,128)S(1)} %convert_element_type.110, f32[2,256,1024]{2,1,0:T(8,128)S(1)} %convert_element_type.116, ...), kind=kLoop, calls=%fused_computation.21 | loop fusion | flops 7332864 | bytes 12611584 | tf_op jit(solution)/shard_map/reduce_sum | solution.py:66
  97.6 1.5 convert_element_type.112
  99.1 1.7 %add_reduce_fusion.1 = (f32[1024]{0:T(1024)S(1)}, f32[1024]{0:T(1024)S(1)}, f32[1024]{0:T(1024)S(1)}, f32[1024]{0:T(1024)S(1)}, f32[1024]{0:T(1024)S(1)}, /*inde...) fusion(f32[2,256,1024]{2,1,0:T(8,128)S(1)} %convert_element_type.115, ...), kind=kLoop, calls=%fused_computation.16 | loop fusion | flops 8380416 | bytes 12615680 | tf_op jit(solution)/shard_map/reduce_sum | solution.py:66
  101.0 0.8 fusion.1
  101.8 0.6 multiply_reduce_fusion
  102.7 39.3 %all_to_all.9 = f32[128,1,512]{2,1,0:T(1,128)S(1)} all-to-all(f32[128,1,512]{2,1,0:T(1,128)S(1)} %copy.8), channel_id=1, replica_groups=mesh['bl'=128,'ta'=4] {'bl'}, dimensions={0} | all-to-all | bytes 524288 | tf_op jit(solution)/shard_map/all_to_all | solution.py:124
  142.2 11.5 %psum.7 = f32[1,512]{1,0:T(1,128)} all-reduce(f32[1,512]{1,0:T(1,128)S(1)} %bitcast.51), channel_id=1, replica_groups=mesh['bl'=128,'ta'=4] {'ta'}, use_global_device_ids=true, to_apply=%region_17.18 | all-reduce | flops 512 | bytes 4096 | tf_op jit(solution)/shard_map/psum | solution.py:125
  (40 shorter events, 1.5 us)
Async XLA Ops:
  0.0 1.2 copy-start
  1.2 3.0 %copy-start.8 = (bf16[1024,1024]{1,0:T(8,128)(2,1)S(1)}, bf16[1024,1024]{1,0:T(8,128)(2,1)}, u32[]{:S(2)}) copy-start(bf16[1024,1024]{1,0:T(8,128)(2,1)} %constant.56.clone) | copy-start | bytes 6291460
  6.0 45.1 %copy-start.3 = (s32[8,128]{1,0:T(8,128)S(1)}, s32[8,128]{1,0:T(8,128)}, u32[]{:S(2)}) copy-start(s32[8,128]{1,0:T(8,128)} %param.11) | copy-start | bytes 12292
  6.0 51.4 %copy-start.1 = (s32[128]{0:T(128)S(1)}, s32[128]{0:T(128)}, u32[]{:S(2)}) copy-start(s32[128]{0:T(128)} %param.9) | copy-start | bytes 1540
  6.1 55.0 %copy-start.2 = (s32[128]{0:T(128)S(1)}, s32[128]{0:T(128)}, u32[]{:S(2)}) copy-start(s32[128]{0:T(128)} %param.10) | copy-start | bytes 1540
  7.3 15.6 %collective-permute-start = (bf16[2,256,1024]{2,1,0:T(8,128)(2,1)}, bf16[2,256,1024]{2,1,0:T(8,128)(2,1)S(1)}, u32[]{:S(2)}, u32[]{:S(2)}) collective-permute-start(bf16[2,256,1024]{2,1,0:T(8,128)(2,1)} %get-tuple-element.47), channel_id=1, source_target_pairs={{0,28},{4,0},{8,4},{12,8},{16,12},{20,16},{24,20},{28,24},{32,60},... | collective-permute-start | bytes 3145736 | tf_op jit(solution)/shard_map/ppermute | solution.py:21
  14.1 13.6 %collective-permute-start.4 = (bf16[2,256,1024]{2,1,0:T(8,128)(2,1)}, bf16[2,256,1024]{2,1,0:T(8,128)(2,1)S(1)}, u32[]{:S(2)}, u32[]{:S(2)}) collective-permute-start(bf16[2,256,1024]{2,1,0:T(8,128)(2,1)} %get-tuple-element.47), channel_id=1, source_target_pairs={{0,4},{4,8},{8,12},{12,16},{16,20},{20,24},{24,28},{28,0},{32,36},... | collective-permute-start | bytes 3145736 | tf_op jit(solution)/shard_map/ppermute | solution.py:21
  22.8 1.0 copy-start.4
  23.8 14.6 %collective-permute-start.1 = (bf16[2,256,1024]{2,1,0:T(8,128)(2,1)S(1)}, bf16[2,256,1024]{2,1,0:T(8,128)(2,1)}, u32[]{:S(2)}, u32[]{:S(2)}) collective-permute-start(bf16[2,256,1024]{2,1,0:T(8,128)(2,1)S(1)} %collective-permute-done), channel_id=1, source_target_pairs={{0,28},{4,0},{8,4},{12,8},{16,12},{20,16},{24,20},{28,24},{32,60},... | collective-permute-start | bytes 3145736 | tf_op jit(solution)/shard_map/ppermute | solution.py:21
  27.8 10.7 %copy-start.6 = (bf16[2,256,1024]{2,1,0:T(8,128)(2,1)}, bf16[2,256,1024]{2,1,0:T(8,128)(2,1)S(1)}, u32[]{:S(2)}) copy-start(bf16[2,256,1024]{2,1,0:T(8,128)(2,1)S(1)} %collective-permute-done.4) | copy-start | bytes 3145732
  27.8 22.8 %collective-permute-start.5 = (bf16[2,256,1024]{2,1,0:T(8,128)(2,1)S(1)}, bf16[2,256,1024]{2,1,0:T(8,128)(2,1)}, u32[]{:S(2)}, u32[]{:S(2)}) collective-permute-start(bf16[2,256,1024]{2,1,0:T(8,128)(2,1)S(1)} %collective-permute-done.4), channel_id=1, source_target_pairs={{0,4},{4,8},{8,12},{12,16},{16,20},{20,24},{24,28},{28,0},{32,36},... | collective-permute-start | bytes 3145736 | tf_op jit(solution)/shard_map/ppermute | solution.py:21
  38.5 19.6 %collective-permute-start.2 = (bf16[2,256,1024]{2,1,0:T(8,128)(2,1)}, bf16[2,256,1024]{2,1,0:T(8,128)(2,1)}, u32[]{:S(2)}, u32[]{:S(2)}) collective-permute-start(bf16[2,256,1024]{2,1,0:T(8,128)(2,1)} %collective-permute-done.1), channel_id=1, source_target_pairs={{0,28},{4,0},{8,4},{12,8},{16,12},{20,16},{24,20},{28,24},{32,60},... | collective-permute-start | bytes 3145736 | tf_op jit(solution)/shard_map/ppermute | solution.py:21
  43.1 48.4 %collective-permute-start.7 = (bf16[2,256,1024]{2,1,0:T(8,128)(2,1)}, bf16[2,256,1024]{2,1,0:T(8,128)(2,1)}, u32[]{:S(2)}, u32[]{:S(2)}) collective-permute-start(bf16[2,256,1024]{2,1,0:T(8,128)(2,1)} %get-tuple-element.47), channel_id=1, source_target_pairs={{480,0},{484,4},{488,8},{492,12},{496,16},{500,20},{504,24},{508,2... | collective-permute-start | bytes 3145736 | tf_op jit(solution)/shard_map/ppermute | solution.py:15
  50.6 41.0 %collective-permute-start.6 = (bf16[2,256,1024]{2,1,0:T(8,128)(2,1)}, bf16[2,256,1024]{2,1,0:T(8,128)(2,1)}, u32[]{:S(2)}, u32[]{:S(2)}) collective-permute-start(bf16[2,256,1024]{2,1,0:T(8,128)(2,1)} %collective-permute-done.5), channel_id=1, source_target_pairs={{0,4},{4,8},{8,12},{12,16},{16,20},{20,24},{24,28},{28,0},{32,36},... | collective-permute-start | bytes 3145736 | tf_op jit(solution)/shard_map/ppermute | solution.py:21
  58.1 39.5 %collective-permute-start.3 = (bf16[2,256,1024]{2,1,0:T(8,128)(2,1)}, bf16[2,256,1024]{2,1,0:T(8,128)(2,1)}, u32[]{:S(2)}, u32[]{:S(2)}) collective-permute-start(bf16[2,256,1024]{2,1,0:T(8,128)(2,1)} %collective-permute-done.2), channel_id=1, source_target_pairs={{0,28},{4,0},{8,4},{12,8},{16,12},{20,16},{24,20},{28,24},{32,60},... | collective-permute-start | bytes 3145736 | tf_op jit(solution)/shard_map/ppermute | solution.py:21
  61.7 1.6 %copy-start.5 = (bf16[2,256,1024]{2,1,0:T(8,128)(2,1)S(1)}, bf16[2,256,1024]{2,1,0:T(8,128)(2,1)}, u32[]{:S(2)}) copy-start(bf16[2,256,1024]{2,1,0:T(8,128)(2,1)} %copy-done.4) | copy-start | bytes 3145732
  99.1 1.9 %copy-start.7 = (s32[1024]{0:T(1024)S(1)}, s32[1024]{0:T(1024)}, u32[]{:S(2)}) copy-start(s32[1024]{0:T(1024)} %param.8) | copy-start | bytes 12292

commit v6 on v2

--- a/solution.py
+++ b/solution.py
@@ -19,6 +19,32 @@
     devices = range(lax.axis_size(axis))
     route = [(i, i - i % group + (i + distance) % group) for i in devices]
     return lax.ppermute(block, axis, route)
+
+
+def vertical_import(block, group):
+    num_blocks = lax.axis_size("bl")
+    num_ta = lax.axis_size("ta")
+    z_ring = 2 * num_ta
+
+    def flat(bl, ta):
+        return bl * num_ta + ta
+
+    def down_z(bl, ta):
+        z_hi = (bl // group) % 2
+        z = (z_hi * num_ta + ta - 1) % z_ring
+        new_bl = bl + ((z // num_ta) - z_hi) * group
+        return new_bl, z % num_ta
+
+    pairs = [(b, t) for b in range(num_blocks) for t in range(num_ta)]
+    target = {(b, t): ((b + group) % num_blocks, t) for b, t in pairs}
+    direct = [(flat(*p), flat(*target[p])) for p in pairs]
+    to_relay = [(flat(*p), flat(*down_z(*p))) for p in pairs]
+    from_relay = [(flat(*down_z(*p)), flat(*target[p])) for p in pairs]
+    split = block.shape[-1] // 2
+    axes = ("bl", "ta")
+    low = lax.ppermute(block[..., :split], axes, direct)
+    high = lax.ppermute(lax.ppermute(block[..., split:], axes, to_relay), axes, from_relay)
+    return jnp.concatenate([low, high], axis=-1)
 
 
 def delay_tables(num_chans):
@@ -81,7 +107,7 @@
     num_blocks = lax.axis_size("bl")
     group = cycle_len
     position = my_block % group
-    below_group = shifted(spectra, "bl", group)
+    below_group = vertical_import(spectra, group)
     ahead = [spectra]
     behind = [spectra]
     for _ in range(group // 2):

time: 153 us -> 186 us (1.22)
  starting transfers between devices: 31.7 us -> 49.6 us
  waiting for transfers between devices: 45.7 us -> 56.7 us
  blocking collectives: 44.7 us -> 48.2 us
  other arithmetic: 14.1 us -> 16.3 us
    ppermute x1 -> x3, starting transfers between devices: 7.45 us -> 28.8 us  [the longest x1 19.4 us: vertical_import(): lax.ppermute(lax.ppermute(block[..., split:], axes, to_relay), axes, from...]
    ppermute x1 -> x3, waiting for transfers between devices: 23.9 us -> 36.8 us  [the longest x1 36.1 us: vertical_import(): lax.ppermute(lax.ppermute(block[..., split:], axes, to_relay), axes, from...]
    all_to_all x1, blocking collectives: 33.1 us -> 41 us  [per_device(): received = lax.all_to_all(partial_table, 'bl', 0, 0, tiled=True)]
    psum x1, blocking collectives: 11.6 us -> 7.2 us  [per_device(): return lax.psum(jnp.sum(received, axis=0, keepdims=True), 'ta')]
    ppermute x7, starting transfers between devices: 24.3 us -> 20.8 us  [group_shifted(): return lax.ppermute(block, axis, route)]
    ppermute x7, waiting for transfers between devices: 21.8 us -> 19.9 us  [group_shifted(): return lax.ppermute(block, axis, route)]
  transfers between devices with their start and end apart: 8 -> 10, of which waited for: 5 -> 5; matrix products, arithmetic and copies ran while one was open for 8% -> 8% of each run, Pallas kernels for 0% -> 0%
where the time goes in v6:
time: 186 us
  waiting for transfers between devices  56.7 us (30%)
  starting transfers between devices  49.6 us (27%)
  blocking collectives  48.2 us (26%)
  other arithmetic  16.3 us (9%)
  between operations  5.44 us (3%)
  matrix products  5.04 us (3%)
  local copies, waits for them, and re-layouts  4.19 us (2%)
    all_to_all x1, blocking collectives, per_device(): received = lax.all_to_all(partial_table, 'bl', 0, 0, tiled=True)  41 us
    ppermute x1, waiting for transfers between devices, vertical_import(): lax.ppermute(lax.ppermute(block[..., split:], axes, to_relay), axes, from...  36.1 us
    ppermute x7, starting transfers between devices, group_shifted(): return lax.ppermute(block, axis, route)  20.8 us
    ppermute x7, waiting for transfers between devices, group_shifted(): return lax.ppermute(block, axis, route)  19.9 us
    ppermute x1, starting transfers between devices, vertical_import(): lax.ppermute(lax.ppermute(block[..., split:], axes, to_relay), axes, from...  19.4 us
    convert_element_type x7, other arithmetic, cross_power(): own_f = own_block.astype(jnp.float32)  7.77 us
    ppermute x1, starting transfers between devices, vertical_import(): lax.ppermute(block[..., split:], axes, to_relay)  7.48 us
    psum x1, blocking collectives, per_device(): return lax.psum(jnp.sum(received, axis=0, keepdims=True), 'ta')  7.2 us
  transfers between devices with their start and end apart: 10, of which 5 were waited for; matrix products, arithmetic and copies ran while one was open for 8% of the time, Pallas kernels for 0%

profile of v6, /device:TPU:1, one launch (start us, length us, event | category | flops | bytes accessed | tf_op | source)
XLA Modules:
  0.0 185.5 jit_solution(1156075702752645930)
XLA Ops:
  0.0 1.2 copy-done
  1.2 3.0 %convolution_bitcast_fusion = f32[512,1024]{1,0:T(8,128)S(1)} fusion(bf16[512,1024]{1,0:T(8,128)(2,1)S(1)} %bitcast.40, bf16[1024,1024]{1,0:T(8,128)(2,1)} %constant.57.clone), kind=kOutput, calls=%fused_computation.6 | convolution fusion | flops 1073741824 | bytes 5242880 | tf_op jit(solution)/shard_map/dot_general | solution.py:81
  4.2 1.3 convolution_bitcast_fusion.1
  6.0 1.2 fusion.14
  7.2 6.9 %collective-permute-start = (bf16[2,256,1024]{2,1,0:T(8,128)(2,1)}, bf16[2,256,1024]{2,1,0:T(8,128)(2,1)}, u32[]{:S(2)}, u32[]{:S(2)}) collective-permute-start(bf16[2,256,1024]{2,1,0:T(8,128)(2,1)} %get-tuple-element.30), channel_id=1, source_target_pairs={{0,28},{4,0},{8,4},{12,8},{16,12},{20,16},{24,20},{28,24},{32,60},... | collective-permute-start | bytes 3145736 | tf_op jit(solution)/shard_map/ppermute | solution.py:21
  14.1 8.8 %collective-permute-done = bf16[2,256,1024]{2,1,0:T(8,128)(2,1)} collective-permute-done((bf16[2,256,1024]{2,1,0:T(8,128)(2,1)}, bf16[2,256,1024]{2,1,0:T(8,128)(2,1)}, u32[]{:S(2)}, u32[]{:S(2)}) %collective-permute-start) | collective-permute-done | bytes 1048608 | tf_op jit(solution)/shard_map/ppermute | solution.py:21
  22.9 3.8 %collective-permute-start.4 = (bf16[2,256,1024]{2,1,0:T(8,128)(2,1)}, bf16[2,256,1024]{2,1,0:T(8,128)(2,1)}, u32[]{:S(2)}, u32[]{:S(2)}) collective-permute-start(bf16[2,256,1024]{2,1,0:T(8,128)(2,1)} %collective-permute-done), channel_id=1, source_target_pairs={{0,28},{4,0},{8,4},{12,8},{16,12},{20,16},{24,20},{28,24},{32,60},... | collective-permute-start | bytes 3145736 | tf_op jit(solution)/shard_map/ppermute | solution.py:21
  26.7 1.1 fusion.7
  27.9 7.5 %collective-permute-start.2 = (bf16[2,256,512]{2,1,0:T(8,128)(2,1)}, bf16[2,256,512]{2,1,0:T(8,128)(2,1)}, u32[]{:S(2)}, u32[]{:S(2)}) collective-permute-start(bf16[2,256,512]{2,1,0:T(8,128)(2,1)} %get-tuple-element.32), channel_id=1, source_target_pairs={{0,35},{1,0},{2,1},{3,2},{4,39},{5,4},{6,5},{7,6},{8,43},{9,8},{10... | collective-permute-start | bytes 1572872 | tf_op jit(solution)/shard_map/ppermute | solution.py:46
  35.3 1.9 %collective-permute-start.1 = (bf16[2,256,512]{2,1,0:T(8,128)(2,1)}, bf16[2,256,512]{2,1,0:T(8,128)(2,1)}, u32[]{:S(2)}, u32[]{:S(2)}) collective-permute-start(bf16[2,256,512]{2,1,0:T(8,128)(2,1)} %get-tuple-element.31), channel_id=1, source_target_pairs={{0,32},{1,33},{2,34},{3,35},{4,36},{5,37},{6,38},{7,39},{8,40},{9,... | collective-permute-start | bytes 1572872 | tf_op jit(solution)/shard_map/ppermute | solution.py:45
  37.3 1.4 collective-permute-start.8
  38.7 3.8 %collective-permute-start.5 = (bf16[2,256,1024]{2,1,0:T(8,128)(2,1)}, bf16[2,256,1024]{2,1,0:T(8,128)(2,1)}, u32[]{:S(2)}, u32[]{:S(2)}) collective-permute-start(bf16[2,256,1024]{2,1,0:T(8,128)(2,1)} %collective-permute-done.4), channel_id=1, source_target_pairs={{0,28},{4,0},{8,4},{12,8},{16,12},{20,16},{24,20},{28,24},{32,60},... | collective-permute-start | bytes 3145736 | tf_op jit(solution)/shard_map/ppermute | solution.py:21
  43.1 0.7 fusion.15
  49.0 0.6 gather_fusion
  49.6 0.8 collective-permute-done.2
  50.4 19.4 %collective-permute-start.3 = (bf16[2,256,512]{2,1,0:T(8,128)(2,1)}, bf16[2,256,512]{2,1,0:T(8,128)(2,1)}, u32[]{:S(2)}, u32[]{:S(2)}) collective-permute-start(bf16[2,256,512]{2,1,0:T(8,128)(2,1)} %collective-permute-done.2), channel_id=1, source_target_pairs={{35,32},{0,33},{1,34},{2,35},{39,36},{4,37},{5,38},{6,39},{43,40},... | collective-permute-start | bytes 1572872 | tf_op jit(solution)/shard_map/ppermute | solution.py:46
  70.5 1.5 convert_element_type.128
  72.0 1.5 convert_element_type.108
  73.5 36.1 %collective-permute-done.3 = bf16[2,256,512]{2,1,0:T(8,128)(2,1)} collective-permute-done((bf16[2,256,512]{2,1,0:T(8,128)(2,1)}, bf16[2,256,512]{2,1,0:T(8,128)(2,1)}, u32[]{:S(2)}, u32[]{:S(2)}) %collective-permute-start.3) | collective-permute-done | bytes 524320 | tf_op jit(solution)/shard_map/ppermute | solution.py:46
  109.5 1.5 maximum_convert_fusion
  111.0 1.5 convert_element_type.113
  112.5 1.5 convert_element_type.125
  113.9 4.9 %collective-permute-start.9 = (bf16[2,256,1024]{2,1,0:T(8,128)(2,1)}, bf16[2,256,1024]{2,1,0:T(8,128)(2,1)S(1)}, u32[]{:S(2)}, u32[]{:S(2)}) collective-permute-start(bf16[2,256,1024]{2,1,0:T(8,128)(2,1)} %collective-permute-done.8), channel_id=1, source_target_pairs={{0,4},{4,8},{8,12},{12,16},{16,20},{20,24},{24,28},{28,0},{32,36},... | collective-permute-start | bytes 3145736 | tf_op jit(solution)/shard_map/ppermute | solution.py:21
  118.9 1.6 add_reduce_fusion.2
  120.6 1.5 convert_element_type.116
  122.0 8.9 %collective-permute-done.9 = bf16[2,256,1024]{2,1,0:T(8,128)(2,1)S(1)} collective-permute-done((bf16[2,256,1024]{2,1,0:T(8,128)(2,1)}, bf16[2,256,1024]{2,1,0:T(8,128)(2,1)S(1)}, u32[]{:S(2)}, u32[]{:S(2)}) %collective-permute-start.9) | collective-permute-done | bytes 1048608 | tf_op jit(solution)/shard_map/ppermute | solution.py:21
  131.2 2.1 %collective-permute-done.6 = bf16[2,256,1024]{2,1,0:T(8,128)(2,1)S(1)} collective-permute-done((bf16[2,256,1024]{2,1,0:T(8,128)(2,1)}, bf16[2,256,1024]{2,1,0:T(8,128)(2,1)S(1)}, u32[]{:S(2)}, u32[]{:S(2)}) %collective-permute-start.6) | collective-permute-done | bytes 1048608 | tf_op jit(solution)/shard_map/ppermute | solution.py:21
  133.6 1.7 add_reduce_fusion.1
  135.4 0.8 fusion.1
  136.2 0.6 multiply_reduce_fusion
  137.1 41.0 %all_to_all.9 = f32[128,1,512]{2,1,0:T(1,128)S(1)} all-to-all(f32[128,1,512]{2,1,0:T(1,128)S(1)} %copy.8), channel_id=1, replica_groups=mesh['bl'=128,'ta'=4] {'bl'}, dimensions={0} | all-to-all | bytes 524288 | tf_op jit(solution)/shard_map/all_to_all | solution.py:146
  178.3 7.2 %psum.7 = f32[1,512]{1,0:T(1,128)} all-reduce(f32[1,512]{1,0:T(1,128)S(1)} %bitcast.51), channel_id=1, replica_groups=mesh['bl'=128,'ta'=4] {'ta'}, use_global_device_ids=true, to_apply=%region_17.18 | all-reduce | flops 512 | bytes 4096 | tf_op jit(solution)/shard_map/psum | solution.py:147
  (39 shorter events, 3.0 us)
Async XLA Ops:
  0.0 1.2 copy-start
  1.2 3.0 %copy-start.5 = (bf16[1024,1024]{1,0:T(8,128)(2,1)S(1)}, bf16[1024,1024]{1,0:T(8,128)(2,1)}, u32[]{:S(2)}) copy-start(bf16[1024,1024]{1,0:T(8,128)(2,1)} %constant.56.clone) | copy-start | bytes 6291460
  7.2 35.3 %copy-start.3 = (s32[8,128]{1,0:T(8,128)S(1)}, s32[8,128]{1,0:T(8,128)}, u32[]{:S(2)}) copy-start(s32[8,128]{1,0:T(8,128)} %param.11) | copy-start | bytes 12292
  7.2 41.8 %copy-start.1 = (s32[128]{0:T(128)S(1)}, s32[128]{0:T(128)}, u32[]{:S(2)}) copy-start(s32[128]{0:T(128)} %param.9) | copy-start | bytes 1540
  7.2 62.6 %copy-start.2 = (s32[128]{0:T(128)S(1)}, s32[128]{0:T(128)}, u32[]{:S(2)}) copy-start(s32[128]{0:T(128)} %param.10) | copy-start | bytes 1540
  7.2 15.7 %collective-permute-start = (bf16[2,256,1024]{2,1,0:T(8,128)(2,1)}, bf16[2,256,1024]{2,1,0:T(8,128)(2,1)}, u32[]{:S(2)}, u32[]{:S(2)}) collective-permute-start(bf16[2,256,1024]{2,1,0:T(8,128)(2,1)} %get-tuple-element.30), channel_id=1, source_target_pairs={{0,28},{4,0},{8,4},{12,8},{16,12},{20,16},{24,20},{28,24},{32,60},... | collective-permute-start | bytes 3145736 | tf_op jit(solution)/shard_map/ppermute | solution.py:21
  14.1 23.2 %collective-permute-start.7 = (bf16[2,256,1024]{2,1,0:T(8,128)(2,1)}, bf16[2,256,1024]{2,1,0:T(8,128)(2,1)}, u32[]{:S(2)}, u32[]{:S(2)}) collective-permute-start(bf16[2,256,1024]{2,1,0:T(8,128)(2,1)} %get-tuple-element.30), channel_id=1, source_target_pairs={{0,4},{4,8},{8,12},{12,16},{16,20},{20,24},{24,28},{28,0},{32,36},... | collective-permute-start | bytes 3145736 | tf_op jit(solution)/shard_map/ppermute | solution.py:21
  22.9 15.8 %collective-permute-start.4 = (bf16[2,256,1024]{2,1,0:T(8,128)(2,1)}, bf16[2,256,1024]{2,1,0:T(8,128)(2,1)}, u32[]{:S(2)}, u32[]{:S(2)}) collective-permute-start(bf16[2,256,1024]{2,1,0:T(8,128)(2,1)} %collective-permute-done), channel_id=1, source_target_pairs={{0,28},{4,0},{8,4},{12,8},{16,12},{20,16},{24,20},{28,24},{32,60},... | collective-permute-start | bytes 3145736 | tf_op jit(solution)/shard_map/ppermute | solution.py:21
  27.9 22.6 %collective-permute-start.2 = (bf16[2,256,512]{2,1,0:T(8,128)(2,1)}, bf16[2,256,512]{2,1,0:T(8,128)(2,1)}, u32[]{:S(2)}, u32[]{:S(2)}) collective-permute-start(bf16[2,256,512]{2,1,0:T(8,128)(2,1)} %get-tuple-element.32), channel_id=1, source_target_pairs={{0,35},{1,0},{2,1},{3,2},{4,39},{5,4},{6,5},{7,6},{8,43},{9,8},{10... | collective-permute-start | bytes 1572872 | tf_op jit(solution)/shard_map/ppermute | solution.py:46
  35.3 38.1 %collective-permute-start.1 = (bf16[2,256,512]{2,1,0:T(8,128)(2,1)}, bf16[2,256,512]{2,1,0:T(8,128)(2,1)}, u32[]{:S(2)}, u32[]{:S(2)}) collective-permute-start(bf16[2,256,512]{2,1,0:T(8,128)(2,1)} %get-tuple-element.31), channel_id=1, source_target_pairs={{0,32},{1,33},{2,34},{3,35},{4,36},{5,37},{6,38},{7,39},{8,40},{9,... | collective-permute-start | bytes 1572872 | tf_op jit(solution)/shard_map/ppermute | solution.py:45
  37.3 75.2 %collective-permute-start.8 = (bf16[2,256,1024]{2,1,0:T(8,128)(2,1)}, bf16[2,256,1024]{2,1,0:T(8,128)(2,1)}, u32[]{:S(2)}, u32[]{:S(2)}) collective-permute-start(bf16[2,256,1024]{2,1,0:T(8,128)(2,1)} %collective-permute-done.7), channel_id=1, source_target_pairs={{0,4},{4,8},{8,12},{12,16},{16,20},{20,24},{24,28},{28,0},{32,36},... | collective-permute-start | bytes 3145736 | tf_op jit(solution)/shard_map/ppermute | solution.py:21
  38.7 80.2 %collective-permute-start.5 = (bf16[2,256,1024]{2,1,0:T(8,128)(2,1)}, bf16[2,256,1024]{2,1,0:T(8,128)(2,1)}, u32[]{:S(2)}, u32[]{:S(2)}) collective-permute-start(bf16[2,256,1024]{2,1,0:T(8,128)(2,1)} %collective-permute-done.4), channel_id=1, source_target_pairs={{0,28},{4,0},{8,4},{12,8},{16,12},{20,16},{24,20},{28,24},{32,60},... | collective-permute-start | bytes 3145736 | tf_op jit(solution)/shard_map/ppermute | solution.py:21
  50.4 59.1 %collective-permute-start.3 = (bf16[2,256,512]{2,1,0:T(8,128)(2,1)}, bf16[2,256,512]{2,1,0:T(8,128)(2,1)}, u32[]{:S(2)}, u32[]{:S(2)}) collective-permute-start(bf16[2,256,512]{2,1,0:T(8,128)(2,1)} %collective-permute-done.2), channel_id=1, source_target_pairs={{35,32},{0,33},{1,34},{2,35},{39,36},{4,37},{5,38},{6,39},{43,40},... | collective-permute-start | bytes 1572872 | tf_op jit(solution)/shard_map/ppermute | solution.py:46
  113.9 17.0 %collective-permute-start.9 = (bf16[2,256,1024]{2,1,0:T(8,128)(2,1)}, bf16[2,256,1024]{2,1,0:T(8,128)(2,1)S(1)}, u32[]{:S(2)}, u32[]{:S(2)}) collective-permute-start(bf16[2,256,1024]{2,1,0:T(8,128)(2,1)} %collective-permute-done.8), channel_id=1, source_target_pairs={{0,4},{4,8},{8,12},{12,16},{16,20},{20,24},{24,28},{28,0},{32,36},... | collective-permute-start | bytes 3145736 | tf_op jit(solution)/shard_map/ppermute | solution.py:21
  118.9 14.4 %collective-permute-start.6 = (bf16[2,256,1024]{2,1,0:T(8,128)(2,1)}, bf16[2,256,1024]{2,1,0:T(8,128)(2,1)S(1)}, u32[]{:S(2)}, u32[]{:S(2)}) collective-permute-start(bf16[2,256,1024]{2,1,0:T(8,128)(2,1)} %collective-permute-done.5), channel_id=1, source_target_pairs={{0,28},{4,0},{8,4},{12,8},{16,12},{20,16},{24,20},{28,24},{32,60},... | collective-permute-start | bytes 3145736 | tf_op jit(solution)/shard_map/ppermute | solution.py:21
  133.6 1.8 copy-start.4

commit v7 on v5

--- a/solution.py
+++ b/solution.py
@@ -81,7 +81,9 @@
     num_blocks = lax.axis_size("bl")
     group = cycle_len
     position = my_block % group
-    below_group = shifted(spectra, "bl", group)
+    split = num_chans // 2
+    below_low = shifted(spectra[:, :, :split], "bl", group)
+    below_high = shifted(spectra[:, :, split:], "bl", group)
     ahead = [spectra]
     behind = [spectra]
     for _ in range(group // 2):
@@ -100,15 +102,18 @@
             held_blocks.append(ahead[offset])
         else:
             held_blocks.append(behind[group - offset])
-    inner_power = lax.optimization_barrier(
-        [cross_power(held, spectra) for held in held_blocks[:-1]]
-    )
-    below_group, ahead[3], behind[3] = lax.optimization_barrier((below_group, ahead[3], behind[3]))
+    below_low, ahead[2] = lax.optimization_barrier((below_low, ahead[2]))
+    low_power = [cross_power(held[:, :, :split], below_low) for held in held_blocks]
+    below_high, ahead[4] = lax.optimization_barrier((below_high, ahead[4]))
     power_rows = []
     for offset in range(1, cycle_len + 1):
-        pair_power = cross_power(held_blocks[offset - 1], below_group)
+        held = held_blocks[offset - 1]
+        high = cross_power(held[:, :, split:], below_high)
+        pair_power = jnp.concatenate([low_power[offset - 1], high])
         if offset < group:
-            pair_power = jnp.where(position + offset < group, inner_power[offset - 1], pair_power)
+            pair_power = jnp.where(
+                position + offset < group, cross_power(held, spectra), pair_power
+            )
         power_rows.append(flags[offset - 1].astype(jnp.float32) * pair_power)
     power_table = jnp.stack(power_rows)
     k_onehot = (delay_kbin[:, None] == jnp.arange(num_kbins, dtype=jnp.int32)[None, :]).astype(

time: 155 us -> 159 us (1.026)
  other arithmetic: 16.6 us -> 24.6 us
  blocking collectives: 50.9 us -> 46 us
  starting transfers between devices: 27.3 us -> 31.8 us
  waiting for transfers between devices: 43.7 us -> 39.9 us
    convert_element_type x7 -> x15, other arithmetic: 9.09 us -> 14.7 us  [cross_power(): own_f = own_block.astype(jnp.float32)]
    all_to_all x1, blocking collectives: 39.3 us -> 34.6 us  [per_device(): received = lax.all_to_all(partial_table, 'bl', 0, 0, tiled=True)]
    ppermute x1 -> x2, waiting for transfers between devices: 25.1 us -> 21.3 us  [shifted(): return lax.ppermute(block, axis, route)]
    ppermute x7, starting transfers between devices: 19.8 us -> 22.4 us  [group_shifted(): return lax.ppermute(block, axis, route)]
    ppermute x1 -> x2, starting transfers between devices: 7.45 us -> 9.37 us  [shifted(): return lax.ppermute(block, axis, route)]
    reduce_sum x2 -> x5, other arithmetic: 3.3 us -> 4.83 us  [cross_power(): return jnp.sum(own_f[0] * other_f[0] + own_f[1] * other_f[1], axis=0)]
    convert_element_type x2 -> x3, other arithmetic: 2.65 us -> 3.54 us  [cross_power(): other_f = other_block.astype(jnp.float32)]
  transfers between devices with their start and end apart: 8 -> 9, of which waited for: 3 -> 3; matrix products, arithmetic and copies ran while one was open for 9% -> 12% of each run, Pallas kernels for 0% -> 0%
where the time goes in v7:
time: 159 us; the launch traced here: 157 us
  blocking collectives  46 us (29%)
  waiting for transfers between devices  39.9 us (25%)
  starting transfers between devices  31.8 us (20%)
  other arithmetic  24.6 us (15%)
  between operations  5.42 us (3%)
  matrix products  5.04 us (3%)
  local copies, waits for them, and re-layouts  4.73 us (3%)
    all_to_all x1, blocking collectives, per_device(): received = lax.all_to_all(partial_table, 'bl', 0, 0, tiled=True)  34.6 us
    ppermute x7, starting transfers between devices, group_shifted(): return lax.ppermute(block, axis, route)  22.4 us
    ppermute x2, waiting for transfers between devices, shifted(): return lax.ppermute(block, axis, route)  21.3 us
    ppermute x7, waiting for transfers between devices, group_shifted(): return lax.ppermute(block, axis, route)  18.6 us
    convert_element_type x15, other arithmetic, cross_power(): own_f = own_block.astype(jnp.float32)  14.7 us
    psum x1, blocking collectives, per_device(): return lax.psum(jnp.sum(received, axis=0, keepdims=True), 'ta')  11.4 us
    ppermute x2, starting transfers between devices, shifted(): return lax.ppermute(block, axis, route)  9.37 us
    reduce_sum x5, other arithmetic, cross_power(): return jnp.sum(own_f[0] * other_f[0] + own_f[1] * other_f[1], axis=0)  4.83 us
  transfers between devices with their start and end apart: 9, of which 3 were waited for; matrix products, arithmetic and copies ran while one was open for 12% of the time, Pallas kernels for 0%

profile of v7, /device:TPU:1, one launch (start us, length us, event | category | flops | bytes accessed | tf_op | source)
XLA Modules:
  0.0 157.5 jit_solution(3551106791772360539)
XLA Ops:
  0.0 1.2 copy-done
  1.2 3.0 %convolution_bitcast_fusion = f32[512,1024]{1,0:T(8,128)S(1)} fusion(bf16[512,1024]{1,0:T(8,128)(2,1)S(1)} %bitcast.55, bf16[1024,1024]{1,0:T(8,128)(2,1)} %constant.57.clone), kind=kOutput, calls=%fused_computation.6 | convolution fusion | flops 1073741824 | bytes 5242880 | tf_op jit(solution)/shard_map/dot_general | solution.py:55
  4.2 1.3 convolution_bitcast_fusion.1
  6.0 1.2 fusion.67
  7.3 6.9 %collective-permute-start = (bf16[2,256,1024]{2,1,0:T(8,128)(2,1)}, bf16[2,256,1024]{2,1,0:T(8,128)(2,1)}, u32[]{:S(2)}, u32[]{:S(2)}) collective-permute-start(bf16[2,256,1024]{2,1,0:T(8,128)(2,1)} %get-tuple-element.58), channel_id=1, source_target_pairs={{0,28},{4,0},{8,4},{12,8},{16,12},{20,16},{24,20},{28,24},{32,60},... | collective-permute-start | bytes 3145736 | tf_op jit(solution)/shard_map/ppermute | solution.py:21
  14.1 8.8 %collective-permute-done = bf16[2,256,1024]{2,1,0:T(8,128)(2,1)} collective-permute-done((bf16[2,256,1024]{2,1,0:T(8,128)(2,1)}, bf16[2,256,1024]{2,1,0:T(8,128)(2,1)}, u32[]{:S(2)}, u32[]{:S(2)}) %collective-permute-start) | collective-permute-done | bytes 1048608 | tf_op jit(solution)/shard_map/ppermute | solution.py:21
  22.9 3.8 %collective-permute-start.2 = (bf16[2,256,1024]{2,1,0:T(8,128)(2,1)}, bf16[2,256,1024]{2,1,0:T(8,128)(2,1)}, u32[]{:S(2)}, u32[]{:S(2)}) collective-permute-start(bf16[2,256,1024]{2,1,0:T(8,128)(2,1)} %collective-permute-done), channel_id=1, source_target_pairs={{0,28},{4,0},{8,4},{12,8},{16,12},{20,16},{24,20},{28,24},{32,60},... | collective-permute-start | bytes 3145736 | tf_op jit(solution)/shard_map/ppermute | solution.py:21
  26.8 1.8 %fusion.68 = (f32[2,256,512]{2,1,0:T(8,128)}, bf16[2,256,512]{2,1,0:T(8,128)(2,1)}, f32[2,256,512]{2,1,0:T(8,128)}, bf16[2,256,512]{2,1,0:T(8,128)(2,1)}) fusion(bf16[1,256,1024]{2,1,0:T(8,128)(2,1)S(1)} %get-tuple-element.37, bf16[1,256,1024]{2,1,0:T(8,128)(2,1)S(1)} %get-tuple-element.36), kind=kLoop, calls=%fused_computation.159 | loop fusion | flops 1048576 | bytes 4194304 | tf_op jit(solution)/shard_map/convert_element_type | solution.py:64
  28.6 7.4 %collective-permute-start.3 = (bf16[2,256,512]{2,1,0:T(8,128)(2,1)}, bf16[2,256,512]{2,1,0:T(8,128)(2,1)}, u32[]{:S(2)}, u32[]{:S(2)}) collective-permute-start(bf16[2,256,512]{2,1,0:T(8,128)(2,1)} %get-tuple-element.54), channel_id=1, source_target_pairs={{480,0},{484,4},{488,8},{492,12},{496,16},{500,20},{504,24},{508,2... | collective-permute-start | bytes 1572872 | tf_op jit(solution)/shard_map/ppermute | solution.py:15
  36.0 1.9 %collective-permute-start.1 = (bf16[2,256,512]{2,1,0:T(8,128)(2,1)}, bf16[2,256,512]{2,1,0:T(8,128)(2,1)}, u32[]{:S(2)}, u32[]{:S(2)}) collective-permute-start(bf16[2,256,512]{2,1,0:T(8,128)(2,1)} %get-tuple-element.33), channel_id=1, source_target_pairs={{480,0},{484,4},{488,8},{492,12},{496,16},{500,20},{504,24},{508,2... | collective-permute-start | bytes 1572872 | tf_op jit(solution)/shard_map/ppermute | solution.py:15
  38.6 1.4 collective-permute-start.7
  40.0 0.7 fusion.72
  47.1 2.0 %collective-permute-start.4 = (bf16[2,256,1024]{2,1,0:T(8,128)(2,1)}, bf16[2,256,1024]{2,1,0:T(8,128)(2,1)S(1)}, u32[]{:S(2)}, u32[]{:S(2)}) collective-permute-start(bf16[2,256,1024]{2,1,0:T(8,128)(2,1)} %collective-permute-done.2), channel_id=1, source_target_pairs={{0,28},{4,0},{8,4},{12,8},{16,12},{20,16},{24,20},{28,24},{32,60},... | collective-permute-start | bytes 3145736 | tf_op jit(solution)/shard_map/ppermute | solution.py:21
  49.1 1.5 convert_element_type.158
  50.6 1.5 convert_element_type.191
  52.0 1.4 slice_convert_fusion.13
  53.4 1.1 collective-permute-start.8
  54.6 1.4 slice_convert_fusion.1
  55.9 21.3 %collective-permute-done.1 = bf16[2,256,512]{2,1,0:T(8,128)(2,1)} collective-permute-done((bf16[2,256,512]{2,1,0:T(8,128)(2,1)}, bf16[2,256,512]{2,1,0:T(8,128)(2,1)}, u32[]{:S(2)}, u32[]{:S(2)}) %collective-permute-start.1) | collective-permute-done | bytes 524320 | tf_op jit(solution)/shard_map/ppermute | solution.py:15
  77.2 1.2 convert_element_type.161
  78.4 1.5 convert_element_type.166
  79.8 1.5 convert_element_type.186
  81.3 1.4 slice_convert_fusion.11
  82.7 7.2 %collective-permute-start.5 = (bf16[2,256,1024]{2,1,0:T(8,128)(2,1)S(1)}, bf16[2,256,1024]{2,1,0:T(8,128)(2,1)S(1)}, u32[]{:S(2)}, u32[]{:S(2)}) collective-permute-start(bf16[2,256,1024]{2,1,0:T(8,128)(2,1)S(1)} %collective-permute-done.4), channel_id=1, source_target_pairs={{0,28},{4,0},{8,4},{12,8},{16,12},{20,16},{24,20},{28,24},{32,60},... | collective-permute-start | bytes 3145736 | tf_op jit(solution)/shard_map/ppermute | solution.py:21
  89.9 1.4 slice_convert_fusion.3
  93.0 9.8 %collective-permute-done.5 = bf16[2,256,1024]{2,1,0:T(8,128)(2,1)S(1)} collective-permute-done((bf16[2,256,1024]{2,1,0:T(8,128)(2,1)S(1)}, bf16[2,256,1024]{2,1,0:T(8,128)(2,1)S(1)}, u32[]{:S(2)}, u32[]{:S(2)}) %collective-permute-start.5) | collective-permute-done | bytes 1048608 | tf_op jit(solution)/shard_map/ppermute | solution.py:21
  102.8 1.2 convert_element_type.163
  106.2 0.7 fusion.28
  107.1 2.2 %fusion.3 = (f32[1024]{0:T(1024)S(1)}, f32[1024]{0:T(1024)S(1)}, f32[1024]{0:T(1024)S(1)}, f32[1024]{0:T(1024)S(1)}, f32[1024]{0:T(1024)S(1)}, /*index=5*/f32[1024]{0:T(1024)S(1)}, f32[1024]{0:T(1024)S(1)}) fusion(f32[2,256,1024]{2,1,0:T(8,128)S(1)} %convert_element_type.191, f32[2,256,1024]{2,1,0:T(8,128)S(1)} %get-tuple-element.57, ...), kind=kLoop, calls=%fused_computation.16 | loop fusion | flops 7332864 | bytes 16805888 | tf_op jit(solution)/shard_map/reduce_sum | solution.py:66
  109.5 0.8 fusion.1
  111.2 34.6 %all_to_all.9 = f32[128,1,512]{2,1,0:T(1,128)S(1)} all-to-all(f32[128,1,512]{2,1,0:T(1,128)S(1)} %copy.8), channel_id=1, replica_groups=mesh['bl'=128,'ta'=4] {'bl'}, dimensions={0} | all-to-all | bytes 524288 | tf_op jit(solution)/shard_map/all_to_all | solution.py:129
  146.0 11.4 %psum.7 = f32[1,512]{1,0:T(1,128)} all-reduce(f32[1,512]{1,0:T(1,128)S(1)} %bitcast.81), channel_id=1, replica_groups=mesh['bl'=128,'ta'=4] {'ta'}, use_global_device_ids=true, to_apply=%region_25.26 | all-reduce | flops 512 | bytes 4096 | tf_op jit(solution)/shard_map/psum | solution.py:130
  (52 shorter events, 8.0 us)
Async XLA Ops:
  0.0 1.2 copy-start
  1.2 3.0 %copy-start.7 = (bf16[1024,1024]{1,0:T(8,128)(2,1)S(1)}, bf16[1024,1024]{1,0:T(8,128)(2,1)}, u32[]{:S(2)}) copy-start(bf16[1024,1024]{1,0:T(8,128)(2,1)} %constant.56.clone) | copy-start | bytes 6291460
  7.2 30.7 %copy-start.3 = (s32[8,128]{1,0:T(8,128)S(1)}, s32[8,128]{1,0:T(8,128)}, u32[]{:S(2)}) copy-start(s32[8,128]{1,0:T(8,128)} %param.11) | copy-start | bytes 12292
  7.3 38.5 %copy-start.1 = (s32[128]{0:T(128)S(1)}, s32[128]{0:T(128)}, u32[]{:S(2)}) copy-start(s32[128]{0:T(128)} %param.9) | copy-start | bytes 1540
  7.3 39.1 %copy-start.2 = (s32[128]{0:T(128)S(1)}, s32[128]{0:T(128)}, u32[]{:S(2)}) copy-start(s32[128]{0:T(128)} %param.10) | copy-start | bytes 1540
  7.3 15.7 %collective-permute-start = (bf16[2,256,1024]{2,1,0:T(8,128)(2,1)}, bf16[2,256,1024]{2,1,0:T(8,128)(2,1)}, u32[]{:S(2)}, u32[]{:S(2)}) collective-permute-start(bf16[2,256,1024]{2,1,0:T(8,128)(2,1)} %get-tuple-element.58), channel_id=1, source_target_pairs={{0,28},{4,0},{8,4},{12,8},{16,12},{20,16},{24,20},{28,24},{32,60},... | collective-permute-start | bytes 3145736 | tf_op jit(solution)/shard_map/ppermute | solution.py:21
  14.1 24.5 %collective-permute-start.6 = (bf16[2,256,1024]{2,1,0:T(8,128)(2,1)}, bf16[2,256,1024]{2,1,0:T(8,128)(2,1)}, u32[]{:S(2)}, u32[]{:S(2)}) collective-permute-start(bf16[2,256,1024]{2,1,0:T(8,128)(2,1)} %get-tuple-element.58), channel_id=1, source_target_pairs={{0,4},{4,8},{8,12},{12,16},{16,20},{20,24},{24,28},{28,0},{32,36},... | collective-permute-start | bytes 3145736 | tf_op jit(solution)/shard_map/ppermute | solution.py:21
  22.9 24.1 %collective-permute-start.2 = (bf16[2,256,1024]{2,1,0:T(8,128)(2,1)}, bf16[2,256,1024]{2,1,0:T(8,128)(2,1)}, u32[]{:S(2)}, u32[]{:S(2)}) collective-permute-start(bf16[2,256,1024]{2,1,0:T(8,128)(2,1)} %collective-permute-done), channel_id=1, source_target_pairs={{0,28},{4,0},{8,4},{12,8},{16,12},{20,16},{24,20},{28,24},{32,60},... | collective-permute-start | bytes 3145736 | tf_op jit(solution)/shard_map/ppermute | solution.py:21
  28.6 64.4 %collective-permute-start.3 = (bf16[2,256,512]{2,1,0:T(8,128)(2,1)}, bf16[2,256,512]{2,1,0:T(8,128)(2,1)}, u32[]{:S(2)}, u32[]{:S(2)}) collective-permute-start(bf16[2,256,512]{2,1,0:T(8,128)(2,1)} %get-tuple-element.54), channel_id=1, source_target_pairs={{480,0},{484,4},{488,8},{492,12},{496,16},{500,20},{504,24},{508,2... | collective-permute-start | bytes 1572872 | tf_op jit(solution)/shard_map/ppermute | solution.py:15
  36.0 41.2 %collective-permute-start.1 = (bf16[2,256,512]{2,1,0:T(8,128)(2,1)}, bf16[2,256,512]{2,1,0:T(8,128)(2,1)}, u32[]{:S(2)}, u32[]{:S(2)}) collective-permute-start(bf16[2,256,512]{2,1,0:T(8,128)(2,1)} %get-tuple-element.33), channel_id=1, source_target_pairs={{480,0},{484,4},{488,8},{492,12},{496,16},{500,20},{504,24},{508,2... | collective-permute-start | bytes 1572872 | tf_op jit(solution)/shard_map/ppermute | solution.py:15
  38.6 14.8 %collective-permute-start.7 = (bf16[2,256,1024]{2,1,0:T(8,128)(2,1)}, bf16[2,256,1024]{2,1,0:T(8,128)(2,1)}, u32[]{:S(2)}, u32[]{:S(2)}) collective-permute-start(bf16[2,256,1024]{2,1,0:T(8,128)(2,1)} %collective-permute-done.6), channel_id=1, source_target_pairs={{0,4},{4,8},{8,12},{12,16},{16,20},{20,24},{24,28},{28,0},{32,36},... | collective-permute-start | bytes 3145736 | tf_op jit(solution)/shard_map/ppermute | solution.py:21
  47.1 35.6 %collective-permute-start.4 = (bf16[2,256,1024]{2,1,0:T(8,128)(2,1)}, bf16[2,256,1024]{2,1,0:T(8,128)(2,1)S(1)}, u32[]{:S(2)}, u32[]{:S(2)}) collective-permute-start(bf16[2,256,1024]{2,1,0:T(8,128)(2,1)} %collective-permute-done.2), channel_id=1, source_target_pairs={{0,28},{4,0},{8,4},{12,8},{16,12},{20,16},{24,20},{28,24},{32,60},... | collective-permute-start | bytes 3145736 | tf_op jit(solution)/shard_map/ppermute | solution.py:21
  53.4 38.7 %collective-permute-start.8 = (bf16[2,256,1024]{2,1,0:T(8,128)(2,1)}, bf16[2,256,1024]{2,1,0:T(8,128)(2,1)S(1)}, u32[]{:S(2)}, u32[]{:S(2)}) collective-permute-start(bf16[2,256,1024]{2,1,0:T(8,128)(2,1)} %collective-permute-done.7), channel_id=1, source_target_pairs={{0,4},{4,8},{8,12},{12,16},{16,20},{20,24},{24,28},{28,0},{32,36},... | collective-permute-start | bytes 3145736 | tf_op jit(solution)/shard_map/ppermute | solution.py:21
  82.7 20.1 %collective-permute-start.5 = (bf16[2,256,1024]{2,1,0:T(8,128)(2,1)S(1)}, bf16[2,256,1024]{2,1,0:T(8,128)(2,1)S(1)}, u32[]{:S(2)}, u32[]{:S(2)}) collective-permute-start(bf16[2,256,1024]{2,1,0:T(8,128)(2,1)S(1)} %collective-permute-done.4), channel_id=1, source_target_pairs={{0,28},{4,0},{8,4},{12,8},{16,12},{20,16},{24,20},{28,24},{32,60},... | collective-permute-start | bytes 3145736 | tf_op jit(solution)/shard_map/ppermute | solution.py:21
  93.0 11.3 %copy-start.5 = (f32[2,256,512]{2,1,0:T(8,128)S(1)}, f32[2,256,512]{2,1,0:T(8,128)}, u32[]{:S(2)}) copy-start(f32[2,256,512]{2,1,0:T(8,128)} %get-tuple-element.32) | copy-start | bytes 3145732
  104.3 1.2 copy-start.4
  107.1 2.4 %copy-start.6 = (s32[1024]{0:T(1024)S(1)}, s32[1024]{0:T(1024)}, u32[]{:S(2)}) copy-start(s32[1024]{0:T(1024)} %param.8) | copy-start | bytes 12292

commit v8 on v2

--- a/solution.py
+++ b/solution.py
@@ -86,7 +86,9 @@
     behind = [spectra]
     for _ in range(group // 2):
         ahead.append(group_shifted(ahead[-1], "bl", group, -1))
-    for _ in range(group - 1 - group // 2):
+    for step in range(group - 1 - group // 2):
+        if step == 1:
+            below_group, behind[-1] = lax.optimization_barrier((below_group, behind[-1]))
         behind.append(group_shifted(behind[-1], "bl", group, 1))
     offsets = jnp.arange(1, cycle_len + 1, dtype=jnp.int32)
     partner_pos = (position + offsets) % group

time: 153 us -> 148 us (0.967)
  starting transfers between devices: 31.7 us -> 24.2 us
  waiting for transfers between devices: 45.7 us -> 49.7 us
  other arithmetic: 14.1 us -> 11.9 us
    ppermute x1, waiting for transfers between devices: 23.9 us -> 38.2 us  [shifted(): return lax.ppermute(block, axis, route)]
    ppermute x7, waiting for transfers between devices: 21.8 us -> 11.5 us  [group_shifted(): return lax.ppermute(block, axis, route)]
    ppermute x7, starting transfers between devices: 24.3 us -> 18.9 us  [group_shifted(): return lax.ppermute(block, axis, route)]
    convert_element_type x2, other arithmetic: 2.64 us -> 0.44 us  [cross_power(): other_f = other_block.astype(jnp.float32)]
    ppermute x1, starting transfers between devices: 7.45 us -> 5.25 us  [shifted(): return lax.ppermute(block, axis, route)]
    unnamed x16 -> x20, local copies, waits for them, and re-layouts: 2.26 us -> 3.21 us
  transfers between devices with their start and end apart: 8 -> 8, of which waited for: 5 -> 4; matrix products, arithmetic and copies ran while one was open for 8% -> 7% of each run, Pallas kernels for 0% -> 0%
where the time goes in v8:
time: 148 us
  waiting for transfers between devices  49.7 us (34%)
  blocking collectives  45.2 us (31%)
  starting transfers between devices  24.2 us (16%)
  other arithmetic  11.9 us (8%)
  local copies, waits for them, and re-layouts  6.15 us (4%)
  between operations  5.34 us (4%)
  matrix products  5.04 us (3%)
    ppermute x1, waiting for transfers between devices, shifted(): return lax.ppermute(block, axis, route)  38.2 us
    all_to_all x1, blocking collectives, per_device(): received = lax.all_to_all(partial_table, 'bl', 0, 0, tiled=True)  33.6 us
    ppermute x7, starting transfers between devices, group_shifted(): return lax.ppermute(block, axis, route)  18.9 us
    psum x1, blocking collectives, per_device(): return lax.psum(jnp.sum(received, axis=0, keepdims=True), 'ta')  11.6 us
    ppermute x7, waiting for transfers between devices, group_shifted(): return lax.ppermute(block, axis, route)  11.5 us
    convert_element_type x7, other arithmetic, cross_power(): own_f = own_block.astype(jnp.float32)  6.62 us
    ppermute x1, starting transfers between devices, shifted(): return lax.ppermute(block, axis, route)  5.25 us
    reduce_sum x2, other arithmetic, cross_power(): return jnp.sum(own_f[0] * other_f[0] + own_f[1] * other_f[1], axis=0)  3.29 us
  transfers between devices with their start and end apart: 8, of which 4 were waited for; matrix products, arithmetic and copies ran while one was open for 7% of the time, Pallas kernels for 0%

profile of v8, /device:TPU:1, one launch (start us, length us, event | category | flops | bytes accessed | tf_op | source)
XLA Modules:
  0.0 147.6 jit_solution(4630944650906577365)
XLA Ops:
  0.0 1.2 copy-done
  1.2 3.0 %convolution_bitcast_fusion = f32[512,1024]{1,0:T(8,128)S(1)} fusion(bf16[512,1024]{1,0:T(8,128)(2,1)S(1)} %bitcast.40, bf16[1024,1024]{1,0:T(8,128)(2,1)} %constant.57.clone), kind=kOutput, calls=%fused_computation.6 | convolution fusion | flops 1073741824 | bytes 5242880 | tf_op jit(solution)/shard_map/dot_general | solution.py:55
  4.2 1.3 convolution_bitcast_fusion.1
  5.5 0.5 fusion.5
  6.3 6.9 %collective-permute-start = (bf16[2,256,1024]{2,1,0:T(8,128)(2,1)S(1)}, bf16[2,256,1024]{2,1,0:T(8,128)(2,1)S(1)}, u32[]{:S(2)}, u32[]{:S(2)}) collective-permute-start(bf16[2,256,1024]{2,1,0:T(8,128)(2,1)S(1)} %get-tuple-element.34), channel_id=1, source_target_pairs={{0,28},{4,0},{8,4},{12,8},{16,12},{20,16},{24,20},{28,24},{32,60},... | collective-permute-start | bytes 3145736 | tf_op jit(solution)/shard_map/ppermute | solution.py:21
  13.2 5.2 %collective-permute-start.1 = (bf16[2,256,1024]{2,1,0:T(8,128)(2,1)S(1)}, bf16[2,256,1024]{2,1,0:T(8,128)(2,1)S(1)}, u32[]{:S(2)}, u32[]{:S(2)}) collective-permute-start(bf16[2,256,1024]{2,1,0:T(8,128)(2,1)S(1)} %get-tuple-element.34), channel_id=1, source_target_pairs={{480,0},{484,4},{488,8},{492,12},{496,16},{500,20},{504,24},{508,2... | collective-permute-start | bytes 3145736 | tf_op jit(solution)/shard_map/ppermute | solution.py:15
  18.4 1.4 collective-permute-start.2
  19.8 1.5 %collective-permute-done = bf16[2,256,1024]{2,1,0:T(8,128)(2,1)S(1)} collective-permute-done((bf16[2,256,1024]{2,1,0:T(8,128)(2,1)S(1)}, bf16[2,256,1024]{2,1,0:T(8,128)(2,1)S(1)}, u32[]{:S(2)}, u32[]{:S(2)}) %collective-permute-start) | collective-permute-done | bytes 1048608 | tf_op jit(solution)/shard_map/ppermute | solution.py:21
  21.4 1.0 copy-done.4
  22.4 4.1 %collective-permute-start.3 = (bf16[2,256,1024]{2,1,0:T(8,128)(2,1)S(1)}, bf16[2,256,1024]{2,1,0:T(8,128)(2,1)}, u32[]{:S(2)}, u32[]{:S(2)}) collective-permute-start(bf16[2,256,1024]{2,1,0:T(8,128)(2,1)S(1)} %collective-permute-done), channel_id=1, source_target_pairs={{0,28},{4,0},{8,4},{12,8},{16,12},{20,16},{24,20},{28,24},{32,60},... | collective-permute-start | bytes 3145736 | tf_op jit(solution)/shard_map/ppermute | solution.py:21
  26.5 38.2 %collective-permute-done.1 = bf16[2,256,1024]{2,1,0:T(8,128)(2,1)S(1)} collective-permute-done((bf16[2,256,1024]{2,1,0:T(8,128)(2,1)S(1)}, bf16[2,256,1024]{2,1,0:T(8,128)(2,1)S(1)}, u32[]{:S(2)}, u32[]{:S(2)}) %collective-permute-start.1) | collective-permute-done | bytes 1048608 | tf_op jit(solution)/shard_map/ppermute | solution.py:15
  64.7 2.8 %collective-permute-start.6 = (bf16[2,256,1024]{2,1,0:T(8,128)(2,1)}, bf16[2,256,1024]{2,1,0:T(8,128)(2,1)}, u32[]{:S(2)}, u32[]{:S(2)}) collective-permute-start(bf16[2,256,1024]{2,1,0:T(8,128)(2,1)} %collective-permute-done.2), channel_id=1, source_target_pairs={{0,4},{4,8},{8,12},{12,16},{16,20},{20,24},{24,28},{28,0},{32,36},... | collective-permute-start | bytes 3145736 | tf_op jit(solution)/shard_map/ppermute | solution.py:21
  67.6 1.1 collective-permute-start.4
  68.7 0.6 gather_fusion.2
  69.4 0.7 fusion.13
  75.1 0.6 gather_fusion
  75.8 0.6 gather_fusion.1
  76.4 1.5 %convert_element_type.128 = f32[2,256,1024]{2,1,0:T(8,128)S(1)} convert(bf16[2,256,1024]{2,1,0:T(8,128)(2,1)} %collective-permute-done.2) | non-fusion elementwise | flops 524288 | bytes 3145728 | tf_op jit(solution)/shard_map/convert_element_type | solution.py:64
  78.3 1.0 copy-done.5
  79.5 1.5 convert_element_type.113
  81.0 1.5 convert_element_type.125
  82.4 1.2 collective-permute-start.7
  83.6 1.4 collective-permute-start.5
  85.0 1.6 %add_reduce_fusion.2 = (f32[1024]{0:T(1024)S(1)}, f32[1024]{0:T(1024)S(1)}, f32[1024]{0:T(1024)S(1)}, f32[1024]{0:T(1024)S(1)}, f32[1024]{0:T(1024)S(1)}, /*index=5*/f32[1024]{0:T(1024)S(1)}, f32[1024]{0:T(1024)S(1)}) fusion(f32[2,256,1024]{2,1,0:T(8,128)S(1)} %convert_element_type.128, f32[2,256,1024]{2,1,0:T(8,128)S(1)} %get-tuple-element.33, ...), kind=kLoop, calls=%fused_computation.17 | loop fusion | flops 7332864 | bytes 12611584 | tf_op jit(solution)/shard_map/reduce_sum | solution.py:66
  86.6 1.5 convert_element_type.116
  88.1 7.5 %collective-permute-done.7 = bf16[2,256,1024]{2,1,0:T(8,128)(2,1)S(1)} collective-permute-done((bf16[2,256,1024]{2,1,0:T(8,128)(2,1)}, bf16[2,256,1024]{2,1,0:T(8,128)(2,1)S(1)}, u32[]{:S(2)}, u32[]{:S(2)}) %collective-permute-start.7) | collective-permute-done | bytes 1048608 | tf_op jit(solution)/shard_map/ppermute | solution.py:21
  95.9 2.4 %collective-permute-done.5 = bf16[2,256,1024]{2,1,0:T(8,128)(2,1)S(1)} collective-permute-done((bf16[2,256,1024]{2,1,0:T(8,128)(2,1)}, bf16[2,256,1024]{2,1,0:T(8,128)(2,1)S(1)}, u32[]{:S(2)}, u32[]{:S(2)}) %collective-permute-start.5) | collective-permute-done | bytes 1048608 | tf_op jit(solution)/shard_map/ppermute | solution.py:21
  98.6 1.7 %add_reduce_fusion.1 = (f32[1024]{0:T(1024)S(1)}, f32[1024]{0:T(1024)S(1)}, f32[1024]{0:T(1024)S(1)}, f32[1024]{0:T(1024)S(1)}, f32[1024]{0:T(1024)S(1)}, /*inde...) fusion(f32[2,256,1024]{2,1,0:T(8,128)S(1)} %convert_element_type.128, ...), kind=kLoop, calls=%fused_computation.16 | loop fusion | flops 8380416 | bytes 12615680 | tf_op jit(solution)/shard_map/reduce_sum | solution.py:66
  100.4 0.8 fusion.1
  101.2 0.6 multiply_reduce_fusion
  102.1 33.6 %all_to_all.9 = f32[128,1,512]{2,1,0:T(1,128)S(1)} all-to-all(f32[128,1,512]{2,1,0:T(1,128)S(1)} %copy.8), channel_id=1, replica_groups=mesh['bl'=128,'ta'=4] {'bl'}, dimensions={0} | all-to-all | bytes 524288 | tf_op jit(solution)/shard_map/all_to_all | solution.py:122
  136.0 11.6 %psum.7 = f32[1,512]{1,0:T(1,128)} all-reduce(f32[1,512]{1,0:T(1,128)S(1)} %bitcast.51), channel_id=1, replica_groups=mesh['bl'=128,'ta'=4] {'ta'}, use_global_device_ids=true, to_apply=%region_17.18 | all-reduce | flops 512 | bytes 4096 | tf_op jit(solution)/shard_map/psum | solution.py:123
  (42 shorter events, 1.9 us)
Async XLA Ops:
  0.0 1.2 copy-start
  1.2 3.0 %copy-start.9 = (bf16[1024,1024]{1,0:T(8,128)(2,1)S(1)}, bf16[1024,1024]{1,0:T(8,128)(2,1)}, u32[]{:S(2)}) copy-start(bf16[1024,1024]{1,0:T(8,128)(2,1)} %constant.56.clone) | copy-start | bytes 6291460
  6.0 62.7 %copy-start.3 = (s32[8,128]{1,0:T(8,128)S(1)}, s32[8,128]{1,0:T(8,128)}, u32[]{:S(2)}) copy-start(s32[8,128]{1,0:T(8,128)} %param.11) | copy-start | bytes 12292
  6.0 69.1 %copy-start.1 = (s32[128]{0:T(128)S(1)}, s32[128]{0:T(128)}, u32[]{:S(2)}) copy-start(s32[128]{0:T(128)} %param.9) | copy-start | bytes 1540
  6.1 69.7 %copy-start.2 = (s32[128]{0:T(128)S(1)}, s32[128]{0:T(128)}, u32[]{:S(2)}) copy-start(s32[128]{0:T(128)} %param.10) | copy-start | bytes 1540
  6.3 15.1 %collective-permute-start = (bf16[2,256,1024]{2,1,0:T(8,128)(2,1)S(1)}, bf16[2,256,1024]{2,1,0:T(8,128)(2,1)S(1)}, u32[]{:S(2)}, u32[]{:S(2)}) collective-permute-start(bf16[2,256,1024]{2,1,0:T(8,128)(2,1)S(1)} %get-tuple-element.34), channel_id=1, source_target_pairs={{0,28},{4,0},{8,4},{12,8},{16,12},{20,16},{24,20},{28,24},{32,60},... | collective-permute-start | bytes 3145736 | tf_op jit(solution)/shard_map/ppermute | solution.py:21
  13.2 51.5 %collective-permute-start.1 = (bf16[2,256,1024]{2,1,0:T(8,128)(2,1)S(1)}, bf16[2,256,1024]{2,1,0:T(8,128)(2,1)S(1)}, u32[]{:S(2)}, u32[]{:S(2)}) collective-permute-start(bf16[2,256,1024]{2,1,0:T(8,128)(2,1)S(1)} %get-tuple-element.34), channel_id=1, source_target_pairs={{480,0},{484,4},{488,8},{492,12},{496,16},{500,20},{504,24},{508,2... | collective-permute-start | bytes 3145736 | tf_op jit(solution)/shard_map/ppermute | solution.py:15
  18.4 46.3 %collective-permute-start.2 = (bf16[2,256,1024]{2,1,0:T(8,128)(2,1)S(1)}, bf16[2,256,1024]{2,1,0:T(8,128)(2,1)}, u32[]{:S(2)}, u32[]{:S(2)}) collective-permute-start(bf16[2,256,1024]{2,1,0:T(8,128)(2,1)S(1)} %get-tuple-element.34), channel_id=1, source_target_pairs={{0,4},{4,8},{8,12},{12,16},{16,20},{20,24},{24,28},{28,0},{32,36},... | collective-permute-start | bytes 3145736 | tf_op jit(solution)/shard_map/ppermute | solution.py:21
  21.4 1.0 copy-start.4
  22.4 45.2 %collective-permute-start.3 = (bf16[2,256,1024]{2,1,0:T(8,128)(2,1)S(1)}, bf16[2,256,1024]{2,1,0:T(8,128)(2,1)}, u32[]{:S(2)}, u32[]{:S(2)}) collective-permute-start(bf16[2,256,1024]{2,1,0:T(8,128)(2,1)S(1)} %collective-permute-done), channel_id=1, source_target_pairs={{0,28},{4,0},{8,4},{12,8},{16,12},{20,16},{24,20},{28,24},{32,60},... | collective-permute-start | bytes 3145736 | tf_op jit(solution)/shard_map/ppermute | solution.py:21
  64.7 2.9 %copy-start.6 = (bf16[2,256,1024]{2,1,0:T(8,128)(2,1)}, bf16[2,256,1024]{2,1,0:T(8,128)(2,1)S(1)}, u32[]{:S(2)}) copy-start(bf16[2,256,1024]{2,1,0:T(8,128)(2,1)S(1)} %collective-permute-done.1) | copy-start | bytes 3145732
  64.7 16.2 %collective-permute-start.6 = (bf16[2,256,1024]{2,1,0:T(8,128)(2,1)}, bf16[2,256,1024]{2,1,0:T(8,128)(2,1)}, u32[]{:S(2)}, u32[]{:S(2)}) collective-permute-start(bf16[2,256,1024]{2,1,0:T(8,128)(2,1)} %collective-permute-done.2), channel_id=1, source_target_pairs={{0,4},{4,8},{8,12},{12,16},{16,20},{20,24},{24,28},{28,0},{32,36},... | collective-permute-start | bytes 3145736 | tf_op jit(solution)/shard_map/ppermute | solution.py:21
  67.6 16.0 %collective-permute-start.4 = (bf16[2,256,1024]{2,1,0:T(8,128)(2,1)}, bf16[2,256,1024]{2,1,0:T(8,128)(2,1)}, u32[]{:S(2)}, u32[]{:S(2)}) collective-permute-start(bf16[2,256,1024]{2,1,0:T(8,128)(2,1)} %collective-permute-done.3), channel_id=1, source_target_pairs={{0,28},{4,0},{8,4},{12,8},{16,12},{20,16},{24,20},{28,24},{32,60},... | collective-permute-start | bytes 3145736 | tf_op jit(solution)/shard_map/ppermute | solution.py:21
  76.4 1.6 %copy-start.7 = (bf16[2,256,1024]{2,1,0:T(8,128)(2,1)S(1)}, bf16[2,256,1024]{2,1,0:T(8,128)(2,1)}, u32[]{:S(2)}) copy-start(bf16[2,256,1024]{2,1,0:T(8,128)(2,1)} %copy-done.6) | copy-start | bytes 3145732
  78.0 1.2 copy-start.5
  82.4 13.2 %collective-permute-start.7 = (bf16[2,256,1024]{2,1,0:T(8,128)(2,1)}, bf16[2,256,1024]{2,1,0:T(8,128)(2,1)S(1)}, u32[]{:S(2)}, u32[]{:S(2)}) collective-permute-start(bf16[2,256,1024]{2,1,0:T(8,128)(2,1)} %collective-permute-done.6), channel_id=1, source_target_pairs={{0,4},{4,8},{8,12},{12,16},{16,20},{20,24},{24,28},{28,0},{32,36},... | collective-permute-start | bytes 3145736 | tf_op jit(solution)/shard_map/ppermute | solution.py:21
  83.6 14.7 %collective-permute-start.5 = (bf16[2,256,1024]{2,1,0:T(8,128)(2,1)}, bf16[2,256,1024]{2,1,0:T(8,128)(2,1)S(1)}, u32[]{:S(2)}, u32[]{:S(2)}) collective-permute-start(bf16[2,256,1024]{2,1,0:T(8,128)(2,1)} %collective-permute-done.4), channel_id=1, source_target_pairs={{0,28},{4,0},{8,4},{12,8},{16,12},{20,16},{24,20},{28,24},{32,60},... | collective-permute-start | bytes 3145736 | tf_op jit(solution)/shard_map/ppermute | solution.py:21
  98.5 1.8 %copy-start.8 = (s32[1024]{0:T(1024)S(1)}, s32[1024]{0:T(1024)}, u32[]{:S(2)}) copy-start(s32[1024]{0:T(1024)} %param.8) | copy-start | bytes 12292

commit v9 on v8

--- a/solution.py
+++ b/solution.py
@@ -43,7 +43,22 @@
     sin_tab = (weight_col * np.sin(phase_angle.astype(np.float64)).astype(np.float32)).astype(
         ml_dtypes.bfloat16
     )
-    return (jnp.asarray(cos_tab), jnp.asarray(sin_tab))
+    half = num_chans // 2
+    cos_half, sin_half, cos_mid, sin_mid = lax.optimization_barrier(
+        (
+            jnp.asarray(cos_tab[:, :half]),
+            jnp.asarray(sin_tab[:, :half]),
+            jnp.asarray(cos_tab[:, half]),
+            jnp.asarray(sin_tab[:, half]),
+        )
+    )
+    cos_full = jnp.concatenate(
+        [cos_half, cos_mid[:, None], cos_half[:, half - 1 : 0 : -1]], axis=1
+    )
+    sin_full = jnp.concatenate(
+        [sin_half, sin_mid[:, None], -sin_half[:, half - 1 : 0 : -1]], axis=1
+    )
+    return (cos_full, sin_full)
 
 
 def delay_transform(block_data, cos_tab, sin_tab):

time: 148 us -> 157 us (1.061)
  local copies, waits for them, and re-layouts: 6.15 us -> 15.4 us
  matrix products: 5.04 us -> 3.34 us
    unnamed x20 -> x33, local copies, waits for them, and re-layouts: 3.21 us -> 9.82 us
    slice x0 -> x2, local copies, waits for them, and re-layouts: none -> 2.23 us  [the longest x1 1.78 us: delay_tables(): sin_half[:, half - 1:0:-1]]
    dot_general x1, matrix products: 2.99 us -> 1.27 us  [delay_transform(): jnp.dot(flat_rows, sin_tab, preferred_element_type=jnp.float32)]
where the time goes in v9:
time: 157 us
  waiting for transfers between devices  49.7 us (32%)
  blocking collectives  45.2 us (29%)
  starting transfers between devices  24.2 us (15%)
  local copies, waits for them, and re-layouts  15.4 us (10%)
  other arithmetic  13.2 us (8%)
  between operations  5.45 us (3%)
  matrix products  3.34 us (2%)
    ppermute x1, waiting for transfers between devices, shifted(): return lax.ppermute(block, axis, route)  38.2 us
    all_to_all x1, blocking collectives, per_device(): received = lax.all_to_all(partial_table, 'bl', 0, 0, tiled=True)  33.6 us
    ppermute x7, starting transfers between devices, group_shifted(): return lax.ppermute(block, axis, route)  18.9 us
    psum x1, blocking collectives, per_device(): return lax.psum(jnp.sum(received, axis=0, keepdims=True), 'ta')  11.6 us
    ppermute x7, waiting for transfers between devices, group_shifted(): return lax.ppermute(block, axis, route)  11.5 us
    unnamed x33, local copies, waits for them, and re-layouts  9.82 us
    convert_element_type x7, other arithmetic, cross_power(): own_f = own_block.astype(jnp.float32)  6.62 us
    ppermute x1, starting transfers between devices, shifted(): return lax.ppermute(block, axis, route)  5.25 us
  transfers between devices with their start and end apart: 8, of which 4 were waited for; matrix products, arithmetic and copies ran while one was open for 7% of the time, Pallas kernels for 0%

profile of v9, /device:TPU:1, one launch (start us, length us, event | category | flops | bytes accessed | tf_op | source)
XLA Modules:
  0.0 156.6 jit_solution(5708443439397202255)
XLA Ops:
  0.0 1.8 %slice.71 = bf16[1024,511]{1,0:T(8,128)(2,1)S(1)} slice(bf16[1024,512]{1,0:T(8,128)(2,1)} %constant.61.clone), slice={[0:1024], [1:512]} | slice | bytes 2093056 | tf_op jit(solution)/shard_map/slice | solution.py:59
  1.8 3.3 %reverse = bf16[1024,512]{1,0:T(8,128)(2,1)S(1)} reverse(bf16[1024,512]{1,0:T(8,128)(2,1)S(1)} %bitcast.42), dimensions={1} | reverse | bytes 2097152
  5.1 1.3 slice_negate_fusion
  7.1 3.3 %reverse.1 = bf16[1024,512]{1,0:T(8,128)(2,1)S(1)} reverse(bf16[1024,512]{1,0:T(8,128)(2,1)S(1)} %bitcast.43), dimensions={1} | reverse | bytes 2097152
  11.9 1.3 fusion.13
  13.2 1.3 fusion.16
  15.3 6.9 %collective-permute-start = (bf16[2,256,1024]{2,1,0:T(8,128)(2,1)S(1)}, bf16[2,256,1024]{2,1,0:T(8,128)(2,1)S(1)}, u32[]{:S(2)}, u32[]{:S(2)}) collective-permute-start(bf16[2,256,1024]{2,1,0:T(8,128)(2,1)S(1)} %get-tuple-element.42), channel_id=1, source_target_pairs={{0,28},{4,0},{8,4},{12,8},{16,12},{20,16},{24,20},{28,24},{32,60},... | collective-permute-start | bytes 3145736 | tf_op jit(solution)/shard_map/ppermute | solution.py:21
  22.2 5.2 %collective-permute-start.1 = (bf16[2,256,1024]{2,1,0:T(8,128)(2,1)S(1)}, bf16[2,256,1024]{2,1,0:T(8,128)(2,1)S(1)}, u32[]{:S(2)}, u32[]{:S(2)}) collective-permute-start(bf16[2,256,1024]{2,1,0:T(8,128)(2,1)S(1)} %get-tuple-element.42), channel_id=1, source_target_pairs={{480,0},{484,4},{488,8},{492,12},{496,16},{500,20},{504,24},{508,2... | collective-permute-start | bytes 3145736 | tf_op jit(solution)/shard_map/ppermute | solution.py:15
  27.4 1.4 collective-permute-start.2
  28.8 1.5 collective-permute-done
  30.4 1.0 copy-done.4
  31.4 4.1 %collective-permute-start.3 = (bf16[2,256,1024]{2,1,0:T(8,128)(2,1)S(1)}, bf16[2,256,1024]{2,1,0:T(8,128)(2,1)}, u32[]{:S(2)}, u32[]{:S(2)}) collective-permute-start(bf16[2,256,1024]{2,1,0:T(8,128)(2,1)S(1)} %collective-permute-done), channel_id=1, source_target_pairs={{0,28},{4,0},{8,4},{12,8},{16,12},{20,16},{24,20},{28,24},{32,60},... | collective-permute-start | bytes 3145736 | tf_op jit(solution)/shard_map/ppermute | solution.py:21
  35.5 38.2 %collective-permute-done.1 = bf16[2,256,1024]{2,1,0:T(8,128)(2,1)S(1)} collective-permute-done((bf16[2,256,1024]{2,1,0:T(8,128)(2,1)S(1)}, bf16[2,256,1024]{2,1,0:T(8,128)(2,1)S(1)}, u32[]{:S(2)}, u32[]{:S(2)}) %collective-permute-start.1) | collective-permute-done | bytes 1048608 | tf_op jit(solution)/shard_map/ppermute | solution.py:15
  73.7 2.8 %collective-permute-start.6 = (bf16[2,256,1024]{2,1,0:T(8,128)(2,1)}, bf16[2,256,1024]{2,1,0:T(8,128)(2,1)}, u32[]{:S(2)}, u32[]{:S(2)}) collective-permute-start(bf16[2,256,1024]{2,1,0:T(8,128)(2,1)} %collective-permute-done.2), channel_id=1, source_target_pairs={{0,4},{4,8},{8,12},{12,16},{16,20},{20,24},{24,28},{28,0},{32,36},... | collective-permute-start | bytes 3145736 | tf_op jit(solution)/shard_map/ppermute | solution.py:21
  76.5 1.2 collective-permute-start.4
  78.4 0.7 fusion.33
  84.1 0.6 gather_fusion
  85.4 1.5 convert_element_type.128
  87.3 1.0 copy-done.5
  88.5 1.5 convert_element_type.113
  89.9 1.5 convert_element_type.125
  91.4 1.1 collective-permute-start.7
  92.6 1.4 collective-permute-start.5
  94.0 1.6 %add_reduce_fusion.2 = (f32[1024]{0:T(1024)S(1)}, f32[1024]{0:T(1024)S(1)}, f32[1024]{0:T(1024)S(1)}, f32[1024]{0:T(1024)S(1)}, f32[1024]{0:T(1024)S(1)}, /*index=5*/f32[1024]{0:T(1024)S(1)}, f32[1024]{0:T(1024)S(1)}) fusion(f32[2,256,1024]{2,1,0:T(8,128)S(1)} %convert_element_type.128, f32[2,256,1024]{2,1,0:T(8,128)S(1)} %get-tuple-element.41, ...), kind=kLoop, calls=%fused_computation.29 | loop fusion | flops 7332864 | bytes 12611584 | tf_op jit(solution)/shard_map/reduce_sum | solution.py:81
  95.6 1.5 convert_element_type.116
  97.1 7.5 %collective-permute-done.7 = bf16[2,256,1024]{2,1,0:T(8,128)(2,1)S(1)} collective-permute-done((bf16[2,256,1024]{2,1,0:T(8,128)(2,1)}, bf16[2,256,1024]{2,1,0:T(8,128)(2,1)S(1)}, u32[]{:S(2)}, u32[]{:S(2)}) %collective-permute-start.7) | collective-permute-done | bytes 1048608 | tf_op jit(solution)/shard_map/ppermute | solution.py:21
  104.9 2.4 %collective-permute-done.5 = bf16[2,256,1024]{2,1,0:T(8,128)(2,1)S(1)} collective-permute-done((bf16[2,256,1024]{2,1,0:T(8,128)(2,1)}, bf16[2,256,1024]{2,1,0:T(8,128)(2,1)S(1)}, u32[]{:S(2)}, u32[]{:S(2)}) %collective-permute-start.5) | collective-permute-done | bytes 1048608 | tf_op jit(solution)/shard_map/ppermute | solution.py:21
  107.5 1.7 %add_reduce_fusion.1 = (f32[1024]{0:T(1024)S(1)}, f32[1024]{0:T(1024)S(1)}, f32[1024]{0:T(1024)S(1)}, f32[1024]{0:T(1024)S(1)}, f32[1024]{0:T(1024)S(1)}, /*inde...) fusion(f32[2,256,1024]{2,1,0:T(8,128)S(1)} %convert_element_type.128, ...), kind=kLoop, calls=%fused_computation.28 | loop fusion | flops 8380416 | bytes 12615680 | tf_op jit(solution)/shard_map/reduce_sum | solution.py:81
  109.4 0.8 fusion.19
  110.2 0.6 multiply_reduce_fusion
  111.1 33.6 %all_to_all.9 = f32[128,1,512]{2,1,0:T(1,128)S(1)} all-to-all(f32[128,1,512]{2,1,0:T(1,128)S(1)} %copy.16), channel_id=1, replica_groups=mesh['bl'=128,'ta'=4] {'bl'}, dimensions={0} | all-to-all | bytes 524288 | tf_op jit(solution)/shard_map/all_to_all | solution.py:137
  145.0 11.6 %psum.7 = f32[1,512]{1,0:T(1,128)} all-reduce(f32[1,512]{1,0:T(1,128)S(1)} %bitcast.53), channel_id=1, replica_groups=mesh['bl'=128,'ta'=4] {'ta'}, use_global_device_ids=true, to_apply=%region_17.18 | all-reduce | flops 512 | bytes 4096 | tf_op jit(solution)/shard_map/psum | solution.py:138
  (60 shorter events, 5.9 us)
Async XLA Ops:
  0.0 11.1 %copy-start = (bf16[2,2,128,1024]{3,2,1,0:T(8,128)(2,1)S(1)}, bf16[2,2,128,1024]{3,2,1,0:T(8,128)(2,1)}, u32[]{:S(2)}) copy-start(bf16[2,2,128,1024]{3,2,1,0:T(8,128)(2,1)} %param.9) | copy-start | bytes 3145732
  1.8 4.6 %copy-start.13 = (bf16[1024]{0:T(1024)(128)(2,1)S(1)}, bf16[1024]{0:T(1024)(128)(2,1)}, u32[]{:S(2)}) copy-start(bf16[1024]{0:T(1024)(128)(2,1)} %constant.63.clone) | copy-start | bytes 6148
  5.1 1.6 %copy-start.9 = (bf16[1024,512]{1,0:T(8,128)(2,1)S(1)}, bf16[1024,512]{1,0:T(8,128)(2,1)}, u32[]{:S(2)}) copy-start(bf16[1024,512]{1,0:T(8,128)(2,1)} %constant.60.clone) | copy-start | bytes 3145732
  7.1 3.8 %copy-start.12 = (bf16[1024]{0:T(1024)(128)(2,1)S(1)}, bf16[1024]{0:T(1024)(128)(2,1)}, u32[]{:S(2)}) copy-start(bf16[1024]{0:T(1024)(128)(2,1)} %constant.62.clone) | copy-start | bytes 6148
  10.4 1.2 copy-start.8
  10.4 1.5 copy-start.11
  11.9 1.3 copy-start.10
  15.0 62.7 %copy-start.3 = (s32[8,128]{1,0:T(8,128)S(1)}, s32[8,128]{1,0:T(8,128)}, u32[]{:S(2)}) copy-start(s32[8,128]{1,0:T(8,128)} %param.13) | copy-start | bytes 12292
  15.0 69.1 %copy-start.1 = (s32[128]{0:T(128)S(1)}, s32[128]{0:T(128)}, u32[]{:S(2)}) copy-start(s32[128]{0:T(128)} %param.11) | copy-start | bytes 1540
  15.1 69.7 %copy-start.2 = (s32[128]{0:T(128)S(1)}, s32[128]{0:T(128)}, u32[]{:S(2)}) copy-start(s32[128]{0:T(128)} %param.12) | copy-start | bytes 1540
  15.3 15.1 %collective-permute-start = (bf16[2,256,1024]{2,1,0:T(8,128)(2,1)S(1)}, bf16[2,256,1024]{2,1,0:T(8,128)(2,1)S(1)}, u32[]{:S(2)}, u32[]{:S(2)}) collective-permute-start(bf16[2,256,1024]{2,1,0:T(8,128)(2,1)S(1)} %get-tuple-element.42), channel_id=1, source_target_pairs={{0,28},{4,0},{8,4},{12,8},{16,12},{20,16},{24,20},{28,24},{32,60},... | collective-permute-start | bytes 3145736 | tf_op jit(solution)/shard_map/ppermute | solution.py:21
  22.2 51.5 %collective-permute-start.1 = (bf16[2,256,1024]{2,1,0:T(8,128)(2,1)S(1)}, bf16[2,256,1024]{2,1,0:T(8,128)(2,1)S(1)}, u32[]{:S(2)}, u32[]{:S(2)}) collective-permute-start(bf16[2,256,1024]{2,1,0:T(8,128)(2,1)S(1)} %get-tuple-element.42), channel_id=1, source_target_pairs={{480,0},{484,4},{488,8},{492,12},{496,16},{500,20},{504,24},{508,2... | collective-permute-start | bytes 3145736 | tf_op jit(solution)/shard_map/ppermute | solution.py:15
  27.4 46.3 %collective-permute-start.2 = (bf16[2,256,1024]{2,1,0:T(8,128)(2,1)S(1)}, bf16[2,256,1024]{2,1,0:T(8,128)(2,1)}, u32[]{:S(2)}, u32[]{:S(2)}) collective-permute-start(bf16[2,256,1024]{2,1,0:T(8,128)(2,1)S(1)} %get-tuple-element.42), channel_id=1, source_target_pairs={{0,4},{4,8},{8,12},{12,16},{16,20},{20,24},{24,28},{28,0},{32,36},... | collective-permute-start | bytes 3145736 | tf_op jit(solution)/shard_map/ppermute | solution.py:21
  30.4 1.0 copy-start.4
  31.4 45.2 %collective-permute-start.3 = (bf16[2,256,1024]{2,1,0:T(8,128)(2,1)S(1)}, bf16[2,256,1024]{2,1,0:T(8,128)(2,1)}, u32[]{:S(2)}, u32[]{:S(2)}) collective-permute-start(bf16[2,256,1024]{2,1,0:T(8,128)(2,1)S(1)} %collective-permute-done), channel_id=1, source_target_pairs={{0,28},{4,0},{8,4},{12,8},{16,12},{20,16},{24,20},{28,24},{32,60},... | collective-permute-start | bytes 3145736 | tf_op jit(solution)/shard_map/ppermute | solution.py:21
  73.7 2.8 %copy-start.6 = (bf16[2,256,1024]{2,1,0:T(8,128)(2,1)}, bf16[2,256,1024]{2,1,0:T(8,128)(2,1)S(1)}, u32[]{:S(2)}) copy-start(bf16[2,256,1024]{2,1,0:T(8,128)(2,1)S(1)} %collective-permute-done.1) | copy-start | bytes 3145732
  73.7 16.2 %collective-permute-start.6 = (bf16[2,256,1024]{2,1,0:T(8,128)(2,1)}, bf16[2,256,1024]{2,1,0:T(8,128)(2,1)}, u32[]{:S(2)}, u32[]{:S(2)}) collective-permute-start(bf16[2,256,1024]{2,1,0:T(8,128)(2,1)} %collective-permute-done.2), channel_id=1, source_target_pairs={{0,4},{4,8},{8,12},{12,16},{16,20},{20,24},{24,28},{28,0},{32,36},... | collective-permute-start | bytes 3145736 | tf_op jit(solution)/shard_map/ppermute | solution.py:21
  76.5 16.0 %collective-permute-start.4 = (bf16[2,256,1024]{2,1,0:T(8,128)(2,1)}, bf16[2,256,1024]{2,1,0:T(8,128)(2,1)}, u32[]{:S(2)}, u32[]{:S(2)}) collective-permute-start(bf16[2,256,1024]{2,1,0:T(8,128)(2,1)} %collective-permute-done.3), channel_id=1, source_target_pairs={{0,28},{4,0},{8,4},{12,8},{16,12},{20,16},{24,20},{28,24},{32,60},... | collective-permute-start | bytes 3145736 | tf_op jit(solution)/shard_map/ppermute | solution.py:21
  85.4 1.6 %copy-start.7 = (bf16[2,256,1024]{2,1,0:T(8,128)(2,1)S(1)}, bf16[2,256,1024]{2,1,0:T(8,128)(2,1)}, u32[]{:S(2)}) copy-start(bf16[2,256,1024]{2,1,0:T(8,128)(2,1)} %copy-done.6) | copy-start | bytes 3145732
  87.0 1.2 copy-start.5
  91.4 13.2 %collective-permute-start.7 = (bf16[2,256,1024]{2,1,0:T(8,128)(2,1)}, bf16[2,256,1024]{2,1,0:T(8,128)(2,1)S(1)}, u32[]{:S(2)}, u32[]{:S(2)}) collective-permute-start(bf16[2,256,1024]{2,1,0:T(8,128)(2,1)} %collective-permute-done.6), channel_id=1, source_target_pairs={{0,4},{4,8},{8,12},{12,16},{16,20},{20,24},{24,28},{28,0},{32,36},... | collective-permute-start | bytes 3145736 | tf_op jit(solution)/shard_map/ppermute | solution.py:21
  92.6 14.7 %collective-permute-start.5 = (bf16[2,256,1024]{2,1,0:T(8,128)(2,1)}, bf16[2,256,1024]{2,1,0:T(8,128)(2,1)S(1)}, u32[]{:S(2)}, u32[]{:S(2)}) collective-permute-start(bf16[2,256,1024]{2,1,0:T(8,128)(2,1)} %collective-permute-done.4), channel_id=1, source_target_pairs={{0,28},{4,0},{8,4},{12,8},{16,12},{20,16},{24,20},{28,24},{32,60},... | collective-permute-start | bytes 3145736 | tf_op jit(solution)/shard_map/ppermute | solution.py:21
  107.5 1.8 %copy-start.14 = (s32[1024]{0:T(1024)S(1)}, s32[1024]{0:T(1024)}, u32[]{:S(2)}) copy-start(s32[1024]{0:T(1024)} %param.10) | copy-start | bytes 12292
